TPU v7x, 128 devices: a whole 4x4x4 slice. The times are simulated.
128 devices in a mesh: pix: 8 (over y_hi, z), tm: 16 (over x, y_lo, core).
Axes of the slice: x: 4, y: 4 (y_hi: 2, y_lo: 2; y = y_hi * 2 + y_lo), z: 4, core: 2. Of those that a mesh axis runs over, the one named last changes fastest.
Arguments:
- frames: float32 [16, 192, 12288], P('tm', 'pix'), may hold values from 0.05 to 5
- pixel_order: int32 [12288], replicated, may hold values from 0 to 12287, each once
- cycle_sizes: int32 [64], replicated, may hold values from 1 to 384, 12288 in all
- kernel: float32 [5], replicated, may hold values from 0.1 to 1
Outputs:
- correlation: float32 [64, 3072, 3072], P('pix', 'tm')
Inputs may be any that keep to these rules, and one draw needn't show every extreme that they name: `cycle_sizes`: every cycle has one or more pixels, the sizes sum to 12288, and one cycle has exactly 384.
All inputs are finite; a program needn't handle non-finite values.
Results may differ from a plain program's by a relative error of at most 0.00005.
Values sent between devices are 32-bit elements; how exact they have to be, the bound alone decides.
No kernel may reach another device: no remote copies, remote signals or barrier semaphores. Data moves between devices by JAX's collectives and lax.ppermute only.
A program may use at most 256 MiB of HBM per device.

v0:
```python
import jax
import jax.numpy as jnp
from jax import lax
from jax.sharding import PartitionSpec as P

REACH = 2


def with_halo(block, sides, width):
    for axis, dim in sides:
        count = lax.axis_size(axis)
        forward = [(i, i + 1) for i in range(count - 1)]
        backward = [(target, source) for source, target in forward]
        low = lax.ppermute(
            lax.slice_in_dim(block, block.shape[dim] - width, None, axis=dim), axis, forward
        )
        high = lax.ppermute(lax.slice_in_dim(block, 0, width, axis=dim), axis, backward)
        block = jnp.concatenate([low, block, high], axis=dim)
    return block


def correlate(left, left_total, right, scale):
    product = jnp.einsum(
        "rct,rcs->rts",
        left,
        right,
        precision=lax.Precision.HIGHEST,
        preferred_element_type=jnp.float32,
    )
    right_total = jnp.sum(right, axis=1)
    return product * scale[:, None, None] / (left_total[:, :, None] * right_total[:, None, :])


def per_device(frames, pixel_order, cycle_sizes, kernel):
    block = frames[0]
    cycles = cycle_sizes.shape[0]
    pixels = block.shape[1]
    cap = 2 * pixels // cycles
    starts = jnp.cumsum(cycle_sizes) - cycle_sizes
    slots = jnp.arange(cap, dtype=jnp.int32)
    where_idx = jnp.minimum(starts[:, None] + slots[None, :], pixels - 1)
    valid = slots[None, :] < cycle_sizes[:, None]
    columns = pixel_order[where_idx]
    flat = jnp.transpose(block)
    picked = jnp.where(valid[:, :, None], flat[columns], 0.0)
    local = lax.all_to_all(picked, "pix", split_axis=0, concat_axis=2, tiled=True)
    owned = local.shape[0]
    tblk = local.shape[2]
    scale = lax.dynamic_slice_in_dim(cycle_sizes, lax.axis_index("pix") * owned, owned).astype(
        jnp.float32
    )
    own_total = jnp.sum(local, axis=1)
    normed = correlate(local, own_total, lax.all_gather(local, "tm", axis=2, tiled=True), scale)
    count = normed.shape[2]
    padded = jnp.pad(normed, ((0, 0), (0, 0), (REACH, REACH)))
    across = kernel[0] * padded[:, :, 0:count]
    for shift_step in range(1, 2 * REACH + 1):
        across = across + kernel[shift_step] * padded[:, :, shift_step : shift_step + count]
    rimmed = with_halo(across, (("tm", 1),), REACH)
    result = kernel[0] * rimmed[:, 0:tblk]
    for shift_step in range(1, 2 * REACH + 1):
        result = result + kernel[shift_step] * rimmed[:, shift_step : shift_step + tblk]
    return result


def solution(mesh):
    placed = (P("tm", "pix", None), P(), P(), P())
    return jax.shard_map(
        per_device, mesh=mesh, in_specs=placed, out_specs=P("pix", "tm", None), check_vma=False
    )
```

profile of v0, /device:TPU:1, one launch (start us, length us, event | category | flops | bytes accessed | tf_op | source)
XLA Modules:
  0.0 637.4 jit_solution(14035396235880347617)
XLA Ops:
  6.5 4.9 copy.15
  11.4 0.7 iota_compare_fusion
  12.2 0.7 copy.16
  12.9 0.1 reduce-window.9
  13.0 0.1 reduce.1
  13.1 0.7 sub.3
  13.9 135.5 %gather_fusion = s32[24576]{0:T(1024)S(1)} fusion(s32[12288]{0:T(1024)S(1)} %copy-done, s32[24576]{0:T(1024)S(1)} %broadcast_clamp_fusion), kind=kCustom, calls=%fused_computation | custom fusion | bytes 294912 | tf_op jit(solution)/shard_map/gather | solution.py:43
  149.6 84.8 %gather_fusion.1 = f32[24576,24]{1,0:T(8,128)} fusion(f32[12288,24]{1,0:T(8,128)} %bitcast.20, s32[24576]{0:T(1024)S(1)} %broadcast_clamp_fusion.1), kind=kCustom, calls=%fused_computation.1 | custom fusion | bytes 4816896 | tf_op jit(solution)/shard_map/gather | solution.py:45
  234.4 7.7 %copy.17 = f32[64,384,24]{1,2,0:T(8,128)S(1)} copy(f32[64,384,24]{2,1,0:T(8,128)} %bitcast.21) | data formatting | bytes 4718592 | tf_op jit(solution)/shard_map/gather | solution.py:45
  242.1 0.3 broadcast_select_fusion
  242.4 38.0 %all_to_all.18 = f32[64,384,24]{1,2,0:T(8,128)S(1)} all-to-all(f32[64,384,24]{1,2,0:T(8,128)S(1)} %broadcast_select_fusion), channel_id=1, replica_groups=mesh['pix'=8,'tm'=16] {'pix'}, dimensions={0} | all-to-all | bytes 4718592 | tf_op jit(solution)/shard_map/all_to_all | solution.py:46
  280.4 1.6 copy.18
  282.1 0.7 fusion.12
  282.7 0.3 reduce_sum.18
  283.1 188.8 %all-gather.2.cloned.1.call-done = f32[8,384,3072]{1,2,0:T(8,128)} async-done(((f32[8,384,192]{1,2,0:T(8,128)}), f32[8,384,3072]{1,2,0:T(8,128)}) %all-gather.2.cloned.1.call-update) | async-done | bytes 37748752 | tf_op jit(solution)/shard_map/all_gather | solution.py:53
  471.9 17.3 %reduce_sum.19 = f32[8,3072]{1,0:T(8,128)S(1)} reduce(f32[8,384,3072]{1,2,0:T(8,128)} %all-gather.2.cloned.1.call-done, f32[]{:T(128)} %constant.6.clone.1), dimensions={1}, to_apply=%region_2.3 | reduce | flops 9412608 | bytes 37847044 | tf_op jit(solution)/shard_map/reduce_sum | solution.py:30
  489.2 47.2 %multiply_divide_fusion = f32[8,192,3072]{2,1,0:T(8,128)} fusion(f32[8,3072]{1,0:T(8,128)S(1)} %reduce_sum.19, f32[8,192]{1,0:T(8,128)S(1)} %mul.80, f32[8]{0:T(128)S(1)} %dynamic-slice_convert_fusion, f32[8,384,192]{1,2,0:T(8,128)S(1)} %bitcast.25, f32[8,384,3072]{1,2,0:T(8,128)} %all-gather.2.cloned.1.call-done), kind=kOutput, calls=%fused_computation.21 | convolution fusion | flops 21757427712 | bytes 59086880 | tf_op jit(solution)/shard_map/rct,rcs->rts/dot_general | solution.py:23
  536.4 41.1 %multiply_add_fusion = f32[8,192,3072]{2,1,0:T(8,128)} fusion(f32[8,192,3072]{2,1,0:T(8,128)} %multiply_divide_fusion, f32[]{:T(128)} %bitcast.12, f32[]{:T(128)} %bitcast.11, f32[]{:T(128)} %bitcast.10, f32[]{:T(128)} %bitcast.9, f32[]{:T(128)} %bitcast), kind=kLoop, calls=%fused_computation.18 | loop fusion | flops 42467328 | bytes 37748756 | tf_op jit(solution)/shard_map/add | solution.py:58
  577.5 1.5 fusion.11
  579.0 3.2 collective-permute-start
  582.3 2.1 collective-permute-start.1
  584.3 0.5 collective-permute-done
  584.8 4.5 collective-permute-done.1
  589.4 41.1 %fusion.3 = f32[8,192,3072]{2,1,0:T(8,128)} fusion(f32[8,192,3072]{2,1,0:T(8,128)} %multiply_add_fusion, f32[8,2,3072]{2,1,0:T(2,128)S(1)} %collective-permute-done.1, f32[8,2,3072]{2,1,0:T(2,128)S(1)} %collective-permute-done, f32[]{:T(128)} %bitcast.12, f32[]{:T(128)} %bitcast.11, f32[]{:T(128)} %bitcast.10, f32[]{:T(128)} %bitcast.9, f32[]{:T(128)} %bitcast), kind=kLoop, calls=%fused_computation.9 | loop fusion | flops 61341696 | bytes 38141972 | tf_op jit(solution)/shard_map/add | solution.py:62
  (22 shorter events, 0.4 us)
Async XLA Ops:
  6.5 7.4 %copy-start = (s32[12288]{0:T(1024)S(1)}, s32[12288]{0:T(1024)}, u32[]{:S(2)}) copy-start(s32[12288]{0:T(1024)} %param.5) | copy-start | bytes 147460
  6.5 465.3 %all-gather.2.cloned.1.call-start = ((), (), s32[]{:S(2)}) async-start(), calls=%async_computation.1 | async-start | bytes 40108032 | tf_op jit(solution)/shard_map/all_gather | solution.py:53
  234.4 47.5 %copy-start.4 = (s32[64]{0:T(128)S(1)}, s32[64]{0:T(128)}, u32[]{:S(2)}) copy-start(s32[64]{0:T(128)} %param.6) | copy-start | bytes 772
  234.4 47.6 %copy-start.3 = (f32[5]{0:T(128)S(1)}, f32[5]{0:T(128)}, u32[]{:S(2)}) copy-start(f32[5]{0:T(128)} %param.7) | copy-start | bytes 64
  283.1 206.1 %copy-start.2 = (f32[8,384,8,24]{1,3,2,0:T(8,128)S(1)}, f32[8,384,8,24]{1,3,2,0:T(8,128)}, u32[]{:S(2)}) copy-start(f32[8,384,8,24]{1,3,2,0:T(8,128)} %copy.18) | copy-start | bytes 7077892
  579.0 5.8 collective-permute-start
  582.2 48.3 %copy-start.1 = (s32[12288]{0:T(1024)S(1)}, s32[12288]{0:T(1024)}, u32[]{:S(2)}) copy-start(s32[12288]{0:T(1024)} %param.5) | copy-start | bytes 147460
  582.3 7.1 %collective-permute-start.1 = (f32[8,2,3072]{2,1,0:T(2,128)S(1)}, f32[8,2,3072]{2,1,0:T(2,128)S(1)}, u32[]{:S(2)}, u32[]{:S(2)}) collective-permute-start(f32[8,2,3072]{2,1,0:T(2,128)S(1)} %get-tuple-element.6), channel_id=1, source_target_pairs={{1,0},{2,1},{3,2},{4,3},{5,4},{6,5},{7,6},{8,7},{9,8},{10,9},{11,1... | collective-permute-start | bytes 589832 | tf_op jit(solution)/shard_map/ppermute | solution.py:17
Sparse Core Ops, SparseCore 0:
  282.1 189.7 all-gather.1
where the time goes:
time: 638 us; the launch traced here: 637 us
  local copies, waits for them, and re-layouts  238 us (37%)
  waiting for transfers between devices  194 us (30%)
  other arithmetic  102 us (16%)
  matrix products  47.2 us (7%)
  blocking collectives  38 us (6%)
  between operations  13.6 us (2%)
    all_gather x1, waiting for transfers between devices, per_device(): lax.all_gather(local, 'tm', axis=2, tiled=True)  189 us
    gather x2, local copies, waits for them, and re-layouts, per_device(): columns = pixel_order[where_idx]  136 us
    gather x2, local copies, waits for them, and re-layouts, per_device(): picked = jnp.where(valid[:, :, None], flat[columns], 0.0)  92.5 us
    dot_general x1, matrix products, correlate(): jnp.einsum('rct,rcs->rts', left, right, precision=lax.Precision.HIGHEST,...  47.2 us
    add x1, other arithmetic, per_device(): result + kernel[shift_step] * rimmed[:, shift_step:shift_step + tblk]  41.1 us
    add x1, other arithmetic, per_device(): across + kernel[shift_step] * padded[:, :, shift_step:shift_step + count]  41.1 us
    all_to_all x1, blocking collectives, per_device(): lax.all_to_all(picked, 'pix', split_axis=0, concat_axis=2, tiled=True)  38 us
    reduce_sum x1, other arithmetic, correlate(): right_total = jnp.sum(right, axis=1)  17.3 us
  transfers between devices with their start and end apart: 3, of which 3 were waited for; matrix products, arithmetic and copies ran while one was open for 0% of the time, Pallas kernels for 0%

commit v1 on v0

v1 whole, which is shorter than its diff:
```python
import functools

import jax
import jax.numpy as jnp
from jax import lax
from jax.experimental import pallas as pl
from jax.experimental.pallas import tpu as pltpu
from jax.sharding import PartitionSpec as P

REACH = 2


def pick_kernel(owned, cap, first_ref, starts_ref, sizes_ref, order_ref, pixels_ref, out_ref):
    out_ref[...] = jnp.zeros_like(out_ref)
    first = first_ref[0]
    for r in range(owned):
        start = starts_ref[first + r]
        size = sizes_ref[first + r]

        def body(c, carry, r=r, start=start):
            row = order_ref[start + c]
            out_ref[pl.ds(r * cap + c, 1), :] = pixels_ref[pl.ds(row, 1), :]
            return carry

        lax.fori_loop(0, size, body, 0)


def pick(first, starts, sizes, order, pixels, owned, cap):
    count, width = pixels.shape
    smem = pl.BlockSpec(memory_space=pltpu.SMEM)
    vmem = pl.BlockSpec(memory_space=pltpu.VMEM)
    return pl.pallas_call(
        functools.partial(pick_kernel, owned, cap),
        out_shape=jax.ShapeDtypeStruct((owned * cap, width), pixels.dtype),
        in_specs=[smem, smem, smem, smem, vmem],
        out_specs=vmem,
        compiler_params=pltpu.CompilerParams(vmem_limit_bytes=40 * 1024 * 1024),
    )(first, starts, sizes, order, pixels)


def halo_frames(block, width):
    count = lax.axis_size("tm")
    forward = [(i, i + 1) for i in range(count - 1)]
    backward = [(i + 1, i) for i in range(count - 1)]
    n = block.shape[-1]
    low = lax.ppermute(block[..., n - width :], "tm", forward)
    high = lax.ppermute(block[..., :width], "tm", backward)
    return jnp.concatenate([low, block, high], axis=-1)


def per_device(frames, pixel_order, cycle_sizes, kernel):
    block = frames[0]
    cycles = cycle_sizes.shape[0]
    pixels = block.shape[1]
    cap = 2 * pixels // cycles
    owned = cycles // lax.axis_size("pix")
    starts = (jnp.cumsum(cycle_sizes) - cycle_sizes).astype(jnp.int32)
    first = (lax.axis_index("pix") * owned).astype(jnp.int32).reshape(1)

    series = lax.all_gather(block, "pix", axis=0, tiled=True)
    tblk = series.shape[0]
    picked = pick(first, starts, cycle_sizes, pixel_order, series.T, owned, cap)
    picked = picked.reshape(owned, cap, tblk)

    total = jnp.sum(picked, axis=1, keepdims=True)
    scaled = picked / total
    rimmed = halo_frames(scaled, REACH)
    smooth = kernel[0] * rimmed[..., 0:tblk]
    for shift_step in range(1, 2 * REACH + 1):
        smooth = smooth + kernel[shift_step] * rimmed[..., shift_step : shift_step + tblk]
    smooth = jnp.swapaxes(smooth, 1, 2)

    scale = lax.dynamic_slice_in_dim(cycle_sizes, first[0], owned).astype(jnp.float32)
    left = smooth * scale[:, None, None]
    right = lax.all_gather(smooth, "tm", axis=1, tiled=True)
    return jnp.einsum(
        "rfs,rgs->rfg",
        left,
        right,
        precision=lax.Precision.HIGH,
        preferred_element_type=jnp.float32,
    )


def solution(mesh):
    placed = (P("tm", "pix", None), P(), P(), P())
    return jax.shard_map(
        per_device, mesh=mesh, in_specs=placed, out_specs=P("pix", "tm", None), check_vma=False
    )
```

time: 638 us -> 414 us (0.65)
  local copies, waits for them, and re-layouts: 238 us -> 28.6 us
  waiting for transfers between devices: 194 us -> 315 us
  other arithmetic: 102 us -> 8.1 us
  blocking collectives: 38 us -> 0 us
  matrix products: 47.2 us -> 28.6 us
  Pallas kernels: 0 us -> 14.4 us
    gather x4 -> x0, local copies, waits for them, and re-layouts: 228 us -> none  [the longest x2 136 us: per_device(): columns = pixel_order[where_idx]]
    all_gather x1 -> x2, waiting for transfers between devices: 189 us -> 313 us  [the longest x1 194 us: per_device(): right = lax.all_gather(smooth, 'tm', axis=1, tiled=True)]
    add x2 -> x0, other arithmetic: 82.2 us -> none  [the longest x1 41.1 us: per_device(): result + kernel[shift_step] * rimmed[:, shift_step:shift_step + tblk]]
    all_to_all x1 -> x0, blocking collectives: 38 us -> none  [per_device(): lax.all_to_all(picked, 'pix', split_axis=0, concat_axis=2, tiled=True)]
    all_gather x0 -> x1, local copies, waits for them, and re-layouts: none -> 22.1 us  [per_device(): series = lax.all_gather(block, 'pix', axis=0, tiled=True)]
    dot_general x1, matrix products: 47.2 us -> 28.6 us  [per_device(): jnp.einsum('rfs,rgs->rfg', left, right, precision=lax.Precision.HIGH, pre...]
    reduce_sum x2 -> x1, other arithmetic: 17.6 us -> 0.22 us  [per_device(): total = jnp.sum(picked, axis=1, keepdims=True)]
    pallas_call x0 -> x1, Pallas kernels: none -> 14.4 us  [pick(): pl.pallas_call(functools.partial(pick_kernel, owned, cap), out_shape=jax....]
  transfers between devices with their start and end apart: 3 -> 4, of which waited for: 3 -> 3; matrix products, arithmetic and copies ran while one was open for 0% -> 0% of each run, Pallas kernels for 0% -> 0%
where the time goes in v1:
time: 414 us
  waiting for transfers between devices  315 us (76%)
  local copies, waits for them, and re-layouts  28.6 us (7%)
  matrix products  28.6 us (7%)
  Pallas kernels  14.4 us (3%)
  between operations  13.5 us (3%)
  other arithmetic  8.1 us (2%)
  starting transfers between devices  5.46 us (1%)
    all_gather x1, waiting for transfers between devices, per_device(): right = lax.all_gather(smooth, 'tm', axis=1, tiled=True)  194 us
    all_gather x1, waiting for transfers between devices, per_device(): series = lax.all_gather(block, 'pix', axis=0, tiled=True)  118 us
    dot_general x1, matrix products, per_device(): jnp.einsum('rfs,rgs->rfg', left, right, precision=lax.Precision.HIGH, pre...  28.6 us
    all_gather x1, local copies, waits for them, and re-layouts, per_device(): series = lax.all_gather(block, 'pix', axis=0, tiled=True)  22.1 us
    pallas_call x1, Pallas kernels, pick(): pl.pallas_call(functools.partial(pick_kernel, owned, cap), out_shape=jax....  14.4 us
  transfers between devices with their start and end apart: 4, of which 3 were waited for; matrix products, arithmetic and copies ran while one was open for 0% of the time, Pallas kernels for 0%

profile of v1, /device:TPU:1, one launch (start us, length us, event | category | flops | bytes accessed | tf_op | source)
XLA Modules:
  0.0 413.8 jit_solution(9333775609667832679)
XLA Ops:
  6.5 3.5 copy.12
  10.0 0.0 all-gather.6.cloned.1.call-update
  10.1 0.0 all-gather.4.cloned.1.call-start
  10.1 0.1 copy.11
  10.2 0.1 reduce-window.9
  10.3 0.1 reduce
  10.5 0.0 copy-start
  10.5 118.4 %all-gather.6.cloned.1.call-done = f32[1,192,12288]{2,0,1:T(1,128)} async-done(((f32[1,24,12288]{2,0,1:T(1,128)}), f32[1,192,12288]{2,0,1:T(1,128)}) %all-gather.6.cloned.1.call-update) | async-done | bytes 9437200 | tf_op jit(solution)/shard_map/all_gather | solution.py:60
  128.9 22.1 %copy.13 = f32[1,192,12288]{1,2,0:T(8,128)} copy(f32[1,192,12288]{2,0,1:T(1,128)} %all-gather.6.cloned.1.call-done) | data formatting | bytes 18874368 | tf_op jit(solution)/shard_map/all_gather | solution.py:60
  151.0 14.4 %shard_map.46 = f32[3072,192]{1,0:T(8,128)S(1)} custom-call(s32[1]{0:T(128)} %bitcast.1.first_ref, s32[64]{0:T(128)S(1)} %sub.3.starts_ref, s32[64]{0:T(128)S(1)} %copy-done.1, s32[12288]{0:T(1024)S(1)} %copy-done, f32[12288,192]{1,0:T(8,128)} %bitcast.17), custom_call_target="tpu_custom_call" | custom-call | tf_op jit(solution)/shard_map/pallas_call | solution.py:32
  165.4 2.2 copy.14
  167.6 0.2 reduce_sum.9
  167.8 0.0 copy-start.3
  167.8 1.9 broadcast_divide_fusion
  169.8 3.5 collective-permute-start
  173.3 1.9 collective-permute-start.1
  175.3 0.7 fusion.15
  175.9 0.0 collective-permute-done
  175.9 2.5 collective-permute-done.1
  178.5 5.6 %fusion.4 = f32[8,192,384]{2,1,0:T(8,128)} fusion(f32[8,384,192]{1,2,0:T(8,128)S(1)} %broadcast_divide_fusion, f32[8,384,2]{1,2,0:T(2,128)S(1)} %collective-permute-done.1, f32[8,384,2]{1,2,0:T(2,128)S(1)} %collective-permute-done, f32[]{:T(128)} %bitcast.9, f32[]{:T(128)} %bitcast.8, f32[]{:T(128)} %bitcast.7, f32[]{:T(128)} %bitcast.6, f32[]{:T(128)} %bitcast), kind=kLoop, calls=%fused_computation.8 | loop fusion | flops 7667712 | bytes 4767764 | tf_op jit(solution)/shard_map/transpose | solution.py:71
  184.1 0.0 all-gather.4.cloned.1.call-update
  184.1 0.1 dynamic-slice_convert_fusion
  184.2 194.2 %all-gather.4.cloned.1.call-done = f32[8,3072,384]{2,1,0:T(8,128)} async-done(((f32[8,192,384]{2,1,0:T(8,128)}), f32[8,3072,384]{2,1,0:T(8,128)}) %all-gather.4.cloned.1.call-update) | async-done | bytes 37748752 | tf_op jit(solution)/shard_map/all_gather | solution.py:75
  378.4 28.6 %fusion.11 = f32[8,192,3072]{2,1,0:T(8,128)} fusion(f32[8,3072,384]{2,1,0:T(8,128)} %all-gather.4.cloned.1.call-done, f32[8,192,384]{2,1,0:T(8,128)S(1)} %copy-done.2, f32[8]{0:T(128)S(1)} %dynamic-slice_convert_fusion), kind=kOutput, calls=%fused_computation.17 | convolution fusion | flops 10872225792 | bytes 58982432 | tf_op jit(solution)/shard_map/rfs,rgs->rfg/dot_general | solution.py:76
  (9 shorter events, 0.0 us)
Async XLA Ops:
  6.5 3.6 copy-start.1
  6.5 122.4 %all-gather.6.cloned.1.call-start = ((), (), s32[]{:S(2)}) async-start(), calls=%async_computation.1 | async-start | bytes 10616832 | tf_op jit(solution)/shard_map/all_gather | solution.py:60
  10.1 368.3 %all-gather.4.cloned.1.call-start = ((), (), s32[]{:S(2)}) async-start(), calls=%async_computation | async-start | bytes 40108032 | tf_op jit(solution)/shard_map/all_gather | solution.py:75
  10.5 140.5 %copy-start = (s32[12288]{0:T(1024)S(1)}, s32[12288]{0:T(1024)}, u32[]{:S(2)}) copy-start(s32[12288]{0:T(1024)} %order_ref.1) | copy-start | bytes 147460
  167.8 7.4 %copy-start.3 = (f32[5]{0:T(128)S(1)}, f32[5]{0:T(128)}, u32[]{:S(2)}) copy-start(f32[5]{0:T(128)} %param.7) | copy-start | bytes 64
  169.8 6.1 %collective-permute-start = (f32[8,384,2]{1,2,0:T(2,128)S(1)}, f32[8,384,2]{1,2,0:T(2,128)S(1)}, u32[]{:S(2)}, u32[]{:S(2)}) collective-permute-start(f32[8,384,2]{1,2,0:T(2,128)S(1)} %get-tuple-element.5), channel_id=1, source_target_pairs={{0,1},{1,2},{2,3},{3,4},{4,5},{5,6},{6,7},{7,8},{8,9},{9,10},{10,1... | collective-permute-start | bytes 73736 | tf_op jit(solution)/shard_map/ppermute | solution.py:46
  173.3 5.1 %collective-permute-start.1 = (f32[8,384,2]{1,2,0:T(2,128)S(1)}, f32[8,384,2]{1,2,0:T(2,128)S(1)}, u32[]{:S(2)}, u32[]{:S(2)}) collective-permute-start(f32[8,384,2]{1,2,0:T(2,128)S(1)} %get-tuple-element.6), channel_id=1, source_target_pairs={{1,0},{2,1},{3,2},{4,3},{5,4},{6,5},{7,6},{8,7},{9,8},{10,9},{11,1... | collective-permute-start | bytes 73736 | tf_op jit(solution)/shard_map/ppermute | solution.py:47
  184.1 194.3 %copy-start.2 = (f32[8,192,384]{2,1,0:T(8,128)S(1)}, f32[8,192,384]{2,1,0:T(8,128)}, u32[]{:S(2)}) copy-start(f32[8,192,384]{2,1,0:T(8,128)} %fusion.4) | copy-start | bytes 7077892
Sparse Core Ops, SparseCore 0:
  10.2 118.6 all-gather.5
  184.3 194.0 all-gather.3

commit v2 on v1

v2 whole, which is shorter than its diff:
```python
import jax
import jax.numpy as jnp
from jax import lax
from jax.sharding import Mesh
from jax.sharding import PartitionSpec as P

REACH = 2
PIX = ("yh", "z")
TM = ("x", "yl", "c")
CHIPS = ("x", "yl")


def halo_frames(block, width):
    count = lax.axis_size(TM)
    forward = [(i, i + 1) for i in range(count - 1)]
    backward = [(i + 1, i) for i in range(count - 1)]
    n = block.shape[-1]
    low = lax.ppermute(block[..., n - width :], TM, forward)
    high = lax.ppermute(block[..., :width], TM, backward)
    return jnp.concatenate([low, block, high], axis=-1)


def correlate(left, right):
    return jnp.einsum(
        "rfs,rgs->rfg", left, right, precision=lax.Precision.HIGH, preferred_element_type=jnp.float32
    )


def per_device(frames, pixel_order, cycle_sizes, kernel):
    block = frames[0]
    sub, pixels = block.shape
    cycles = cycle_sizes.shape[0]
    cap = 2 * pixels // cycles
    groups = lax.axis_size(PIX)
    owned = cycles // groups
    half = owned // 2
    window = owned * cap
    starts = (jnp.cumsum(cycle_sizes) - cycle_sizes).astype(jnp.int32)
    me = lax.axis_index(PIX)

    ordered = jnp.take(block.T, pixel_order, axis=0)
    ordered = jnp.pad(ordered, ((0, window), (0, 0)))
    chunks = jnp.stack(
        [lax.dynamic_slice_in_dim(ordered, starts[d * owned], window, 0) for d in range(groups)]
    )
    got = lax.all_to_all(chunks, PIX, 0, 0, tiled=True)
    got = jnp.pad(got, ((0, 0), (0, cap), (0, 0)))

    base = starts[me * owned]
    slots = jnp.arange(cap, dtype=jnp.int32)
    picked = []
    for l in range(owned):
        r = me * owned + l
        rows = lax.dynamic_slice_in_dim(got, starts[r] - base, cap, 1)
        picked.append(jnp.where((slots < cycle_sizes[r])[None, :, None], rows, 0.0))
    picked = jnp.stack(picked)
    picked = jnp.transpose(picked, (0, 2, 1, 3)).reshape(owned, cap, groups * sub)
    tblk = groups * sub

    total = jnp.sum(picked, axis=1, keepdims=True)
    scaled = picked / total
    rimmed = halo_frames(scaled, REACH)
    smooth = kernel[0] * rimmed[..., 0:tblk]
    for shift_step in range(1, 2 * REACH + 1):
        smooth = smooth + kernel[shift_step] * rimmed[..., shift_step : shift_step + tblk]
    smooth = jnp.swapaxes(smooth, 1, 2)

    core = lax.axis_index("c")
    keep = lax.dynamic_slice_in_dim(smooth, core * half, half, 0)
    give = lax.dynamic_slice_in_dim(smooth, (1 - core) * half, half, 0)
    other = lax.ppermute(give, "c", [(0, 1), (1, 0)])
    pair = jnp.where(core == 0, jnp.concatenate([keep, other], 1), jnp.concatenate([other, keep], 1))
    right = lax.all_gather(pair, CHIPS, axis=1, tiled=True)

    scale = lax.dynamic_slice_in_dim(cycle_sizes, me * owned + core * half, half).astype(jnp.float32)
    scale = scale[:, None, None]
    sent = correlate(other * scale, right)
    back = lax.ppermute(sent, "c", [(0, 1), (1, 0)])
    mine = correlate(keep * scale, right)
    return jnp.where(core == 0, jnp.concatenate([mine, back], 0), jnp.concatenate([back, mine], 0))


def solution(mesh):
    pix, tm = mesh.shape["pix"], mesh.shape["tm"]
    fine = Mesh(mesh.devices.reshape(2, pix // 2, tm // 4, 2, 2), PIX + TM)
    placed = (P(TM, PIX, None), P(), P(), P())
    return jax.shard_map(
        per_device, mesh=fine, in_specs=placed, out_specs=P(PIX, TM, None), check_vma=False
    )
```

time: 414 us -> 595 us (1.44)
  waiting for transfers between devices: 315 us -> 386 us
  local copies, waits for them, and re-layouts: 28.6 us -> 83.7 us
  other arithmetic: 8.1 us -> 41.4 us
  between operations: 13.5 us -> 37.4 us
  Pallas kernels: 14.4 us -> 0 us
  starting transfers between devices: 5.46 us -> 14.9 us
    all_gather x2 -> x1, waiting for transfers between devices: 313 us -> 365 us  [per_device(): right = lax.all_gather(pair, CHIPS, axis=1, tiled=True)]
    gather x0 -> x1, local copies, waits for them, and re-layouts: none -> 43.9 us  [per_device(): ordered = jnp.take(block.T, pixel_order, axis=0)]
    select_n x0 -> x3, other arithmetic: none -> 25.9 us  [the longest x1 15.7 us: per_device(): jnp.where(core == 0, jnp.concatenate([mine, back], 0), jnp.concatenate([b...]
    dynamic_slice x0 -> x11, local copies, waits for them, and re-layouts: none -> 23.6 us  [the longest x9 21.8 us: per_device(): lax.dynamic_slice_in_dim(ordered, starts[d * owned], window, 0)]
    all_gather x1 -> x0, local copies, waits for them, and re-layouts: 22.1 us -> none  [per_device(): series = lax.all_gather(block, 'pix', axis=0, tiled=True)]
    all_to_all x0 -> x1, waiting for transfers between devices: none -> 15.2 us  [per_device(): got = lax.all_to_all(chunks, PIX, 0, 0, tiled=True)]
    pallas_call x1 -> x0, Pallas kernels: 14.4 us -> none  [pick(): pl.pallas_call(functools.partial(pick_kernel, owned, cap), out_shape=jax....]
    unnamed x9 -> x32, local copies, waits for them, and re-layouts: 3.53 us -> 14 us
  transfers between devices with their start and end apart: 4 -> 6, of which waited for: 3 -> 5; matrix products, arithmetic and copies ran while one was open for 0% -> 3% of each run, Pallas kernels for 0% -> 0%
where the time goes in v2:
time: 595 us; the launch traced here: 594 us
  waiting for transfers between devices  386 us (65%)
  local copies, waits for them, and re-layouts  83.7 us (14%)
  other arithmetic  41.4 us (7%)
  between operations  37.4 us (6%)
  matrix products  30.1 us (5%)
  starting transfers between devices  14.9 us (3%)
    all_gather x1, waiting for transfers between devices, per_device(): right = lax.all_gather(pair, CHIPS, axis=1, tiled=True)  365 us
    gather x1, local copies, waits for them, and re-layouts, per_device(): ordered = jnp.take(block.T, pixel_order, axis=0)  43.9 us
    dot_general x2, matrix products, correlate(): jnp.einsum('rfs,rgs->rfg', left, right, precision=lax.Precision.HIGH, pre...  30.1 us
    dynamic_slice x9, local copies, waits for them, and re-layouts, per_device(): lax.dynamic_slice_in_dim(ordered, starts[d * owned], window, 0)  21.8 us
    select_n x1, other arithmetic, per_device(): jnp.where(core == 0, jnp.concatenate([mine, back], 0), jnp.concatenate([b...  15.7 us
    all_to_all x1, waiting for transfers between devices, per_device(): got = lax.all_to_all(chunks, PIX, 0, 0, tiled=True)  15.2 us
    unnamed x32, local copies, waits for them, and re-layouts  14 us
  transfers between devices with their start and end apart: 6, of which 5 were waited for; matrix products, arithmetic and copies ran while one was open for 3% of the time, Pallas kernels for 0%

profile of v2, /device:TPU:1, one launch (start us, length us, event | category | flops | bytes accessed | tf_op | source)
XLA Modules:
  0.0 593.9 jit_solution(16584004930738798835)
XLA Ops:
  8.2 1.7 fusion.42
  21.5 4.9 copy.7
  31.3 43.9 %gather_fusion = f32[12288,24]{1,0:T(8,128)} fusion(f32[12288,24]{1,0:T(8,128)} %bitcast.91, s32[12288]{0:T(1024)S(1)} %fusion.39), kind=kCustom, calls=%fused_computation | custom fusion | bytes 2408448 | tf_op jit(solution)/shard_map/jit(_take)/gather | solution.py:41
  75.2 8.6 %broadcast_select_fusion = f32[12288,24]{1,0:T(8,128)S(1)} fusion(f32[12288,24]{1,0:T(8,128)} %gather_fusion, pred[12288]{0:T(1024)(128)(4,1)S(1)} %compare_and_fusion), kind=kLoop, calls=%fused_computation.10 | loop fusion | flops 294912 | bytes 2371584 | tf_op jit(solution)/shard_map/jit(_take)/select_n | solution.py:41
  83.8 7.3 %pad_dynamic-slice_fusion = (f32[3072,24]{1,0:T(8,128)}, f32[3072,24]{1,0:T(8,128)}, f32[3072,24]{1,0:T(8,128)}, f32[3072,24]{1,0:T(8,128)}, f32[3072,24]{1,0:T(...) fusion(s32[]{:T(128)S(6)} %select_n.149, f32[12288,24]{1,0:T(8,128)S(1)} %broadcast_select_fusion, ...), kind=kLoop, calls=%fused_computation.2 | loop fusion | bytes 3538976 | tf_op jit(solution)/shard_map/dynamic_slice | solution.py:44
  91.1 2.0 copy.16
  93.1 2.6 copy.10
  98.0 2.7 copy.13
  100.7 2.6 copy.14
  105.6 1.7 bitcast_dynamic-update-slice_fusion.7
  107.3 1.7 bitcast_dynamic-update-slice_fusion.6
  113.4 8.5 %all-to-all-start = ((f32[8,3072,24]{1,2,0:T(8,128)}), f32[8,3072,24]{1,2,0:T(8,128)S(1)}, u32[]{:S(2)}, u32[]{:S(2)}) async-start(f32[8,3072,24]{1,2,0:T(8,128)} %bitcast_dynamic-update-slice_fusion), calls=%async_computation | async-start | bytes 4718592 | tf_op jit(solution)/shard_map/all_to_all | solution.py:46
  135.7 15.2 %all-to-all-done = f32[8,3072,24]{1,2,0:T(8,128)S(1)} async-done(((f32[8,3072,24]{1,2,0:T(8,128)}), f32[8,3072,24]{1,2,0:T(8,128)S(1)}, u32[]{:S(2)}, u32[]{:S(2)}) %all-to-all-start) | async-done | bytes 2359328 | tf_op jit(solution)/shard_map/all_to_all | solution.py:46
  153.8 2.0 bitcast_divide_fusion
  155.8 3.4 collective-permute-start
  159.2 1.9 collective-permute-start.1
  161.8 2.5 collective-permute-done.1
  164.3 4.7 fusion.3
  169.5 2.8 collective-permute-done.2
  172.3 1.6 maximum_select_fusion.1
  174.6 364.7 %all-gather.2.cloned.1.call-done = f32[4,3072,384]{2,1,0:T(8,128)} async-done(((f32[4,384,384]{2,1,0:T(8,128)}), f32[4,3072,384]{2,1,0:T(8,128)}) %all-gather.2.cloned.1.call-update) | async-done | bytes 18874384 | tf_op jit(solution)/shard_map/all_gather | solution.py:73
  539.3 16.5 %fusion.10 = f32[4,192,3072]{2,1,0:T(8,128)} fusion(f32[4,3072,384]{2,1,0:T(8,128)} %all-gather.2.cloned.1.call-done, f32[4,192,384]{2,1,0:T(8,128)S(1)} %collective-permute-done.2, f32[4]{0:T(128)S(1)} %dynamic-slice_convert_fusion), kind=kOutput, calls=%fused_computation.37 | convolution fusion | flops 5436112896 | bytes 29491216 | tf_op jit(solution)/shard_map/rfs,rgs->rfg/dot_general | solution.py:24
  556.7 13.6 %fusion.12 = f32[4,192,3072]{2,1,0:T(8,128)S(1)} fusion(f32[4,3072,384]{2,1,0:T(8,128)} %all-gather.2.cloned.1.call-done, f32[4,192,384]{2,1,0:T(8,128)S(1)} %get-tuple-element.13, f32[4]{0:T(128)S(1)} %dynamic-slice_convert_fusion), kind=kOutput, calls=%fused_computation.40 | convolution fusion | flops 5436112896 | bytes 29491216 | tf_op jit(solution)/shard_map/rfs,rgs->rfg/dot_general | solution.py:24
  571.3 15.7 %maximum_select_fusion = f32[8,192,3072]{2,1,0:T(8,128)} fusion(f32[4,192,3072]{2,1,0:T(8,128)} %collective-permute-done.3, f32[4,192,3072]{2,1,0:T(8,128)S(1)} %fusion.12, pred[]{:T(512)S(6)} %eq.4), kind=kLoop, calls=%fused_computation.1 | loop fusion | flops 14155776 | bytes 37748736 | tf_op jit(solution)/shard_map/jit(_where)/select_n | solution.py:80
  (68 shorter events, 23.9 us)
Async XLA Ops:
  91.1 4.6 copy-start.4
  91.1 5.8 copy-start.3
  96.8 6.4 %copy-start.2 = (f32[3072,24]{1,0:T(8,128)S(1)}, f32[3072,24]{1,0:T(8,128)}, u32[]{:S(2)}) copy-start(f32[3072,24]{1,0:T(8,128)} %get-tuple-element.11) | copy-start | bytes 884740
  98.0 6.4 %copy-start.1 = (f32[3072,24]{1,0:T(8,128)S(1)}, f32[3072,24]{1,0:T(8,128)}, u32[]{:S(2)}) copy-start(f32[3072,24]{1,0:T(8,128)} %get-tuple-element.12) | copy-start | bytes 884740
  104.4 4.6 copy-start.9
  104.4 5.3 copy-start.8
  104.4 6.0 %copy-start.7 = (f32[3072,24]{0,1:T(8,128)S(1)}, f32[3072,24]{0,1:T(8,128)}, u32[]{:S(2)}) copy-start(f32[3072,24]{0,1:T(8,128)} %copy.13) | copy-start | bytes 884740
  104.4 6.8 %copy-start.6 = (f32[3072,24]{0,1:T(8,128)S(1)}, f32[3072,24]{0,1:T(8,128)}, u32[]{:S(2)}) copy-start(f32[3072,24]{0,1:T(8,128)} %copy.14) | copy-start | bytes 884740
  104.4 7.5 %copy-start.5 = (f32[3072,24]{0,1:T(8,128)S(1)}, f32[3072,24]{0,1:T(8,128)}, u32[]{:S(2)}) copy-start(f32[3072,24]{0,1:T(8,128)} %copy.15) | copy-start | bytes 884740
  113.4 37.5 %all-to-all-start = ((f32[8,3072,24]{1,2,0:T(8,128)}), f32[8,3072,24]{1,2,0:T(8,128)S(1)}, u32[]{:S(2)}, u32[]{:S(2)}) async-start(f32[8,3072,24]{1,2,0:T(8,128)} %bitcast_dynamic-update-slice_fusion), calls=%async_computation | async-start | bytes 4718592 | tf_op jit(solution)/shard_map/all_to_all | solution.py:46
  121.9 417.4 %all-gather.2.cloned.1.call-start = ((), (), s32[]{:S(2)}) async-start(), calls=%async_computation.1 | async-start | bytes 21233664 | tf_op jit(solution)/shard_map/all_gather | solution.py:73
  152.1 1.4 copy-start
  153.8 7.3 %copy-start.11 = (f32[5]{0:T(128)S(1)}, f32[5]{0:T(128)}, u32[]{:S(2)}) copy-start(f32[5]{0:T(128)} %param.7) | copy-start | bytes 64
  155.8 6.0 %collective-permute-start = (f32[8,384,2]{1,2,0:T(2,128)S(1)}, f32[8,384,2]{1,2,0:T(2,128)S(1)}, u32[]{:S(2)}, u32[]{:S(2)}) collective-permute-start(f32[8,384,2]{1,2,0:T(2,128)S(1)} %get-tuple-element.15), channel_id=1, source_target_pairs={{0,1},{1,2},{2,3},{3,4},{4,5},{5,6},{6,7},{7,8},{8,9},{9,10},{10,1... | collective-permute-start | bytes 73736 | tf_op jit(solution)/shard_map/ppermute | solution.py:18
  159.2 5.1 collective-permute-start.1
  169.2 3.1 collective-permute-start.2
  173.9 0.7 copy-start.10
  555.8 15.5 %collective-permute-start.3 = (f32[4,192,3072]{2,1,0:T(8,128)}, f32[4,192,3072]{2,1,0:T(8,128)}, u32[]{:S(2)}, u32[]{:S(2)}) collective-permute-start(f32[4,192,3072]{2,1,0:T(8,128)} %fusion.10), channel_id=1, source_target_pairs={{0,1},{1,0},{2,3},{3,2},{4,5},{5,4},{6,7},{7,6},{8,9},{9,8},{10,11... | collective-permute-start | bytes 28311560 | tf_op jit(solution)/shard_map/ppermute | solution.py:78
Sparse Core Ops, SparseCore 0:
  174.0 365.2 all-gather.1

commit v3 on v2

--- a/solution.py
+++ b/solution.py
@@ -66,11 +66,14 @@
     smooth = jnp.swapaxes(smooth, 1, 2)
 
     core = lax.axis_index("c")
+    spots = lax.axis_size(TM)
+    chunks = jnp.broadcast_to(smooth.reshape(1, 2, half, tblk, cap), (spots // 2, 2, half, tblk, cap))
+    chunks = chunks.reshape(spots * half, tblk, cap)
+    right = lax.all_to_all(chunks, TM, 0, 1, tiled=True)
+
     keep = lax.dynamic_slice_in_dim(smooth, core * half, half, 0)
-    give = lax.dynamic_slice_in_dim(smooth, (1 - core) * half, half, 0)
-    other = lax.ppermute(give, "c", [(0, 1), (1, 0)])
-    pair = jnp.where(core == 0, jnp.concatenate([keep, other], 1), jnp.concatenate([other, keep], 1))
-    right = lax.all_gather(pair, CHIPS, axis=1, tiled=True)
+    sibling = lax.axis_index(TM) + 1 - 2 * core
+    other = lax.dynamic_slice_in_dim(right, sibling * tblk, tblk, 1)
 
     scale = lax.dynamic_slice_in_dim(cycle_sizes, me * owned + core * half, half).astype(jnp.float32)
     scale = scale[:, None, None]

time: 595 us -> 543 us (0.913)
  waiting for transfers between devices: 386 us -> 323 us
  local copies, waits for them, and re-layouts: 83.7 us -> 102 us
  between operations: 37.4 us -> 23.9 us
  starting transfers between devices: 14.9 us -> 21.4 us
    all_gather x1 -> x0, waiting for transfers between devices: 365 us -> none  [per_device(): right = lax.all_gather(pair, CHIPS, axis=1, tiled=True)]
    all_to_all x0 -> x1, waiting for transfers between devices: none -> 305 us  [per_device(): right = lax.all_to_all(chunks, TM, 0, 1, tiled=True)]
    all_to_all x0 -> x1, local copies, waits for them, and re-layouts: none -> 12.8 us  [per_device(): right = lax.all_to_all(chunks, TM, 0, 1, tiled=True)]
    broadcast_in_dim x0 -> x1, local copies, waits for them, and re-layouts: none -> 9.13 us  [per_device(): jnp.broadcast_to(smooth.reshape(1, 2, half, tblk, cap), (spots // 2, 2, h...]
    all_to_all x0 -> x1, starting transfers between devices: none -> 6.87 us  [per_device(): right = lax.all_to_all(chunks, TM, 0, 1, tiled=True)]
    unnamed x32 -> x30, local copies, waits for them, and re-layouts: 14 us -> 12.4 us
  transfers between devices with their start and end apart: 6 -> 5, of which waited for: 5 -> 4; matrix products, arithmetic and copies ran while one was open for 3% -> 4% of each run, Pallas kernels for 0% -> 0%
where the time goes in v3:
time: 543 us; the launch traced here: 542 us
  waiting for transfers between devices  323 us (59%)
  local copies, waits for them, and re-layouts  102 us (19%)
  other arithmetic  39.8 us (7%)
  matrix products  30.6 us (6%)
  between operations  23.9 us (4%)
  starting transfers between devices  21.4 us (4%)
    all_to_all x1, waiting for transfers between devices, per_device(): right = lax.all_to_all(chunks, TM, 0, 1, tiled=True)  305 us
    gather x1, local copies, waits for them, and re-layouts, per_device(): ordered = jnp.take(block.T, pixel_order, axis=0)  43.9 us
    dot_general x2, matrix products, correlate(): jnp.einsum('rfs,rgs->rfg', left, right, precision=lax.Precision.HIGH, pre...  30.6 us
    dynamic_slice x9, local copies, waits for them, and re-layouts, per_device(): lax.dynamic_slice_in_dim(ordered, starts[d * owned], window, 0)  20.3 us
    select_n x1, other arithmetic, per_device(): jnp.where(core == 0, jnp.concatenate([mine, back], 0), jnp.concatenate([b...  15.7 us
    all_to_all x1, waiting for transfers between devices, per_device(): got = lax.all_to_all(chunks, PIX, 0, 0, tiled=True)  15.1 us
    all_to_all x1, local copies, waits for them, and re-layouts, per_device(): right = lax.all_to_all(chunks, TM, 0, 1, tiled=True)  12.8 us
    unnamed x30, local copies, waits for them, and re-layouts  12.4 us
  transfers between devices with their start and end apart: 5, of which 4 were waited for; matrix products, arithmetic and copies ran while one was open for 4% of the time, Pallas kernels for 0%

profile of v3, /device:TPU:1, one launch (start us, length us, event | category | flops | bytes accessed | tf_op | source)
XLA Modules:
  0.0 541.5 jit_solution(9563031401118302733)
XLA Ops:
  1.6 1.7 fusion.46
  14.8 4.9 copy.17
  24.6 43.9 %gather_fusion = f32[12288,24]{1,0:T(8,128)} fusion(f32[12288,24]{1,0:T(8,128)} %bitcast.95, s32[12288]{0:T(1024)S(1)} %fusion.41), kind=kCustom, calls=%fused_computation | custom fusion | bytes 2408448 | tf_op jit(solution)/shard_map/jit(_take)/gather | solution.py:41
  68.5 8.6 %broadcast_select_fusion = f32[12288,24]{1,0:T(8,128)S(1)} fusion(f32[12288,24]{1,0:T(8,128)} %gather_fusion, pred[12288]{0:T(1024)(128)(4,1)S(1)} %compare_and_fusion), kind=kLoop, calls=%fused_computation.10 | loop fusion | flops 294912 | bytes 2371584 | tf_op jit(solution)/shard_map/jit(_take)/select_n | solution.py:41
  77.1 7.3 %pad_dynamic-slice_fusion = (f32[3072,24]{1,0:T(8,128)}, f32[3072,24]{1,0:T(8,128)}, f32[3072,24]{1,0:T(8,128)}, f32[3072,24]{1,0:T(8,128)}, f32[3072,24]{1,0:T(...) fusion(s32[]{:T(128)S(6)} %select_n.141, f32[12288,24]{1,0:T(8,128)S(1)} %broadcast_select_fusion, ...), kind=kLoop, calls=%fused_computation.2 | loop fusion | bytes 3538976 | tf_op jit(solution)/shard_map/dynamic_slice | solution.py:44
  84.4 2.0 copy.19
  87.1 2.6 copy.20
  92.0 2.7 copy.23
  94.7 2.6 copy.24
  98.2 1.7 bitcast_dynamic-update-slice_fusion.6
  104.3 8.5 %all-to-all-start = ((f32[8,3072,24]{1,2,0:T(8,128)}), f32[8,3072,24]{1,2,0:T(8,128)S(1)}, u32[]{:S(2)}, u32[]{:S(2)}) async-start(f32[8,3072,24]{1,2,0:T(8,128)} %bitcast_dynamic-update-slice_fusion), calls=%async_computation | async-start | bytes 4718592 | tf_op jit(solution)/shard_map/all_to_all | solution.py:46
  126.7 15.1 %all-to-all-done = f32[8,3072,24]{1,2,0:T(8,128)S(1)} async-done(((f32[8,3072,24]{1,2,0:T(8,128)}), f32[8,3072,24]{1,2,0:T(8,128)S(1)}, u32[]{:S(2)}, u32[]{:S(2)}) %all-to-all-start) | async-done | bytes 2359328 | tf_op jit(solution)/shard_map/all_to_all | solution.py:46
  144.7 2.0 bitcast_divide_fusion
  146.7 3.4 collective-permute-start
  150.1 2.1 collective-permute-start.1
  152.8 2.4 collective-permute-done.1
  155.2 4.6 fusion.3
  159.8 9.1 %broadcast_in_dim.96 = f32[8,2,4,192,384]{4,3,2,1,0:T(8,128)} broadcast(f32[2,4,192,384]{3,2,1,0:T(8,128)S(1)} %bitcast.99), dimensions={1,2,3,4} | broadcast | bytes 21233664 | tf_op jit(solution)/shard_map/broadcast_in_dim | solution.py:70
  169.0 6.9 %all-to-all-start.1 = ((f32[64,192,384]{2,1,0:T(8,128)}), f32[64,192,384]{2,1,0:T(8,128)}, u32[]{:S(2)}, u32[]{:S(2)}) async-start(f32[64,192,384]{2,1,0:T(8,128)} %bitcast.98), calls=%async_computation.1 | async-start | bytes 37748736 | tf_op jit(solution)/shard_map/all_to_all | solution.py:72
  175.9 304.8 %all-to-all-done.1 = f32[64,192,384]{2,1,0:T(8,128)} async-done(((f32[64,192,384]{2,1,0:T(8,128)}), f32[64,192,384]{2,1,0:T(8,128)}, u32[]{:S(2)}, u32[]{:S(2)}) %all-to-all-start.1) | async-done | bytes 18874400 | tf_op jit(solution)/shard_map/all_to_all | solution.py:72
  480.8 12.8 %copy.27 = f32[4,16,192,384]{3,2,1,0:T(8,128)} copy(f32[4,16,192,384]{3,2,0,1:T(8,128)} %bitcast.53) | data formatting | bytes 37748736 | tf_op jit(solution)/shard_map/all_to_all | solution.py:72
  493.6 17.0 %fusion.10 = f32[4,192,3072]{2,1,0:T(8,128)} fusion(f32[4,3072,384]{2,1,0:T(8,128)} %bitcast.96, s32[]{:T(128)S(6)} %select_n.166, f32[4]{0:T(128)S(1)} %dynamic-slice_convert_fusion), kind=kOutput, calls=%fused_computation.36 | convolution fusion | flops 5436112896 | bytes 29491220 | tf_op jit(solution)/shard_map/rfs,rgs->rfg/dot_general | solution.py:24
  511.1 13.6 %fusion.13 = f32[4,192,3072]{2,1,0:T(8,128)S(1)} fusion(f32[4,3072,384]{2,1,0:T(8,128)} %bitcast.97, f32[8,384,192]{1,2,0:T(8,128)S(1)} %fusion.3, s32[]{:T(128)S(6)} %select_n.164, f32[4]{0:T(128)S(1)} %dynamic-slice_convert_fusion), kind=kOutput, calls=%fused_computation.39 | convolution fusion | flops 5436112896 | bytes 29491716 | tf_op jit(solution)/shard_map/rfs,rgs->rfg/dot_general | solution.py:24
  525.8 15.7 %maximum_select_fusion = f32[8,192,3072]{2,1,0:T(8,128)} fusion(f32[4,192,3072]{2,1,0:T(8,128)} %collective-permute-done.2, f32[4,192,3072]{2,1,0:T(8,128)S(1)} %fusion.13, pred[]{:T(512)S(6)} %eq.3), kind=kLoop, calls=%fused_computation.1 | loop fusion | flops 14155776 | bytes 37748736 | tf_op jit(solution)/shard_map/jit(_where)/select_n | solution.py:83
  (63 shorter events, 21.8 us)
Async XLA Ops:
  84.4 5.3 copy-start.4
  86.3 4.5 copy-start.3
  90.8 6.5 %copy-start.2 = (f32[3072,24]{1,0:T(8,128)S(1)}, f32[3072,24]{1,0:T(8,128)}, u32[]{:S(2)}) copy-start(f32[3072,24]{1,0:T(8,128)} %get-tuple-element.11) | copy-start | bytes 884740
  92.0 5.8 %copy-start.1 = (f32[3072,24]{1,0:T(8,128)S(1)}, f32[3072,24]{1,0:T(8,128)}, u32[]{:S(2)}) copy-start(f32[3072,24]{1,0:T(8,128)} %get-tuple-element.5) | copy-start | bytes 884740
  97.7 2.2 copy-start.8
  97.7 2.9 copy-start.7
  97.7 3.6 copy-start.6
  97.7 4.4 copy-start.5
  104.3 37.5 %all-to-all-start = ((f32[8,3072,24]{1,2,0:T(8,128)}), f32[8,3072,24]{1,2,0:T(8,128)S(1)}, u32[]{:S(2)}, u32[]{:S(2)}) async-start(f32[8,3072,24]{1,2,0:T(8,128)} %bitcast_dynamic-update-slice_fusion), calls=%async_computation | async-start | bytes 4718592 | tf_op jit(solution)/shard_map/all_to_all | solution.py:46
  142.9 1.4 copy-start
  144.7 7.5 %copy-start.10 = (f32[5]{0:T(128)S(1)}, f32[5]{0:T(128)}, u32[]{:S(2)}) copy-start(f32[5]{0:T(128)} %param.7) | copy-start | bytes 64
  146.7 6.1 %collective-permute-start = (f32[8,384,2]{1,2,0:T(2,128)S(1)}, f32[8,384,2]{1,2,0:T(2,128)S(1)}, u32[]{:S(2)}, u32[]{:S(2)}) collective-permute-start(f32[8,384,2]{1,2,0:T(2,128)S(1)} %get-tuple-element.13), channel_id=1, source_target_pairs={{0,1},{1,2},{2,3},{3,4},{4,5},{5,6},{6,7},{7,8},{8,9},{9,10},{10,1... | collective-permute-start | bytes 73736 | tf_op jit(solution)/shard_map/ppermute | solution.py:18
  150.1 5.1 collective-permute-start.1
  169.0 6.9 %copy-start.9 = (s32[64]{0:T(128)S(1)}, s32[64]{0:T(128)}, u32[]{:S(2)}) copy-start(s32[64]{0:T(128)} %param.6) | copy-start | bytes 772
  169.0 311.8 %all-to-all-start.1 = ((f32[64,192,384]{2,1,0:T(8,128)}), f32[64,192,384]{2,1,0:T(8,128)}, u32[]{:S(2)}, u32[]{:S(2)}) async-start(f32[64,192,384]{2,1,0:T(8,128)} %bitcast.98), calls=%async_computation.1 | async-start | bytes 37748736 | tf_op jit(solution)/shard_map/all_to_all | solution.py:72
  510.6 15.2 %collective-permute-start.2 = (f32[4,192,3072]{2,1,0:T(8,128)}, f32[4,192,3072]{2,1,0:T(8,128)}, u32[]{:S(2)}, u32[]{:S(2)}) collective-permute-start(f32[4,192,3072]{2,1,0:T(8,128)} %fusion.10), channel_id=1, source_target_pairs={{0,1},{1,0},{2,3},{3,2},{4,5},{5,4},{6,7},{7,6},{8,9},{9,8},{10,11... | collective-permute-start | bytes 28311560 | tf_op jit(solution)/shard_map/ppermute | solution.py:81

commit v4 on v2

v4 whole, which is shorter than its diff:
```python
import jax
import jax.numpy as jnp
from jax import lax
from jax.sharding import PartitionSpec as P

REACH = 2
PARTS = 2


def halo_frames(block, width):
    count = lax.axis_size("tm")
    forward = [(i, i + 1) for i in range(count - 1)]
    backward = [(i + 1, i) for i in range(count - 1)]
    n = block.shape[-1]
    low = lax.ppermute(block[..., n - width :], "tm", forward)
    high = lax.ppermute(block[..., :width], "tm", backward)
    return jnp.concatenate([low, block, high], axis=-1)


def correlate(left, right):
    return jnp.einsum(
        "rfs,rgs->rfg", left, right, precision=lax.Precision.HIGH, preferred_element_type=jnp.float32
    )


def per_device(frames, pixel_order, cycle_sizes, kernel):
    block = frames[0]
    sub, pixels = block.shape
    cycles = cycle_sizes.shape[0]
    cap = 2 * pixels // cycles
    groups = lax.axis_size("pix")
    owned = cycles // groups
    step = owned // PARTS
    window = step * cap
    tblk = groups * sub
    starts = (jnp.cumsum(cycle_sizes) - cycle_sizes).astype(jnp.int32)
    me = lax.axis_index("pix")
    slots = jnp.arange(cap, dtype=jnp.int32)

    ordered = jnp.take(block.T, pixel_order, axis=0)
    ordered = jnp.pad(ordered, ((0, window), (0, 0)))

    outs = []
    for part in range(PARTS):
        chunks = jnp.stack(
            [
                lax.dynamic_slice_in_dim(ordered, starts[d * owned + part * step], window, 0)
                for d in range(groups)
            ]
        )
        got = lax.all_to_all(chunks, "pix", 0, 0, tiled=True)
        got = jnp.pad(got, ((0, 0), (0, cap), (0, 0)))
        first = me * owned + part * step
        picked = []
        for l in range(step):
            rows = lax.dynamic_slice_in_dim(got, starts[first + l] - starts[first], cap, 1)
            picked.append(jnp.where((slots < cycle_sizes[first + l])[None, :, None], rows, 0.0))
        picked = jnp.stack(picked)
        picked = jnp.transpose(picked, (0, 2, 1, 3)).reshape(step, cap, tblk)

        total = jnp.sum(picked, axis=1, keepdims=True)
        rimmed = halo_frames(picked / total, REACH)
        smooth = kernel[0] * rimmed[..., 0:tblk]
        for shift_step in range(1, 2 * REACH + 1):
            smooth = smooth + kernel[shift_step] * rimmed[..., shift_step : shift_step + tblk]
        smooth = jnp.swapaxes(smooth, 1, 2)

        scale = lax.dynamic_slice_in_dim(cycle_sizes, first, step).astype(jnp.float32)
        right = lax.all_gather(smooth, "tm", axis=1, tiled=True)
        outs.append(correlate(smooth * scale[:, None, None], right))
    return jnp.concatenate(outs, 0)


def solution(mesh):
    placed = (P("tm", "pix", None), P(), P(), P())
    return jax.shard_map(
        per_device, mesh=mesh, in_specs=placed, out_specs=P("pix", "tm", None), check_vma=False
    )
```

time: 595 us -> 423 us (0.71)
  waiting for transfers between devices: 386 us -> 176 us
  local copies, waits for them, and re-layouts: 83.7 us -> 97.6 us
  between operations: 37.4 us -> 50.9 us
  starting transfers between devices: 14.9 us -> 24.7 us
    all_gather x1 -> x2, waiting for transfers between devices: 365 us -> 138 us  [per_device(): right = lax.all_gather(smooth, 'tm', axis=1, tiled=True)]
    select_n x2 -> x0, other arithmetic: 17.3 us -> none  [the longest x1 15.7 us: per_device(): jnp.where(core == 0, jnp.concatenate([mine, back], 0), jnp.concatenate([b...]
    all_to_all x1 -> x2, waiting for transfers between devices: 15.2 us -> 31.4 us  [per_device(): got = lax.all_to_all(chunks, 'pix', 0, 0, tiled=True)]
    concatenate x0 -> x1, other arithmetic: none -> 10.6 us  [per_device(): return jnp.concatenate(outs, 0)]
    transpose x0 -> x2, other arithmetic: none -> 9.73 us  [per_device(): smooth = jnp.swapaxes(smooth, 1, 2)]
    dynamic_slice x11 -> x20, local copies, waits for them, and re-layouts: 23.6 us -> 29.6 us  [the longest x18 28.2 us: per_device(): lax.dynamic_slice_in_dim(ordered, starts[d * owned + part * step], window...]
    unnamed x32 -> x47, local copies, waits for them, and re-layouts: 14 us -> 19.9 us
    all_to_all x1 -> x2, starting transfers between devices: 8.48 us -> 13.4 us  [per_device(): got = lax.all_to_all(chunks, 'pix', 0, 0, tiled=True)]
  transfers between devices with their start and end apart: 6 -> 8, of which waited for: 5 -> 6; matrix products, arithmetic and copies ran while one was open for 3% -> 10% of each run, Pallas kernels for 0% -> 0%
where the time goes in v4:
time: 423 us; the launch traced here: 421 us
  waiting for transfers between devices  176 us (42%)
  local copies, waits for them, and re-layouts  97.6 us (23%)
  between operations  50.9 us (12%)
  other arithmetic  38.7 us (9%)
  matrix products  33.3 us (8%)
  starting transfers between devices  24.7 us (6%)
    all_gather x2, waiting for transfers between devices, per_device(): right = lax.all_gather(smooth, 'tm', axis=1, tiled=True)  138 us
    gather x1, local copies, waits for them, and re-layouts, per_device(): ordered = jnp.take(block.T, pixel_order, axis=0)  43.9 us
    dot_general x2, matrix products, correlate(): jnp.einsum('rfs,rgs->rfg', left, right, precision=lax.Precision.HIGH, pre...  33.3 us
    all_to_all x2, waiting for transfers between devices, per_device(): got = lax.all_to_all(chunks, 'pix', 0, 0, tiled=True)  31.4 us
    dynamic_slice x18, local copies, waits for them, and re-layouts, per_device(): lax.dynamic_slice_in_dim(ordered, starts[d * owned + part * step], window...  28.2 us
    unnamed x47, local copies, waits for them, and re-layouts  19.9 us
    all_to_all x2, starting transfers between devices, per_device(): got = lax.all_to_all(chunks, 'pix', 0, 0, tiled=True)  13.4 us
    concatenate x1, other arithmetic, per_device(): return jnp.concatenate(outs, 0)  10.6 us
  transfers between devices with their start and end apart: 8, of which 6 were waited for; matrix products, arithmetic and copies ran while one was open for 10% of the time, Pallas kernels for 0%

profile of v4, /device:TPU:1, one launch (start us, length us, event | category | flops | bytes accessed | tf_op | source)
XLA Modules:
  0.0 421.3 jit_solution(16379470149673220710)
XLA Ops:
  31.2 4.9 %copy.7 = f32[1,24,12288]{1,2,0:T(8,128)} copy(f32[1,24,12288]{2,1,0:T(8,128)} %param.4) | data formatting | bytes 2359296 | tf_op args[0]
  40.3 43.9 %gather_fusion = f32[12288,24]{1,0:T(8,128)} fusion(f32[12288,24]{1,0:T(8,128)} %bitcast.103, s32[12288]{0:T(1024)S(1)} %fusion.42), kind=kCustom, calls=%fused_computation | custom fusion | bytes 2408448 | tf_op jit(solution)/shard_map/jit(_take)/gather | solution.py:40
  84.2 8.6 %broadcast_select_fusion = f32[12288,24]{1,0:T(8,128)S(1)} fusion(f32[12288,24]{1,0:T(8,128)} %gather_fusion, pred[12288]{0:T(1024)(128)(4,1)S(1)} %compare_and_fusion), kind=kLoop, calls=%fused_computation.18 | loop fusion | flops 294912 | bytes 2371584 | tf_op jit(solution)/shard_map/jit(_take)/select_n | solution.py:40
  92.8 3.4 pad_dynamic-slice_fusion.15
  96.3 2.1 copy.19
  98.3 2.0 copy.20
  109.0 6.7 %pad_dynamic-slice_fusion.8 = (f32[1536,24]{1,0:T(8,128)}, f32[1536,24]{1,0:T(8,128)}, f32[1536,24]{1,0:T(8,128)}, f32[1536,24]{1,0:T(8,128)}, f32[1536,24]{1,0:...) fusion(s32[]{:T(128)S(6)} %select_n.154, ...), kind=kLoop, calls=%fused_computation.10 | loop fusion | bytes 2506788 | tf_op jit(solution)/shard_map/dynamic_slice | solution.py:47
  115.7 2.0 copy.17
  127.7 8.6 %all-to-all-start.1 = ((f32[8,1536,24]{1,2,0:T(8,128)}), f32[8,1536,24]{1,2,0:T(8,128)S(1)}, u32[]{:S(2)}, u32[]{:S(2)}) async-start(f32[8,1536,24]{1,2,0:T(8,128)} %bitcast_dynamic-update-slice_fusion), calls=%async_computation.1 | async-start | bytes 2359296 | tf_op jit(solution)/shard_map/all_to_all | solution.py:51
  143.3 8.7 %all-to-all-done.1 = f32[8,1536,24]{1,2,0:T(8,128)S(1)} async-done(((f32[8,1536,24]{1,2,0:T(8,128)}), f32[8,1536,24]{1,2,0:T(8,128)S(1)}, u32[]{:S(2)}, u32[]{:S(2)}) %all-to-all-start.1) | async-done | bytes 1179680 | tf_op jit(solution)/shard_map/all_to_all | solution.py:51
  154.2 4.4 %collective-permute-start.2 = (f32[4,384,2]{1,2,0:T(2,128)S(1)}, f32[4,384,2]{1,2,0:T(2,128)S(1)}, u32[]{:S(2)}, u32[]{:S(2)}) collective-permute-start(f32[4,384,2]{1,2,0:T(2,128)S(1)} %get-tuple-element.27), channel_id=1, source_target_pairs={{0,1},{1,2},{2,3},{3,4},{4,5},{5,6},{6,7},{7,8},{8,9},{9,10},{10,1... | collective-permute-start | bytes 36872 | tf_op jit(solution)/shard_map/ppermute | solution.py:15
  161.2 2.4 collective-permute-done.3
  163.6 4.9 %fusion.4 = f32[4,192,384]{2,1,0:T(8,128)} fusion(f32[4,384,192]{1,2,0:T(8,128)S(1)} %bitcast_divide_fusion, f32[4,384,2]{1,2,0:T(2,128)S(1)} %collective-permute-done.3, f32[4,384,2]{1,2,0:T(2,128)S(1)} %collective-permute-done.2, f32[]{:T(128)} %bitcast.36, f32[]{:T(128)} %bitcast.35, f32[]{:T(128)} %bitcast.34, f32[]{:T(128)} %bitcast.33, f32[]{:T(128)} %bitcast), kind=kLoop, calls=%fused_computation.37 | loop fusion | flops 3833856 | bytes 2383892 | tf_op jit(solution)/shard_map/transpose | solution.py:66
  171.9 2.1 copy.10
  183.2 4.8 %all-to-all-start = ((f32[8,1536,24]{1,2,0:T(8,128)}), f32[8,1536,24]{1,2,0:T(8,128)S(1)}, u32[]{:S(2)}, u32[]{:S(2)}) async-start(f32[8,1536,24]{1,2,0:T(8,128)} %bitcast_dynamic-update-slice_fusion.8), calls=%async_computation | async-start | bytes 2359296 | tf_op jit(solution)/shard_map/all_to_all | solution.py:51
  194.3 22.7 %all-to-all-done = f32[8,1536,24]{1,2,0:T(8,128)S(1)} async-done(((f32[8,1536,24]{1,2,0:T(8,128)}), f32[8,1536,24]{1,2,0:T(8,128)S(1)}, u32[]{:S(2)}, u32[]{:S(2)}) %all-to-all-start) | async-done | bytes 1179680 | tf_op jit(solution)/shard_map/all_to_all | solution.py:51
  217.9 2.8 collective-permute-start
  222.6 3.9 collective-permute-done.1
  226.4 4.9 %fusion.13 = f32[4,192,384]{2,1,0:T(8,128)} fusion(f32[4,384,192]{1,2,0:T(8,128)S(1)} %bitcast_divide_fusion.1, f32[4,384,2]{1,2,0:T(2,128)S(1)} %collective-permute-done.1, f32[4,384,2]{1,2,0:T(2,128)S(1)} %collective-permute-done, f32[]{:T(128)} %bitcast.36, f32[]{:T(128)} %bitcast.35, f32[]{:T(128)} %bitcast.34, f32[]{:T(128)} %bitcast.33, f32[]{:T(128)} %bitcast), kind=kLoop, calls=%fused_computation.46 | loop fusion | flops 3833856 | bytes 2383892 | tf_op jit(solution)/shard_map/transpose | solution.py:66
  232.0 51.3 %all-gather.5.cloned.1.call-done = f32[4,3072,384]{2,1,0:T(8,128)} async-done(((f32[4,192,384]{2,1,0:T(8,128)}), f32[4,3072,384]{2,1,0:T(8,128)}) %all-gather.5.cloned.1.call-update) | async-done | bytes 18874384 | tf_op jit(solution)/shard_map/all_gather | solution.py:69
  283.4 16.6 %fusion.22 = f32[4,192,3072]{2,1,0:T(8,128)} fusion(f32[4,3072,384]{2,1,0:T(8,128)} %all-gather.5.cloned.1.call-done, f32[4,192,384]{2,1,0:T(8,128)S(1)} %copy-done.2, f32[4]{0:T(128)S(1)} %get-tuple-element.34), kind=kOutput, calls=%fused_computation.65 | convolution fusion | flops 5436112896 | bytes 29491216 | tf_op jit(solution)/shard_map/rfs,rgs->rfg/dot_general | solution.py:21
  300.0 87.1 %all-gather.3.cloned.1.call-done = f32[4,3072,384]{2,1,0:T(8,128)} async-done(((f32[4,192,384]{2,1,0:T(8,128)}), f32[4,3072,384]{2,1,0:T(8,128)}) %all-gather.3.cloned.1.call-update) | async-done | bytes 18874384 | tf_op jit(solution)/shard_map/all_gather | solution.py:69
  387.1 16.7 %fusion.24 = f32[4,192,3072]{2,1,0:T(8,128)} fusion(f32[4,3072,384]{2,1,0:T(8,128)} %all-gather.3.cloned.1.call-done, f32[4,192,384]{2,1,0:T(8,128)S(1)} %copy-done.3, f32[4]{0:T(128)S(1)} %get-tuple-element.33), kind=kOutput, calls=%fused_computation.67 | convolution fusion | flops 5436112896 | bytes 29491216 | tf_op jit(solution)/shard_map/rfs,rgs->rfg/dot_general | solution.py:21
  403.8 10.6 %pad_maximum_fusion = f32[8,192,3072]{2,1,0:T(8,128)} fusion(f32[4,192,3072]{2,1,0:T(8,128)S(1)} %copy-done, f32[4,192,3072]{2,1,0:T(8,128)} %fusion.24), kind=kLoop, calls=%fused_computation.1 | loop fusion | flops 4718592 | bytes 37748736 | tf_op jit(solution)/shard_map/concatenate | solution.py:71
  (95 shorter events, 44.3 us)
Async XLA Ops:
  92.8 3.5 copy-start.1
  117.8 8.6 %copy-start.6 = (f32[1536,24]{0,1:T(8,128)S(1)}, f32[1536,24]{0,1:T(8,128)}, u32[]{:S(2)}) copy-start(f32[1536,24]{0,1:T(8,128)} %copy.23) | copy-start | bytes 442372
  118.7 6.4 %copy-start.8 = (f32[1536,24]{0,1:T(8,128)S(1)}, f32[1536,24]{0,1:T(8,128)}, u32[]{:S(2)}) copy-start(f32[1536,24]{0,1:T(8,128)} %copy.21) | copy-start | bytes 442372
  118.7 7.0 %copy-start.7 = (f32[1536,24]{0,1:T(8,128)S(1)}, f32[1536,24]{0,1:T(8,128)}, u32[]{:S(2)}) copy-start(f32[1536,24]{0,1:T(8,128)} %copy.22) | copy-start | bytes 442372
  127.7 12.3 %copy-start.13 = (s32[64]{0:T(128)S(1)}, s32[64]{0:T(128)}, u32[]{:S(2)}) copy-start(s32[64]{0:T(128)} %param.6) | copy-start | bytes 772
  127.7 24.3 %all-to-all-start.1 = ((f32[8,1536,24]{1,2,0:T(8,128)}), f32[8,1536,24]{1,2,0:T(8,128)S(1)}, u32[]{:S(2)}, u32[]{:S(2)}) async-start(f32[8,1536,24]{1,2,0:T(8,128)} %bitcast_dynamic-update-slice_fusion), calls=%async_computation.1 | async-start | bytes 2359296 | tf_op jit(solution)/shard_map/all_to_all | solution.py:51
  136.3 147.0 %all-gather.5.cloned.1.call-start = ((), (), s32[]{:S(2)}) async-start(), calls=%async_computation.3 | async-start | bytes 20054016 | tf_op jit(solution)/shard_map/all_gather | solution.py:69
  153.3 7.2 %copy-start.15 = (f32[5]{0:T(128)S(1)}, f32[5]{0:T(128)}, u32[]{:S(2)}) copy-start(f32[5]{0:T(128)} %param.7) | copy-start | bytes 64
  154.2 7.0 %collective-permute-start.2 = (f32[4,384,2]{1,2,0:T(2,128)S(1)}, f32[4,384,2]{1,2,0:T(2,128)S(1)}, u32[]{:S(2)}, u32[]{:S(2)}) collective-permute-start(f32[4,384,2]{1,2,0:T(2,128)S(1)} %get-tuple-element.27), channel_id=1, source_target_pairs={{0,1},{1,2},{2,3},{3,4},{4,5},{5,6},{6,7},{7,8},{8,9},{9,10},{10,1... | collective-permute-start | bytes 36872 | tf_op jit(solution)/shard_map/ppermute | solution.py:15
  158.6 5.0 %collective-permute-start.3 = (f32[4,384,2]{1,2,0:T(2,128)S(1)}, f32[4,384,2]{1,2,0:T(2,128)S(1)}, u32[]{:S(2)}, u32[]{:S(2)}) collective-permute-start(f32[4,384,2]{1,2,0:T(2,128)S(1)} %get-tuple-element.28), channel_id=1, source_target_pairs={{1,0},{2,1},{3,2},{4,3},{5,4},{6,5},{7,6},{8,7},{9,8},{10,9},{11,1... | collective-permute-start | bytes 36872 | tf_op jit(solution)/shard_map/ppermute | solution.py:16
  168.5 1.1 copy-start.5
  170.5 5.5 %copy-start.4 = (f32[1536,24]{1,0:T(8,128)S(1)}, f32[1536,24]{1,0:T(8,128)}, u32[]{:S(2)}) copy-start(f32[1536,24]{1,0:T(8,128)} %get-tuple-element.8) | copy-start | bytes 442372
  176.9 0.9 copy-start.9
  177.2 1.3 copy-start.12
  177.2 2.0 copy-start.11
  177.2 2.7 copy-start.10
  183.2 33.8 %all-to-all-start = ((f32[8,1536,24]{1,2,0:T(8,128)}), f32[8,1536,24]{1,2,0:T(8,128)S(1)}, u32[]{:S(2)}, u32[]{:S(2)}) async-start(f32[8,1536,24]{1,2,0:T(8,128)} %bitcast_dynamic-update-slice_fusion.8), calls=%async_computation | async-start | bytes 2359296 | tf_op jit(solution)/shard_map/all_to_all | solution.py:51
  187.9 199.2 %all-gather.3.cloned.1.call-start = ((), (), s32[]{:S(2)}) async-start(), calls=%async_computation.2 | async-start | bytes 20054016 | tf_op jit(solution)/shard_map/all_gather | solution.py:69
  217.9 4.7 %collective-permute-start = (f32[4,384,2]{1,2,0:T(2,128)S(1)}, f32[4,384,2]{1,2,0:T(2,128)S(1)}, u32[]{:S(2)}, u32[]{:S(2)}) collective-permute-start(f32[4,384,2]{1,2,0:T(2,128)S(1)} %get-tuple-element.21), channel_id=1, source_target_pairs={{0,1},{1,2},{2,3},{3,4},{4,5},{5,6},{6,7},{7,8},{8,9},{9,10},{10,1... | collective-permute-start | bytes 36872 | tf_op jit(solution)/shard_map/ppermute | solution.py:15
  220.6 5.8 %collective-permute-start.1 = (f32[4,384,2]{1,2,0:T(2,128)S(1)}, f32[4,384,2]{1,2,0:T(2,128)S(1)}, u32[]{:S(2)}, u32[]{:S(2)}) collective-permute-start(f32[4,384,2]{1,2,0:T(2,128)S(1)} %get-tuple-element.22), channel_id=1, source_target_pairs={{1,0},{2,1},{3,2},{4,3},{5,4},{6,5},{7,6},{8,7},{9,8},{10,9},{11,1... | collective-permute-start | bytes 36872 | tf_op jit(solution)/shard_map/ppermute | solution.py:16
  231.3 0.7 copy-start.14
  231.3 52.1 %copy-start.2 = (f32[4,192,384]{2,1,0:T(8,128)S(1)}, f32[4,192,384]{2,1,0:T(8,128)}, u32[]{:S(2)}) copy-start(f32[4,192,384]{2,1,0:T(8,128)} %fusion.4) | copy-start | bytes 3538948
  283.4 103.7 %copy-start.3 = (f32[4,192,384]{2,1,0:T(8,128)S(1)}, f32[4,192,384]{2,1,0:T(8,128)}, u32[]{:S(2)}) copy-start(f32[4,192,384]{2,1,0:T(8,128)} %fusion.13) | copy-start | bytes 3538948
  387.1 16.7 %copy-start = (f32[4,192,3072]{2,1,0:T(8,128)S(1)}, f32[4,192,3072]{2,1,0:T(8,128)}, u32[]{:S(2)}) copy-start(f32[4,192,3072]{2,1,0:T(8,128)} %fusion.22) | copy-start | bytes 28311556
Sparse Core Ops, SparseCore 0:
  168.6 114.7 all-gather.4
  285.0 102.0 all-gather.2

commit v5 on v4

--- a/solution.py
+++ b/solution.py
@@ -4,7 +4,7 @@
 from jax.sharding import PartitionSpec as P
 
 REACH = 2
-PARTS = 2
+PARTS = 4
 
 
 def halo_frames(block, width):
@@ -37,17 +37,18 @@
     me = lax.axis_index("pix")
     slots = jnp.arange(cap, dtype=jnp.int32)
 
-    ordered = jnp.take(block.T, pixel_order, axis=0)
-    ordered = jnp.pad(ordered, ((0, window), (0, 0)))
+    order = jnp.pad(pixel_order, (0, window))
+    series = block.T
 
     outs = []
     for part in range(PARTS):
-        chunks = jnp.stack(
+        wanted = jnp.stack(
             [
-                lax.dynamic_slice_in_dim(ordered, starts[d * owned + part * step], window, 0)
+                lax.dynamic_slice_in_dim(order, starts[d * owned + part * step], window, 0)
                 for d in range(groups)
             ]
         )
+        chunks = jnp.take(series, wanted, axis=0)
         got = lax.all_to_all(chunks, "pix", 0, 0, tiled=True)
         got = jnp.pad(got, ((0, 0), (0, cap), (0, 0)))
         first = me * owned + part * step

time: 423 us -> 396 us (0.936)
  waiting for transfers between devices: 176 us -> 93.6 us
  between operations: 50.9 us -> 78.8 us
  starting transfers between devices: 24.7 us -> 42.9 us
  matrix products: 33.3 us -> 42.1 us
    all_gather x2 -> x4, waiting for transfers between devices: 138 us -> 33.7 us  [per_device(): right = lax.all_gather(smooth, 'tm', axis=1, tiled=True)]
    gather x1 -> x8, local copies, waits for them, and re-layouts: 43.9 us -> 83 us  [per_device(): chunks = jnp.take(series, wanted, axis=0)]
    dynamic_slice x19 -> x4, local copies, waits for them, and re-layouts: 28.9 us -> 2.14 us  [per_device(): lax.dynamic_slice_in_dim(order, starts[d * owned + part * step], window, 0)]
    all_to_all x2 -> x4, waiting for transfers between devices: 31.4 us -> 48 us  [per_device(): got = lax.all_to_all(chunks, 'pix', 0, 0, tiled=True)]
    unnamed x47 -> x19, local copies, waits for them, and re-layouts: 19.9 us -> 4.9 us
    dot_general x2 -> x4, matrix products: 33.3 us -> 42.1 us  [correlate(): jnp.einsum('rfs,rgs->rfg', left, right, precision=lax.Precision.HIGH, pre...]
    all_to_all x2 -> x4, starting transfers between devices: 13.4 us -> 21.6 us  [per_device(): got = lax.all_to_all(chunks, 'pix', 0, 0, tiled=True)]
    transpose x2 -> x4, other arithmetic: 9.73 us -> 16.9 us  [per_device(): smooth = jnp.swapaxes(smooth, 1, 2)]
  transfers between devices with their start and end apart: 8 -> 16, of which waited for: 6 -> 9; matrix products, arithmetic and copies ran while one was open for 10% -> 32% of each run, Pallas kernels for 0% -> 0%
where the time goes in v5:
time: 396 us; the launch traced here: 394 us
  local copies, waits for them, and re-layouts  94.9 us (24%)
  waiting for transfers between devices  93.6 us (24%)
  between operations  78.8 us (20%)
  starting transfers between devices  42.9 us (11%)
  matrix products  42.1 us (11%)
  other arithmetic  41.3 us (10%)
    gather x8, local copies, waits for them, and re-layouts, per_device(): chunks = jnp.take(series, wanted, axis=0)  83 us
    all_to_all x4, waiting for transfers between devices, per_device(): got = lax.all_to_all(chunks, 'pix', 0, 0, tiled=True)  48 us
    dot_general x4, matrix products, correlate(): jnp.einsum('rfs,rgs->rfg', left, right, precision=lax.Precision.HIGH, pre...  42.1 us
    all_gather x4, waiting for transfers between devices, per_device(): right = lax.all_gather(smooth, 'tm', axis=1, tiled=True)  33.7 us
    all_to_all x4, starting transfers between devices, per_device(): got = lax.all_to_all(chunks, 'pix', 0, 0, tiled=True)  21.6 us
    transpose x4, other arithmetic, per_device(): smooth = jnp.swapaxes(smooth, 1, 2)  16.9 us
    ppermute x4, starting transfers between devices, halo_frames(): low = lax.ppermute(block[..., n - width:], 'tm', forward)  13.3 us
    ppermute x4, waiting for transfers between devices, halo_frames(): high = lax.ppermute(block[..., :width], 'tm', backward)  11.9 us
  transfers between devices with their start and end apart: 16, of which 9 were waited for; matrix products, arithmetic and copies ran while one was open for 32% of the time, Pallas kernels for 0%

profile of v5, /device:TPU:1, one launch (start us, length us, event | category | flops | bytes accessed | tf_op | source)
XLA Modules:
  0.0 393.6 jit_solution(4242730677922799710)
XLA Ops:
  37.9 4.9 %copy.12 = f32[1,24,12288]{1,2,0:T(8,128)} copy(f32[1,24,12288]{2,1,0:T(8,128)} %param.6) | data formatting | bytes 2359296 | tf_op args[0]
  42.8 18.9 %gather_fusion.3 = f32[6144,24]{1,0:T(8,128)S(1)} fusion(f32[12288,24]{1,0:T(8,128)} %bitcast.105, s32[6144]{0:T(1024)S(1)} %broadcast_clamp_fusion), kind=kCustom, calls=%fused_computation.3.clone | custom fusion | bytes 1204224 | tf_op jit(solution)/shard_map/jit(_take)/gather | solution.py:51
  65.4 8.5 %all-to-all-start.3 = ((f32[8,768,24]{1,2,0:T(8,128)}), f32[8,768,24]{1,2,0:T(8,128)S(1)}, u32[]{:S(2)}, u32[]{:S(2)}) async-start(f32[8,768,24]{1,2,0:T(8,128)} %broadcast_select_fusion), calls=%async_computation.3 | async-start | bytes 1179648 | tf_op jit(solution)/shard_map/all_to_all | solution.py:52
  77.3 6.5 %all-to-all-done.3 = f32[8,768,24]{1,2,0:T(8,128)S(1)} async-done(((f32[8,768,24]{1,2,0:T(8,128)}), f32[8,768,24]{1,2,0:T(8,128)S(1)}, u32[]{:S(2)}, u32[]{:S(2)}) %all-to-all-start.3) | async-done | bytes 589856 | tf_op jit(solution)/shard_map/all_to_all | solution.py:52
  84.3 4.8 %collective-permute-start.6 = (f32[2,384,2]{1,2,0:T(2,128)S(1)}, f32[2,384,2]{1,2,0:T(2,128)S(1)}, u32[]{:S(2)}, u32[]{:S(2)}) collective-permute-start(f32[2,384,2]{1,2,0:T(2,128)S(1)} %get-tuple-element.18), channel_id=1, source_target_pairs={{0,1},{1,2},{2,3},{3,4},{4,5},{5,6},{6,7},{7,8},{8,9},{9,10},{10,1... | collective-permute-start | bytes 18440 | tf_op jit(solution)/shard_map/ppermute | solution.py:15
  94.1 4.2 %fusion.4 = f32[2,192,384]{2,1,0:T(8,128)} fusion(f32[2,384,192]{1,2,0:T(8,128)S(1)} %bitcast_divide_fusion, f32[2,384,2]{1,2,0:T(2,128)S(1)} %collective-permute-done.7, f32[2,384,2]{1,2,0:T(2,128)S(1)} %collective-permute-done.6, f32[]{:T(128)} %bitcast.23, f32[]{:T(128)} %bitcast.22, f32[]{:T(128)} %bitcast.21, f32[]{:T(128)} %bitcast.20, f32[]{:T(128)} %bitcast), kind=kLoop, calls=%fused_computation.29 | loop fusion | flops 1916928 | bytes 1191956 | tf_op jit(solution)/shard_map/transpose | solution.py:67
  115.9 19.0 %gather_fusion.2 = f32[6144,24]{1,0:T(8,128)S(1)} fusion(f32[12288,24]{1,0:T(8,128)} %bitcast.106, s32[6144]{0:T(1024)S(1)} %broadcast_clamp_fusion.1), kind=kCustom, calls=%fused_computation.2.clone | custom fusion | bytes 1204224 | tf_op jit(solution)/shard_map/jit(_take)/gather | solution.py:51
  138.7 3.9 all-to-all-start.2
  145.3 13.7 %all-to-all-done.2 = f32[8,768,24]{1,2,0:T(8,128)S(1)} async-done(((f32[8,768,24]{1,2,0:T(8,128)}), f32[8,768,24]{1,2,0:T(8,128)S(1)}, u32[]{:S(2)}, u32[]{:S(2)}) %all-to-all-start.2) | async-done | bytes 589856 | tf_op jit(solution)/shard_map/all_to_all | solution.py:52
  167.0 4.2 %fusion.13 = f32[2,192,384]{2,1,0:T(8,128)} fusion(f32[2,384,192]{1,2,0:T(8,128)S(1)} %bitcast_divide_fusion.1, f32[2,384,2]{1,2,0:T(2,128)S(1)} %collective-permute-done.5, f32[2,384,2]{1,2,0:T(2,128)S(1)} %collective-permute-done.4, f32[]{:T(128)} %bitcast.23, f32[]{:T(128)} %bitcast.22, f32[]{:T(128)} %bitcast.21, f32[]{:T(128)} %bitcast.20, f32[]{:T(128)} %bitcast), kind=kLoop, calls=%fused_computation.38 | loop fusion | flops 1916928 | bytes 1191956 | tf_op jit(solution)/shard_map/transpose | solution.py:67
  188.7 19.0 %gather_fusion.1 = f32[6144,24]{1,0:T(8,128)S(1)} fusion(f32[12288,24]{1,0:T(8,128)} %bitcast.107, s32[6144]{0:T(1024)S(1)} %broadcast_clamp_fusion.2), kind=kCustom, calls=%fused_computation.1.clone | custom fusion | bytes 1204224 | tf_op jit(solution)/shard_map/jit(_take)/gather | solution.py:51
  211.5 4.7 %all-to-all-start.1 = ((f32[8,768,24]{1,2,0:T(8,128)}), f32[8,768,24]{1,2,0:T(8,128)S(1)}, u32[]{:S(2)}, u32[]{:S(2)}) async-start(f32[8,768,24]{1,2,0:T(8,128)} %broadcast_select_fusion.2), calls=%async_computation.1 | async-start | bytes 1179648 | tf_op jit(solution)/shard_map/all_to_all | solution.py:52
  218.6 13.9 %all-to-all-done.1 = f32[8,768,24]{1,2,0:T(8,128)S(1)} async-done(((f32[8,768,24]{1,2,0:T(8,128)}), f32[8,768,24]{1,2,0:T(8,128)S(1)}, u32[]{:S(2)}, u32[]{:S(2)}) %all-to-all-start.1) | async-done | bytes 589856 | tf_op jit(solution)/shard_map/all_to_all | solution.py:52
  240.9 4.2 %fusion.22 = f32[2,192,384]{2,1,0:T(8,128)} fusion(f32[2,384,192]{1,2,0:T(8,128)S(1)} %bitcast_divide_fusion.2, f32[2,384,2]{1,2,0:T(2,128)S(1)} %collective-permute-done.3, f32[2,384,2]{1,2,0:T(2,128)S(1)} %collective-permute-done.2, f32[]{:T(128)} %bitcast.23, f32[]{:T(128)} %bitcast.22, f32[]{:T(128)} %bitcast.21, f32[]{:T(128)} %bitcast.20, f32[]{:T(128)} %bitcast), kind=kLoop, calls=%fused_computation.47 | loop fusion | flops 1916928 | bytes 1191956 | tf_op jit(solution)/shard_map/transpose | solution.py:67
  245.4 18.9 %gather_fusion = f32[6144,24]{1,0:T(8,128)S(1)} fusion(f32[12288,24]{1,0:T(8,128)} %bitcast.108, s32[6144]{0:T(1024)S(1)} %broadcast_clamp_fusion.3), kind=kCustom, calls=%fused_computation.clone | custom fusion | bytes 1204224 | tf_op jit(solution)/shard_map/jit(_take)/gather | solution.py:51
  268.1 4.6 %all-to-all-start = ((f32[8,768,24]{1,2,0:T(8,128)}), f32[8,768,24]{1,2,0:T(8,128)S(1)}, u32[]{:S(2)}, u32[]{:S(2)}) async-start(f32[8,768,24]{1,2,0:T(8,128)} %broadcast_select_fusion.3), calls=%async_computation | async-start | bytes 1179648 | tf_op jit(solution)/shard_map/all_to_all | solution.py:52
  275.2 13.9 %all-to-all-done = f32[8,768,24]{1,2,0:T(8,128)S(1)} async-done(((f32[8,768,24]{1,2,0:T(8,128)}), f32[8,768,24]{1,2,0:T(8,128)S(1)}, u32[]{:S(2)}, u32[]{:S(2)}) %all-to-all-start) | async-done | bytes 589856 | tf_op jit(solution)/shard_map/all_to_all | solution.py:52
  298.3 4.2 %fusion.31 = f32[2,192,384]{2,1,0:T(8,128)} fusion(f32[2,384,192]{1,2,0:T(8,128)S(1)} %bitcast_divide_fusion.3, f32[2,384,2]{1,2,0:T(2,128)S(1)} %collective-permute-done.1, f32[2,384,2]{1,2,0:T(2,128)S(1)} %collective-permute-done, f32[]{:T(128)} %bitcast.23, f32[]{:T(128)} %bitcast.22, f32[]{:T(128)} %bitcast.21, f32[]{:T(128)} %bitcast.20, f32[]{:T(128)} %bitcast), kind=kLoop, calls=%fused_computation.56 | loop fusion | flops 1916928 | bytes 1191956 | tf_op jit(solution)/shard_map/transpose | solution.py:67
  302.6 11.3 %fusion.44 = f32[2,192,3072]{2,1,0:T(8,128)} fusion(f32[2,3072,384]{2,1,0:T(8,128)} %all-gather.11.cloned.1.call-done, f32[2,192,384]{2,1,0:T(8,128)S(1)} %copy-done.2, f32[2]{0:T(128)S(1)} %get-tuple-element.57), kind=kOutput, calls=%fused_computation.89 | convolution fusion | flops 2718056448 | bytes 14745608 | tf_op jit(solution)/shard_map/rfs,rgs->rfg/dot_general | solution.py:21
  313.9 11.2 %fusion.46 = f32[2,192,3072]{2,1,0:T(8,128)} fusion(f32[2,3072,384]{2,1,0:T(8,128)} %all-gather.9.cloned.1.call-done, f32[2,192,384]{2,1,0:T(8,128)S(1)} %copy-done.3, f32[2]{0:T(128)S(1)} %get-tuple-element.55), kind=kOutput, calls=%fused_computation.91 | convolution fusion | flops 2718056448 | bytes 14745608 | tf_op jit(solution)/shard_map/rfs,rgs->rfg/dot_general | solution.py:21
  325.1 11.6 %fusion.48 = f32[2,192,3072]{2,1,0:T(8,128)} fusion(f32[2,3072,384]{2,1,0:T(8,128)} %all-gather.7.cloned.1.call-done, f32[2,192,384]{2,1,0:T(8,128)S(1)} %copy-done.4, f32[2]{0:T(128)S(1)} %get-tuple-element.56), kind=kOutput, calls=%fused_computation.93 | convolution fusion | flops 2718056448 | bytes 14745608 | tf_op jit(solution)/shard_map/rfs,rgs->rfg/dot_general | solution.py:21
  336.7 33.7 %all-gather.5.cloned.1.call-done = f32[2,3072,384]{2,1,0:T(8,128)} async-done(((f32[2,192,384]{2,1,0:T(8,128)}), f32[2,3072,384]{2,1,0:T(8,128)}) %all-gather.5.cloned.1.call-update) | async-done | bytes 9437200 | tf_op jit(solution)/shard_map/all_gather | solution.py:70
  370.4 8.0 %fusion.50 = f32[2,192,3072]{2,1,0:T(8,128)S(1)} fusion(f32[2,3072,384]{2,1,0:T(8,128)} %all-gather.5.cloned.1.call-done, f32[2,192,384]{2,1,0:T(8,128)S(1)} %copy-done.5, f32[2]{0:T(128)S(1)} %get-tuple-element.54), kind=kOutput, calls=%fused_computation.95 | convolution fusion | flops 2718056448 | bytes 14745608 | tf_op jit(solution)/shard_map/rfs,rgs->rfg/dot_general | solution.py:21
  378.4 8.7 %pad_maximum_fusion = f32[8,192,3072]{2,1,0:T(8,128)} fusion(f32[2,192,3072]{2,1,0:T(8,128)} %fusion.44, f32[2,192,3072]{2,1,0:T(8,128)S(1)} %copy-done, f32[2,192,3072]{2,1,0:T(8,128)S(1)} %copy-done.1, f32[2,192,3072]{2,1,0:T(8,128)S(1)} %fusion.50), kind=kLoop, calls=%fused_computation.4 | loop fusion | flops 14155776 | bytes 37748736 | tf_op jit(solution)/shard_map/concatenate | solution.py:72
  (146 shorter events, 58.5 us)
Async XLA Ops:
  42.8 32.6 %copy-start.7 = (s32[64]{0:T(128)S(1)}, s32[64]{0:T(128)}, u32[]{:S(2)}) copy-start(s32[64]{0:T(128)} %param.8) | copy-start | bytes 772
  61.6 29.5 %copy-start.8 = (f32[5]{0:T(128)S(1)}, f32[5]{0:T(128)}, u32[]{:S(2)}) copy-start(f32[5]{0:T(128)} %param.9) | copy-start | bytes 64
  61.7 54.0 %copy-start.6 = (s32[12288]{0:T(1024)S(1)}, s32[12288]{0:T(1024)}, u32[]{:S(2)}) copy-start(s32[12288]{0:T(1024)} %param.7) | copy-start | bytes 147460
  65.4 18.3 %all-to-all-start.3 = ((f32[8,768,24]{1,2,0:T(8,128)}), f32[8,768,24]{1,2,0:T(8,128)S(1)}, u32[]{:S(2)}, u32[]{:S(2)}) async-start(f32[8,768,24]{1,2,0:T(8,128)} %broadcast_select_fusion), calls=%async_computation.3 | async-start | bytes 1179648 | tf_op jit(solution)/shard_map/all_to_all | solution.py:52
  73.9 228.7 %all-gather.11.cloned.1.call-start = ((), (), s32[]{:S(2)}) async-start(), calls=%async_computation.7 | async-start | bytes 10027008 | tf_op jit(solution)/shard_map/all_gather | solution.py:70
  84.3 7.4 %collective-permute-start.6 = (f32[2,384,2]{1,2,0:T(2,128)S(1)}, f32[2,384,2]{1,2,0:T(2,128)S(1)}, u32[]{:S(2)}, u32[]{:S(2)}) collective-permute-start(f32[2,384,2]{1,2,0:T(2,128)S(1)} %get-tuple-element.18), channel_id=1, source_target_pairs={{0,1},{1,2},{2,3},{3,4},{4,5},{5,6},{6,7},{7,8},{8,9},{9,10},{10,1... | collective-permute-start | bytes 18440 | tf_op jit(solution)/shard_map/ppermute | solution.py:15
  89.2 4.9 %collective-permute-start.7 = (f32[2,384,2]{1,2,0:T(2,128)S(1)}, f32[2,384,2]{1,2,0:T(2,128)S(1)}, u32[]{:S(2)}, u32[]{:S(2)}) collective-permute-start(f32[2,384,2]{1,2,0:T(2,128)S(1)} %get-tuple-element.19), channel_id=1, source_target_pairs={{1,0},{2,1},{3,2},{4,3},{5,4},{6,5},{7,6},{8,7},{9,8},{10,9},{11,1... | collective-permute-start | bytes 18440 | tf_op jit(solution)/shard_map/ppermute | solution.py:16
  138.7 20.3 %all-to-all-start.2 = ((f32[8,768,24]{1,2,0:T(8,128)}), f32[8,768,24]{1,2,0:T(8,128)S(1)}, u32[]{:S(2)}, u32[]{:S(2)}) async-start(f32[8,768,24]{1,2,0:T(8,128)} %broadcast_select_fusion.1), calls=%async_computation.2 | async-start | bytes 1179648 | tf_op jit(solution)/shard_map/all_to_all | solution.py:52
  142.6 171.3 %all-gather.9.cloned.1.call-start = ((), (), s32[]{:S(2)}) async-start(), calls=%async_computation.6 | async-start | bytes 10027008 | tf_op jit(solution)/shard_map/all_gather | solution.py:70
  159.6 4.5 %collective-permute-start.4 = (f32[2,384,2]{1,2,0:T(2,128)S(1)}, f32[2,384,2]{1,2,0:T(2,128)S(1)}, u32[]{:S(2)}, u32[]{:S(2)}) collective-permute-start(f32[2,384,2]{1,2,0:T(2,128)S(1)} %get-tuple-element.14), channel_id=1, source_target_pairs={{0,1},{1,2},{2,3},{3,4},{4,5},{5,6},{6,7},{7,8},{8,9},{9,10},{10,1... | collective-permute-start | bytes 18440 | tf_op jit(solution)/shard_map/ppermute | solution.py:15
  162.1 4.9 %collective-permute-start.5 = (f32[2,384,2]{1,2,0:T(2,128)S(1)}, f32[2,384,2]{1,2,0:T(2,128)S(1)}, u32[]{:S(2)}, u32[]{:S(2)}) collective-permute-start(f32[2,384,2]{1,2,0:T(2,128)S(1)} %get-tuple-element.15), channel_id=1, source_target_pairs={{1,0},{2,1},{3,2},{4,3},{5,4},{6,5},{7,6},{8,7},{9,8},{10,9},{11,1... | collective-permute-start | bytes 18440 | tf_op jit(solution)/shard_map/ppermute | solution.py:16
  211.5 21.0 %all-to-all-start.1 = ((f32[8,768,24]{1,2,0:T(8,128)}), f32[8,768,24]{1,2,0:T(8,128)S(1)}, u32[]{:S(2)}, u32[]{:S(2)}) async-start(f32[8,768,24]{1,2,0:T(8,128)} %broadcast_select_fusion.2), calls=%async_computation.1 | async-start | bytes 1179648 | tf_op jit(solution)/shard_map/all_to_all | solution.py:52
  216.2 109.0 %all-gather.7.cloned.1.call-start = ((), (), s32[]{:S(2)}) async-start(), calls=%async_computation.5 | async-start | bytes 10027008 | tf_op jit(solution)/shard_map/all_gather | solution.py:70
  233.1 4.8 %collective-permute-start.2 = (f32[2,384,2]{1,2,0:T(2,128)S(1)}, f32[2,384,2]{1,2,0:T(2,128)S(1)}, u32[]{:S(2)}, u32[]{:S(2)}) collective-permute-start(f32[2,384,2]{1,2,0:T(2,128)S(1)} %get-tuple-element.10), channel_id=1, source_target_pairs={{0,1},{1,2},{2,3},{3,4},{4,5},{5,6},{6,7},{7,8},{8,9},{9,10},{10,1... | collective-permute-start | bytes 18440 | tf_op jit(solution)/shard_map/ppermute | solution.py:15
  236.0 4.9 %collective-permute-start.3 = (f32[2,384,2]{1,2,0:T(2,128)S(1)}, f32[2,384,2]{1,2,0:T(2,128)S(1)}, u32[]{:S(2)}, u32[]{:S(2)}) collective-permute-start(f32[2,384,2]{1,2,0:T(2,128)S(1)} %get-tuple-element.11), channel_id=1, source_target_pairs={{1,0},{2,1},{3,2},{4,3},{5,4},{6,5},{7,6},{8,7},{9,8},{10,9},{11,1... | collective-permute-start | bytes 18440 | tf_op jit(solution)/shard_map/ppermute | solution.py:16
  266.1 36.5 %copy-start.2 = (f32[2,192,384]{2,1,0:T(8,128)S(1)}, f32[2,192,384]{2,1,0:T(8,128)}, u32[]{:S(2)}) copy-start(f32[2,192,384]{2,1,0:T(8,128)} %fusion.4) | copy-start | bytes 1769476
  268.1 21.0 %all-to-all-start = ((f32[8,768,24]{1,2,0:T(8,128)}), f32[8,768,24]{1,2,0:T(8,128)S(1)}, u32[]{:S(2)}, u32[]{:S(2)}) async-start(f32[8,768,24]{1,2,0:T(8,128)} %broadcast_select_fusion.3), calls=%async_computation | async-start | bytes 1179648 | tf_op jit(solution)/shard_map/all_to_all | solution.py:52
  272.6 97.7 %all-gather.5.cloned.1.call-start = ((), (), s32[]{:S(2)}) async-start(), calls=%async_computation.4 | async-start | bytes 10027008 | tf_op jit(solution)/shard_map/all_gather | solution.py:70
  289.6 5.2 %collective-permute-start = (f32[2,384,2]{1,2,0:T(2,128)S(1)}, f32[2,384,2]{1,2,0:T(2,128)S(1)}, u32[]{:S(2)}, u32[]{:S(2)}) collective-permute-start(f32[2,384,2]{1,2,0:T(2,128)S(1)} %get-tuple-element.6), channel_id=1, source_target_pairs={{0,1},{1,2},{2,3},{3,4},{4,5},{5,6},{6,7},{7,8},{8,9},{9,10},{10,1... | collective-permute-start | bytes 18440 | tf_op jit(solution)/shard_map/ppermute | solution.py:15
  292.7 5.6 %collective-permute-start.1 = (f32[2,384,2]{1,2,0:T(2,128)S(1)}, f32[2,384,2]{1,2,0:T(2,128)S(1)}, u32[]{:S(2)}, u32[]{:S(2)}) collective-permute-start(f32[2,384,2]{1,2,0:T(2,128)S(1)} %get-tuple-element.7), channel_id=1, source_target_pairs={{1,0},{2,1},{3,2},{4,3},{5,4},{6,5},{7,6},{8,7},{9,8},{10,9},{11,1... | collective-permute-start | bytes 18440 | tf_op jit(solution)/shard_map/ppermute | solution.py:16
  302.6 11.3 %copy-start.3 = (f32[2,192,384]{2,1,0:T(8,128)S(1)}, f32[2,192,384]{2,1,0:T(8,128)}, u32[]{:S(2)}) copy-start(f32[2,192,384]{2,1,0:T(8,128)} %fusion.13) | copy-start | bytes 1769476
  313.9 11.2 %copy-start.4 = (f32[2,192,384]{2,1,0:T(8,128)S(1)}, f32[2,192,384]{2,1,0:T(8,128)}, u32[]{:S(2)}) copy-start(f32[2,192,384]{2,1,0:T(8,128)} %fusion.22) | copy-start | bytes 1769476
  325.1 45.2 %copy-start.5 = (f32[2,192,384]{2,1,0:T(8,128)S(1)}, f32[2,192,384]{2,1,0:T(8,128)}, u32[]{:S(2)}) copy-start(f32[2,192,384]{2,1,0:T(8,128)} %fusion.31) | copy-start | bytes 1769476
  370.4 8.0 %copy-start.1 = (f32[2,192,3072]{2,1,0:T(8,128)S(1)}, f32[2,192,3072]{2,1,0:T(8,128)}, u32[]{:S(2)}) copy-start(f32[2,192,3072]{2,1,0:T(8,128)} %fusion.48) | copy-start | bytes 14155780
  (1 other events, 8.0 us)
Sparse Core Ops, SparseCore 0:
  98.5 62.7 all-gather.10
  171.4 65.3 all-gather.8
  245.3 65.8 all-gather.6
  312.7 57.6 all-gather.4

commit v6 on v5

--- a/solution.py
+++ b/solution.py
@@ -33,8 +33,11 @@
     step = owned // PARTS
     window = step * cap
     tblk = groups * sub
-    starts = (jnp.cumsum(cycle_sizes) - cycle_sizes).astype(jnp.int32)
+    starts = (jnp.cumsum(cycle_sizes) - cycle_sizes).astype(jnp.int32).reshape(groups, owned)
+    sends = starts[:, ::step]
     me = lax.axis_index("pix")
+    mine = lax.dynamic_index_in_dim(starts, me, 0, keepdims=False)
+    sizes = lax.dynamic_index_in_dim(cycle_sizes.reshape(groups, owned), me, 0, keepdims=False)
     slots = jnp.arange(cap, dtype=jnp.int32)
 
     order = jnp.pad(pixel_order, (0, window))
@@ -43,19 +46,18 @@
     outs = []
     for part in range(PARTS):
         wanted = jnp.stack(
-            [
-                lax.dynamic_slice_in_dim(order, starts[d * owned + part * step], window, 0)
-                for d in range(groups)
-            ]
+            [lax.dynamic_slice_in_dim(order, sends[d, part], window, 0) for d in range(groups)]
         )
         chunks = jnp.take(series, wanted, axis=0)
         got = lax.all_to_all(chunks, "pix", 0, 0, tiled=True)
         got = jnp.pad(got, ((0, 0), (0, cap), (0, 0)))
-        first = me * owned + part * step
+        first = part * step
+        offsets = mine[first : first + step] - mine[first]
+        masks = slots[None, :] < sizes[first : first + step, None]
         picked = []
         for l in range(step):
-            rows = lax.dynamic_slice_in_dim(got, starts[first + l] - starts[first], cap, 1)
-            picked.append(jnp.where((slots < cycle_sizes[first + l])[None, :, None], rows, 0.0))
+            rows = lax.dynamic_slice_in_dim(got, offsets[l], cap, 1)
+            picked.append(jnp.where(masks[l][None, :, None], rows, 0.0))
         picked = jnp.stack(picked)
         picked = jnp.transpose(picked, (0, 2, 1, 3)).reshape(step, cap, tblk)
 
@@ -66,7 +68,7 @@
             smooth = smooth + kernel[shift_step] * rimmed[..., shift_step : shift_step + tblk]
         smooth = jnp.swapaxes(smooth, 1, 2)
 
-        scale = lax.dynamic_slice_in_dim(cycle_sizes, first, step).astype(jnp.float32)
+        scale = sizes[first : first + step].astype(jnp.float32)
         right = lax.all_gather(smooth, "tm", axis=1, tiled=True)
         outs.append(correlate(smooth * scale[:, None, None], right))
     return jnp.concatenate(outs, 0)

time: 396 us -> 398 us (level)
  between operations: 78.8 us -> 91.3 us
  waiting for transfers between devices: 93.6 us -> 82 us
    all_to_all x4, waiting for transfers between devices: 48 us -> 36.8 us  [per_device(): got = lax.all_to_all(chunks, 'pix', 0, 0, tiled=True)]
    lt x4, other arithmetic: 5.02 us -> 0.29 us  [per_device(): masks = slots[None, :] < sizes[first:first + step, None]]
where the time goes in v6:
time: 398 us; the launch traced here: 396 us
  local copies, waits for them, and re-layouts  97.1 us (24%)
  between operations  91.3 us (23%)
  waiting for transfers between devices  82 us (21%)
  starting transfers between devices  43 us (11%)
  matrix products  42.1 us (11%)
  other arithmetic  40.2 us (10%)
    gather x8, local copies, waits for them, and re-layouts, per_device(): chunks = jnp.take(series, wanted, axis=0)  83 us
    dot_general x4, matrix products, correlate(): jnp.einsum('rfs,rgs->rfg', left, right, precision=lax.Precision.HIGH, pre...  42.1 us
    all_to_all x4, waiting for transfers between devices, per_device(): got = lax.all_to_all(chunks, 'pix', 0, 0, tiled=True)  36.8 us
    all_gather x4, waiting for transfers between devices, per_device(): right = lax.all_gather(smooth, 'tm', axis=1, tiled=True)  33.3 us
    all_to_all x4, starting transfers between devices, per_device(): got = lax.all_to_all(chunks, 'pix', 0, 0, tiled=True)  21.6 us
    transpose x4, other arithmetic, per_device(): smooth = jnp.swapaxes(smooth, 1, 2)  17.7 us
    ppermute x4, starting transfers between devices, halo_frames(): low = lax.ppermute(block[..., n - width:], 'tm', forward)  13.4 us
    ppermute x4, waiting for transfers between devices, halo_frames(): high = lax.ppermute(block[..., :width], 'tm', backward)  11.8 us
  transfers between devices with their start and end apart: 16, of which 9 were waited for; matrix products, arithmetic and copies ran while one was open for 32% of the time, Pallas kernels for 0%

profile of v6, /device:TPU:1, one launch (start us, length us, event | category | flops | bytes accessed | tf_op | source)
XLA Modules:
  0.0 395.8 jit_solution(2266987076901544714)
XLA Ops:
  37.8 4.9 %copy.12 = f32[1,24,12288]{1,2,0:T(8,128)} copy(f32[1,24,12288]{2,1,0:T(8,128)} %param.6) | data formatting | bytes 2359296 | tf_op args[0]
  42.6 18.9 %gather_fusion.3 = f32[6144,24]{1,0:T(8,128)S(1)} fusion(f32[12288,24]{1,0:T(8,128)} %bitcast.121, s32[6144]{0:T(1024)S(1)} %broadcast_clamp_fusion), kind=kCustom, calls=%fused_computation.3.clone | custom fusion | bytes 1204224 | tf_op jit(solution)/shard_map/jit(_take)/gather | solution.py:51
  65.3 8.5 %all-to-all-start.3 = ((f32[8,768,24]{1,2,0:T(8,128)}), f32[8,768,24]{1,2,0:T(8,128)S(1)}, u32[]{:S(2)}, u32[]{:S(2)}) async-start(f32[8,768,24]{1,2,0:T(8,128)} %broadcast_select_fusion), calls=%async_computation.3 | async-start | bytes 1179648 | tf_op jit(solution)/shard_map/all_to_all | solution.py:52
  84.3 4.8 %collective-permute-start.6 = (f32[2,384,2]{1,2,0:T(2,128)S(1)}, f32[2,384,2]{1,2,0:T(2,128)S(1)}, u32[]{:S(2)}, u32[]{:S(2)}) collective-permute-start(f32[2,384,2]{1,2,0:T(2,128)S(1)} %get-tuple-element.26), channel_id=1, source_target_pairs={{0,1},{1,2},{2,3},{3,4},{4,5},{5,6},{6,7},{7,8},{8,9},{9,10},{10,1... | collective-permute-start | bytes 18440 | tf_op jit(solution)/shard_map/ppermute | solution.py:15
  94.1 4.4 %fusion.4 = f32[2,192,384]{2,1,0:T(8,128)} fusion(f32[2,384,192]{1,2,0:T(8,128)S(1)} %bitcast_divide_fusion, f32[2,384,2]{1,2,0:T(2,128)S(1)} %collective-permute-done.7, f32[2,384,2]{1,2,0:T(2,128)S(1)} %collective-permute-done.6, f32[]{:T(128)} %bitcast.24, f32[]{:T(128)} %bitcast.23, f32[]{:T(128)} %bitcast.22, f32[]{:T(128)} %bitcast.21, f32[]{:T(128)} %bitcast), kind=kLoop, calls=%fused_computation.33 | loop fusion | flops 1916928 | bytes 1191956 | tf_op jit(solution)/shard_map/transpose | solution.py:69
  116.6 19.0 %gather_fusion.2 = f32[6144,24]{1,0:T(8,128)S(1)} fusion(f32[12288,24]{1,0:T(8,128)} %bitcast.122, s32[6144]{0:T(1024)S(1)} %broadcast_clamp_fusion.1), kind=kCustom, calls=%fused_computation.2.clone | custom fusion | bytes 1204224 | tf_op jit(solution)/shard_map/jit(_take)/gather | solution.py:51
  139.5 3.9 all-to-all-start.2
  148.0 11.8 %all-to-all-done.2 = f32[8,768,24]{1,2,0:T(8,128)S(1)} async-done(((f32[8,768,24]{1,2,0:T(8,128)}), f32[8,768,24]{1,2,0:T(8,128)S(1)}, u32[]{:S(2)}, u32[]{:S(2)}) %all-to-all-start.2) | async-done | bytes 589856 | tf_op jit(solution)/shard_map/all_to_all | solution.py:52
  168.1 4.4 %fusion.13 = f32[2,192,384]{2,1,0:T(8,128)} fusion(f32[2,384,192]{1,2,0:T(8,128)S(1)} %bitcast_divide_fusion.1, f32[2,384,2]{1,2,0:T(2,128)S(1)} %collective-permute-done.5, f32[2,384,2]{1,2,0:T(2,128)S(1)} %collective-permute-done.4, f32[]{:T(128)} %bitcast.24, f32[]{:T(128)} %bitcast.23, f32[]{:T(128)} %bitcast.22, f32[]{:T(128)} %bitcast.21, f32[]{:T(128)} %bitcast), kind=kLoop, calls=%fused_computation.42 | loop fusion | flops 1916928 | bytes 1191956 | tf_op jit(solution)/shard_map/transpose | solution.py:69
  190.7 19.0 %gather_fusion.1 = f32[6144,24]{1,0:T(8,128)S(1)} fusion(f32[12288,24]{1,0:T(8,128)} %bitcast.123, s32[6144]{0:T(1024)S(1)} %broadcast_clamp_fusion.2), kind=kCustom, calls=%fused_computation.1.clone | custom fusion | bytes 1204224 | tf_op jit(solution)/shard_map/jit(_take)/gather | solution.py:51
  213.5 4.6 %all-to-all-start.1 = ((f32[8,768,24]{1,2,0:T(8,128)}), f32[8,768,24]{1,2,0:T(8,128)S(1)}, u32[]{:S(2)}, u32[]{:S(2)}) async-start(f32[8,768,24]{1,2,0:T(8,128)} %broadcast_select_fusion.2), calls=%async_computation.1 | async-start | bytes 1179648 | tf_op jit(solution)/shard_map/all_to_all | solution.py:52
  222.8 11.7 %all-to-all-done.1 = f32[8,768,24]{1,2,0:T(8,128)S(1)} async-done(((f32[8,768,24]{1,2,0:T(8,128)}), f32[8,768,24]{1,2,0:T(8,128)S(1)}, u32[]{:S(2)}, u32[]{:S(2)}) %all-to-all-start.1) | async-done | bytes 589856 | tf_op jit(solution)/shard_map/all_to_all | solution.py:52
  243.0 4.5 %fusion.22 = f32[2,192,384]{2,1,0:T(8,128)} fusion(f32[2,384,192]{1,2,0:T(8,128)S(1)} %bitcast_divide_fusion.2, f32[2,384,2]{1,2,0:T(2,128)S(1)} %collective-permute-done.3, f32[2,384,2]{1,2,0:T(2,128)S(1)} %collective-permute-done.2, f32[]{:T(128)} %bitcast.24, f32[]{:T(128)} %bitcast.23, f32[]{:T(128)} %bitcast.22, f32[]{:T(128)} %bitcast.21, f32[]{:T(128)} %bitcast), kind=kLoop, calls=%fused_computation.51 | loop fusion | flops 1916928 | bytes 1191956 | tf_op jit(solution)/shard_map/transpose | solution.py:69
  247.6 18.9 %gather_fusion = f32[6144,24]{1,0:T(8,128)S(1)} fusion(f32[12288,24]{1,0:T(8,128)} %bitcast.124, s32[6144]{0:T(1024)S(1)} %broadcast_clamp_fusion.3), kind=kCustom, calls=%fused_computation.clone | custom fusion | bytes 1204224 | tf_op jit(solution)/shard_map/jit(_take)/gather | solution.py:51
  270.3 4.6 %all-to-all-start = ((f32[8,768,24]{1,2,0:T(8,128)}), f32[8,768,24]{1,2,0:T(8,128)S(1)}, u32[]{:S(2)}, u32[]{:S(2)}) async-start(f32[8,768,24]{1,2,0:T(8,128)} %broadcast_select_fusion.3), calls=%async_computation | async-start | bytes 1179648 | tf_op jit(solution)/shard_map/all_to_all | solution.py:52
  279.8 11.5 %all-to-all-done = f32[8,768,24]{1,2,0:T(8,128)S(1)} async-done(((f32[8,768,24]{1,2,0:T(8,128)}), f32[8,768,24]{1,2,0:T(8,128)S(1)}, u32[]{:S(2)}, u32[]{:S(2)}) %all-to-all-start) | async-done | bytes 589856 | tf_op jit(solution)/shard_map/all_to_all | solution.py:52
  297.1 3.5 collective-permute-done.1
  300.6 4.4 %fusion.31 = f32[2,192,384]{2,1,0:T(8,128)} fusion(f32[2,384,192]{1,2,0:T(8,128)S(1)} %bitcast_divide_fusion.3, f32[2,384,2]{1,2,0:T(2,128)S(1)} %collective-permute-done.1, f32[2,384,2]{1,2,0:T(2,128)S(1)} %collective-permute-done, f32[]{:T(128)} %bitcast.24, f32[]{:T(128)} %bitcast.23, f32[]{:T(128)} %bitcast.22, f32[]{:T(128)} %bitcast.21, f32[]{:T(128)} %bitcast), kind=kLoop, calls=%fused_computation.60 | loop fusion | flops 1916928 | bytes 1191956 | tf_op jit(solution)/shard_map/transpose | solution.py:69
  305.1 11.3 %fusion.44 = f32[2,192,3072]{2,1,0:T(8,128)} fusion(f32[2,3072,384]{2,1,0:T(8,128)} %all-gather.11.cloned.1.call-done, f32[2,192,384]{2,1,0:T(8,128)S(1)} %copy-done.2, f32[2]{0:T(128)S(1)} %get-tuple-element.95), kind=kOutput, calls=%fused_computation.93 | convolution fusion | flops 2718056448 | bytes 14745608 | tf_op jit(solution)/shard_map/rfs,rgs->rfg/dot_general | solution.py:21
  316.4 11.2 %fusion.46 = f32[2,192,3072]{2,1,0:T(8,128)} fusion(f32[2,3072,384]{2,1,0:T(8,128)} %all-gather.9.cloned.1.call-done, f32[2,192,384]{2,1,0:T(8,128)S(1)} %copy-done.3, f32[2]{0:T(128)S(1)} %get-tuple-element.96), kind=kOutput, calls=%fused_computation.95 | convolution fusion | flops 2718056448 | bytes 14745608 | tf_op jit(solution)/shard_map/rfs,rgs->rfg/dot_general | solution.py:21
  327.6 11.6 %fusion.48 = f32[2,192,3072]{2,1,0:T(8,128)} fusion(f32[2,3072,384]{2,1,0:T(8,128)} %all-gather.7.cloned.1.call-done, f32[2,192,384]{2,1,0:T(8,128)S(1)} %copy-done.4, f32[2]{0:T(128)S(1)} %get-tuple-element.97), kind=kOutput, calls=%fused_computation.97 | convolution fusion | flops 2718056448 | bytes 14745608 | tf_op jit(solution)/shard_map/rfs,rgs->rfg/dot_general | solution.py:21
  339.2 33.3 %all-gather.5.cloned.1.call-done = f32[2,3072,384]{2,1,0:T(8,128)} async-done(((f32[2,192,384]{2,1,0:T(8,128)}), f32[2,3072,384]{2,1,0:T(8,128)}) %all-gather.5.cloned.1.call-update) | async-done | bytes 9437200 | tf_op jit(solution)/shard_map/all_gather | solution.py:72
  372.5 8.0 %fusion.50 = f32[2,192,3072]{2,1,0:T(8,128)S(1)} fusion(f32[2,3072,384]{2,1,0:T(8,128)} %all-gather.5.cloned.1.call-done, f32[2,192,384]{2,1,0:T(8,128)S(1)} %copy-done.5, f32[2]{0:T(128)S(1)} %get-tuple-element.94), kind=kOutput, calls=%fused_computation.99 | convolution fusion | flops 2718056448 | bytes 14745608 | tf_op jit(solution)/shard_map/rfs,rgs->rfg/dot_general | solution.py:21
  380.5 8.7 %pad_maximum_fusion = f32[8,192,3072]{2,1,0:T(8,128)} fusion(f32[2,192,3072]{2,1,0:T(8,128)} %fusion.44, f32[2,192,3072]{2,1,0:T(8,128)S(1)} %copy-done, f32[2,192,3072]{2,1,0:T(8,128)S(1)} %copy-done.1, f32[2,192,3072]{2,1,0:T(8,128)S(1)} %fusion.50), kind=kLoop, calls=%fused_computation.4 | loop fusion | flops 14155776 | bytes 37748736 | tf_op jit(solution)/shard_map/concatenate | solution.py:74
  (158 shorter events, 57.2 us)
Async XLA Ops:
  42.6 31.2 %copy-start.8 = (s32[64]{0:T(128)S(1)}, s32[64]{0:T(128)}, u32[]{:S(2)}) copy-start(s32[64]{0:T(128)} %param.8) | copy-start | bytes 772
  61.5 29.5 %copy-start.7 = (f32[5]{0:T(128)S(1)}, f32[5]{0:T(128)}, u32[]{:S(2)}) copy-start(f32[5]{0:T(128)} %param.9) | copy-start | bytes 64
  61.5 54.9 %copy-start.6 = (s32[12288]{0:T(1024)S(1)}, s32[12288]{0:T(1024)}, u32[]{:S(2)}) copy-start(s32[12288]{0:T(1024)} %param.7) | copy-start | bytes 147460
  65.3 18.3 %all-to-all-start.3 = ((f32[8,768,24]{1,2,0:T(8,128)}), f32[8,768,24]{1,2,0:T(8,128)S(1)}, u32[]{:S(2)}, u32[]{:S(2)}) async-start(f32[8,768,24]{1,2,0:T(8,128)} %broadcast_select_fusion), calls=%async_computation.3 | async-start | bytes 1179648 | tf_op jit(solution)/shard_map/all_to_all | solution.py:52
  73.8 231.3 %all-gather.11.cloned.1.call-start = ((), (), s32[]{:S(2)}) async-start(), calls=%async_computation.7 | async-start | bytes 10027008 | tf_op jit(solution)/shard_map/all_gather | solution.py:72
  84.3 7.5 %collective-permute-start.6 = (f32[2,384,2]{1,2,0:T(2,128)S(1)}, f32[2,384,2]{1,2,0:T(2,128)S(1)}, u32[]{:S(2)}, u32[]{:S(2)}) collective-permute-start(f32[2,384,2]{1,2,0:T(2,128)S(1)} %get-tuple-element.26), channel_id=1, source_target_pairs={{0,1},{1,2},{2,3},{3,4},{4,5},{5,6},{6,7},{7,8},{8,9},{9,10},{10,1... | collective-permute-start | bytes 18440 | tf_op jit(solution)/shard_map/ppermute | solution.py:15
  89.1 4.9 %collective-permute-start.7 = (f32[2,384,2]{1,2,0:T(2,128)S(1)}, f32[2,384,2]{1,2,0:T(2,128)S(1)}, u32[]{:S(2)}, u32[]{:S(2)}) collective-permute-start(f32[2,384,2]{1,2,0:T(2,128)S(1)} %get-tuple-element.27), channel_id=1, source_target_pairs={{1,0},{2,1},{3,2},{4,3},{5,4},{6,5},{7,6},{8,7},{9,8},{10,9},{11,1... | collective-permute-start | bytes 18440 | tf_op jit(solution)/shard_map/ppermute | solution.py:16
  139.5 20.4 %all-to-all-start.2 = ((f32[8,768,24]{1,2,0:T(8,128)}), f32[8,768,24]{1,2,0:T(8,128)S(1)}, u32[]{:S(2)}, u32[]{:S(2)}) async-start(f32[8,768,24]{1,2,0:T(8,128)} %broadcast_select_fusion.1), calls=%async_computation.2 | async-start | bytes 1179648 | tf_op jit(solution)/shard_map/all_to_all | solution.py:52
  143.4 173.0 %all-gather.9.cloned.1.call-start = ((), (), s32[]{:S(2)}) async-start(), calls=%async_computation.6 | async-start | bytes 10027008 | tf_op jit(solution)/shard_map/all_gather | solution.py:72
  160.5 4.6 %collective-permute-start.4 = (f32[2,384,2]{1,2,0:T(2,128)S(1)}, f32[2,384,2]{1,2,0:T(2,128)S(1)}, u32[]{:S(2)}, u32[]{:S(2)}) collective-permute-start(f32[2,384,2]{1,2,0:T(2,128)S(1)} %get-tuple-element.22), channel_id=1, source_target_pairs={{0,1},{1,2},{2,3},{3,4},{4,5},{5,6},{6,7},{7,8},{8,9},{9,10},{10,1... | collective-permute-start | bytes 18440 | tf_op jit(solution)/shard_map/ppermute | solution.py:15
  163.1 4.9 %collective-permute-start.5 = (f32[2,384,2]{1,2,0:T(2,128)S(1)}, f32[2,384,2]{1,2,0:T(2,128)S(1)}, u32[]{:S(2)}, u32[]{:S(2)}) collective-permute-start(f32[2,384,2]{1,2,0:T(2,128)S(1)} %get-tuple-element.23), channel_id=1, source_target_pairs={{1,0},{2,1},{3,2},{4,3},{5,4},{6,5},{7,6},{8,7},{9,8},{10,9},{11,1... | collective-permute-start | bytes 18440 | tf_op jit(solution)/shard_map/ppermute | solution.py:16
  213.5 21.0 %all-to-all-start.1 = ((f32[8,768,24]{1,2,0:T(8,128)}), f32[8,768,24]{1,2,0:T(8,128)S(1)}, u32[]{:S(2)}, u32[]{:S(2)}) async-start(f32[8,768,24]{1,2,0:T(8,128)} %broadcast_select_fusion.2), calls=%async_computation.1 | async-start | bytes 1179648 | tf_op jit(solution)/shard_map/all_to_all | solution.py:52
  218.1 109.5 %all-gather.7.cloned.1.call-start = ((), (), s32[]{:S(2)}) async-start(), calls=%async_computation.5 | async-start | bytes 10027008 | tf_op jit(solution)/shard_map/all_gather | solution.py:72
  235.1 4.8 %collective-permute-start.2 = (f32[2,384,2]{1,2,0:T(2,128)S(1)}, f32[2,384,2]{1,2,0:T(2,128)S(1)}, u32[]{:S(2)}, u32[]{:S(2)}) collective-permute-start(f32[2,384,2]{1,2,0:T(2,128)S(1)} %get-tuple-element.18), channel_id=1, source_target_pairs={{0,1},{1,2},{2,3},{3,4},{4,5},{5,6},{6,7},{7,8},{8,9},{9,10},{10,1... | collective-permute-start | bytes 18440 | tf_op jit(solution)/shard_map/ppermute | solution.py:15
  238.0 4.9 %collective-permute-start.3 = (f32[2,384,2]{1,2,0:T(2,128)S(1)}, f32[2,384,2]{1,2,0:T(2,128)S(1)}, u32[]{:S(2)}, u32[]{:S(2)}) collective-permute-start(f32[2,384,2]{1,2,0:T(2,128)S(1)} %get-tuple-element.19), channel_id=1, source_target_pairs={{1,0},{2,1},{3,2},{4,3},{5,4},{6,5},{7,6},{8,7},{9,8},{10,9},{11,1... | collective-permute-start | bytes 18440 | tf_op jit(solution)/shard_map/ppermute | solution.py:16
  268.3 36.8 %copy-start.2 = (f32[2,192,384]{2,1,0:T(8,128)S(1)}, f32[2,192,384]{2,1,0:T(8,128)}, u32[]{:S(2)}) copy-start(f32[2,192,384]{2,1,0:T(8,128)} %fusion.4) | copy-start | bytes 1769476
  270.3 21.0 %all-to-all-start = ((f32[8,768,24]{1,2,0:T(8,128)}), f32[8,768,24]{1,2,0:T(8,128)S(1)}, u32[]{:S(2)}, u32[]{:S(2)}) async-start(f32[8,768,24]{1,2,0:T(8,128)} %broadcast_select_fusion.3), calls=%async_computation | async-start | bytes 1179648 | tf_op jit(solution)/shard_map/all_to_all | solution.py:52
  274.9 97.6 %all-gather.5.cloned.1.call-start = ((), (), s32[]{:S(2)}) async-start(), calls=%async_computation.4 | async-start | bytes 10027008 | tf_op jit(solution)/shard_map/all_gather | solution.py:72
  292.0 5.2 %collective-permute-start = (f32[2,384,2]{1,2,0:T(2,128)S(1)}, f32[2,384,2]{1,2,0:T(2,128)S(1)}, u32[]{:S(2)}, u32[]{:S(2)}) collective-permute-start(f32[2,384,2]{1,2,0:T(2,128)S(1)} %get-tuple-element.14), channel_id=1, source_target_pairs={{0,1},{1,2},{2,3},{3,4},{4,5},{5,6},{6,7},{7,8},{8,9},{9,10},{10,1... | collective-permute-start | bytes 18440 | tf_op jit(solution)/shard_map/ppermute | solution.py:15
  295.0 5.6 %collective-permute-start.1 = (f32[2,384,2]{1,2,0:T(2,128)S(1)}, f32[2,384,2]{1,2,0:T(2,128)S(1)}, u32[]{:S(2)}, u32[]{:S(2)}) collective-permute-start(f32[2,384,2]{1,2,0:T(2,128)S(1)} %get-tuple-element.15), channel_id=1, source_target_pairs={{1,0},{2,1},{3,2},{4,3},{5,4},{6,5},{7,6},{8,7},{9,8},{10,9},{11,1... | collective-permute-start | bytes 18440 | tf_op jit(solution)/shard_map/ppermute | solution.py:16
  305.1 11.3 %copy-start.3 = (f32[2,192,384]{2,1,0:T(8,128)S(1)}, f32[2,192,384]{2,1,0:T(8,128)}, u32[]{:S(2)}) copy-start(f32[2,192,384]{2,1,0:T(8,128)} %fusion.13) | copy-start | bytes 1769476
  316.4 11.2 %copy-start.4 = (f32[2,192,384]{2,1,0:T(8,128)S(1)}, f32[2,192,384]{2,1,0:T(8,128)}, u32[]{:S(2)}) copy-start(f32[2,192,384]{2,1,0:T(8,128)} %fusion.22) | copy-start | bytes 1769476
  327.6 44.9 %copy-start.5 = (f32[2,192,384]{2,1,0:T(8,128)S(1)}, f32[2,192,384]{2,1,0:T(8,128)}, u32[]{:S(2)}) copy-start(f32[2,192,384]{2,1,0:T(8,128)} %fusion.31) | copy-start | bytes 1769476
  372.5 8.0 %copy-start.1 = (f32[2,192,3072]{2,1,0:T(8,128)S(1)}, f32[2,192,3072]{2,1,0:T(8,128)}, u32[]{:S(2)}) copy-start(f32[2,192,3072]{2,1,0:T(8,128)} %fusion.48) | copy-start | bytes 14155780
  (1 other events, 8.0 us)
Sparse Core Ops, SparseCore 0:
  98.6 62.8 all-gather.10
  172.7 65.2 all-gather.8
  247.6 65.7 all-gather.6
  314.8 57.6 all-gather.4

commit v7 on v6

--- a/solution.py
+++ b/solution.py
@@ -40,26 +40,31 @@
     sizes = lax.dynamic_index_in_dim(cycle_sizes.reshape(groups, owned), me, 0, keepdims=False)
     slots = jnp.arange(cap, dtype=jnp.int32)
 
-    order = jnp.pad(pixel_order, (0, window))
+    lanes = 128
+    span = window + lanes
+    order = jnp.pad(pixel_order, (0, span)).reshape(-1, lanes)
+    aligned = (sends // lanes) * lanes
     series = block.T
+    reach = jnp.arange(span, dtype=jnp.int32)
 
     outs = []
     for part in range(PARTS):
-        wanted = jnp.stack(
-            [lax.dynamic_slice_in_dim(order, sends[d, part], window, 0) for d in range(groups)]
-        )
-        chunks = jnp.take(series, wanted, axis=0)
+        rows = (aligned[:, part] // lanes)[:, None] + jnp.arange(span // lanes, dtype=jnp.int32)
+        wanted = jnp.take(order, rows, axis=0).reshape(groups * span)
+        chunks = jnp.take(series, wanted, axis=0).reshape(groups, span, sub)
         got = lax.all_to_all(chunks, "pix", 0, 0, tiled=True)
-        got = jnp.pad(got, ((0, 0), (0, cap), (0, 0)))
+
         first = part * step
-        offsets = mine[first : first + step] - mine[first]
-        masks = slots[None, :] < sizes[first : first + step, None]
-        picked = []
-        for l in range(step):
-            rows = lax.dynamic_slice_in_dim(got, offsets[l], cap, 1)
-            picked.append(jnp.where(masks[l][None, :, None], rows, 0.0))
-        picked = jnp.stack(picked)
-        picked = jnp.transpose(picked, (0, 2, 1, 3)).reshape(step, cap, tblk)
+        offsets = mine[first : first + step] - (mine[first] // lanes) * lanes
+        hit = reach[None, None, :] == offsets[:, None, None] + slots[None, :, None]
+        hit = hit & (slots[None, :, None] < sizes[first : first + step, None, None])
+        picked = jnp.einsum(
+            "lcj,sjf->lcsf",
+            hit.astype(jnp.float32),
+            got,
+            precision=lax.Precision.HIGHEST,
+            preferred_element_type=jnp.float32,
+        ).reshape(step, cap, tblk)
 
         total = jnp.sum(picked, axis=1, keepdims=True)
         rimmed = halo_frames(picked / total, REACH)

time: 398 us -> 403 us (1.013)
  between operations: 91.3 us -> 23.8 us
  local copies, waits for them, and re-layouts: 97.1 us -> 133 us
  other arithmetic: 40.2 us -> 57.7 us
  waiting for transfers between devices: 82 us -> 91.2 us
  matrix products: 42.1 us -> 49.7 us
    gather x8 -> x12, local copies, waits for them, and re-layouts: 83 us -> 111 us  [the longest x4 108 us: per_device(): chunks = jnp.take(series, wanted, axis=0).reshape(groups, span, sub)]
    select_n x8 -> x11, other arithmetic: 7.91 us -> 28.7 us  [the longest x4 28 us: per_device(): chunks = jnp.take(series, wanted, axis=0).reshape(groups, span, sub)]
    all_to_all x4, waiting for transfers between devices: 36.8 us -> 54.8 us  [per_device(): got = lax.all_to_all(chunks, 'pix', 0, 0, tiled=True)]
    reshape x0 -> x9, local copies, waits for them, and re-layouts: none -> 14.3 us  [the longest x4 13.5 us: per_device(): chunks = jnp.take(series, wanted, axis=0).reshape(groups, span, sub)]
    all_gather x4, waiting for transfers between devices: 33.3 us -> 25 us  [per_device(): right = lax.all_gather(smooth, 'tm', axis=1, tiled=True)]
    dot_general x0 -> x4, matrix products: none -> 7.85 us  [per_device(): jnp.einsum('lcj,sjf->lcsf', hit.astype(jnp.float32), got, precision=lax.P...]
    slice x11 -> x1, local copies, waits for them, and re-layouts: 4.75 us -> 0.67 us  [per_device(): offsets = mine[first:first + step] - mine[first] // lanes * lanes]
  transfers between devices with their start and end apart: 16 -> 16, of which waited for: 9 -> 8; matrix products, arithmetic and copies ran while one was open for 32% -> 43% of each run, Pallas kernels for 0% -> 0%
where the time goes in v7:
time: 403 us; the launch traced here: 401 us
  local copies, waits for them, and re-layouts  133 us (33%)
  waiting for transfers between devices  91.2 us (23%)
  other arithmetic  57.7 us (14%)
  matrix products  49.7 us (12%)
  starting transfers between devices  45.4 us (11%)
  between operations  23.8 us (6%)
    gather x4, local copies, waits for them, and re-layouts, per_device(): chunks = jnp.take(series, wanted, axis=0).reshape(groups, span, sub)  108 us
    all_to_all x4, waiting for transfers between devices, per_device(): got = lax.all_to_all(chunks, 'pix', 0, 0, tiled=True)  54.8 us
    dot_general x4, matrix products, correlate(): jnp.einsum('rfs,rgs->rfg', left, right, precision=lax.Precision.HIGH, pre...  41.8 us
    select_n x4, other arithmetic, per_device(): chunks = jnp.take(series, wanted, axis=0).reshape(groups, span, sub)  28 us
    all_gather x4, waiting for transfers between devices, per_device(): right = lax.all_gather(smooth, 'tm', axis=1, tiled=True)  25 us
    all_to_all x4, starting transfers between devices, per_device(): got = lax.all_to_all(chunks, 'pix', 0, 0, tiled=True)  24.1 us
    transpose x4, other arithmetic, per_device(): smooth = jnp.swapaxes(smooth, 1, 2)  17.6 us
    reshape x4, local copies, waits for them, and re-layouts, per_device(): chunks = jnp.take(series, wanted, axis=0).reshape(groups, span, sub)  13.5 us
  transfers between devices with their start and end apart: 16, of which 8 were waited for; matrix products, arithmetic and copies ran while one was open for 43% of the time, Pallas kernels for 0%

profile of v7, /device:TPU:1, one launch (start us, length us, event | category | flops | bytes accessed | tf_op | source)
XLA Modules:
  0.0 400.9 jit_solution(15091290072951538104)
XLA Ops:
  10.3 4.9 %copy.8 = f32[1,24,12288]{1,2,0:T(8,128)} copy(f32[1,24,12288]{2,1,0:T(8,128)} %param.8) | data formatting | bytes 2359296 | tf_op args[0]
  15.2 27.1 %gather_fusion.7 = f32[7168,24]{1,0:T(8,128)} fusion(f32[12288,24]{1,0:T(8,128)} %bitcast.111, s32[7168]{0:T(1024)S(1)} %fusion.87), kind=kCustom, calls=%fused_computation.7.clone | custom fusion | bytes 1404928 | tf_op jit(solution)/shard_map/jit(_take)/gather | solution.py:54
  42.3 7.0 %broadcast_select_fusion = f32[7168,24]{1,0:T(8,128)} fusion(f32[7168,24]{1,0:T(8,128)} %gather_fusion.7, pred[7168]{0:T(1024)(128)(4,1)S(1)} %compare_and_fusion), kind=kLoop, calls=%fused_computation.25 | loop fusion | flops 172032 | bytes 1383424 | tf_op jit(solution)/shard_map/jit(_take)/select_n | solution.py:54
  52.6 8.5 %all-to-all-start.3 = ((f32[8,896,24]{1,2,0:T(8,128)}), f32[8,896,24]{1,2,0:T(8,128)S(1)}, u32[]{:S(2)}, u32[]{:S(2)}) async-start(f32[8,896,24]{1,2,0:T(8,128)} %copy.16), calls=%async_computation.3 | async-start | bytes 1376256 | tf_op jit(solution)/shard_map/all_to_all | solution.py:55
  89.0 27.1 %gather_fusion.5 = f32[7168,24]{1,0:T(8,128)} fusion(f32[12288,24]{1,0:T(8,128)} %bitcast.112, s32[7168]{0:T(1024)S(1)} %fusion.86), kind=kCustom, calls=%fused_computation.6.clone | custom fusion | bytes 1404928 | tf_op jit(solution)/shard_map/jit(_take)/gather | solution.py:54
  116.1 7.0 %broadcast_select_fusion.1 = f32[7168,24]{1,0:T(8,128)} fusion(f32[7168,24]{1,0:T(8,128)} %gather_fusion.5, pred[7168]{0:T(1024)(128)(4,1)S(1)} %compare_and_fusion.1), kind=kLoop, calls=%fused_computation.26 | loop fusion | flops 172032 | bytes 1383424 | tf_op jit(solution)/shard_map/jit(_take)/select_n | solution.py:54
  126.5 6.4 %all-to-all-start.2 = ((f32[8,896,24]{1,2,0:T(8,128)}), f32[8,896,24]{1,2,0:T(8,128)S(1)}, u32[]{:S(2)}, u32[]{:S(2)}) async-start(f32[8,896,24]{1,2,0:T(8,128)} %copy.14), calls=%async_computation.2 | async-start | bytes 1376256 | tf_op jit(solution)/shard_map/all_to_all | solution.py:55
  133.2 18.3 %all-to-all-done.2 = f32[8,896,24]{1,2,0:T(8,128)S(1)} async-done(((f32[8,896,24]{1,2,0:T(8,128)}), f32[8,896,24]{1,2,0:T(8,128)S(1)}, u32[]{:S(2)}, u32[]{:S(2)}) %all-to-all-start.2) | async-done | bytes 688160 | tf_op jit(solution)/shard_map/all_to_all | solution.py:55
  161.5 4.4 %fusion.41 = f32[2,192,384]{2,1,0:T(8,128)} fusion(f32[2,384,192]{1,2,0:T(8,128)S(1)} %bitcast_divide_fusion.1, f32[2,384,2]{1,2,0:T(2,128)S(1)} %collective-permute-done.5, f32[2,384,2]{1,2,0:T(2,128)S(1)} %collective-permute-done.4, f32[]{:T(128)} %bitcast.16, f32[]{:T(128)} %bitcast.15, f32[]{:T(128)} %bitcast.14, f32[]{:T(128)} %bitcast.13, f32[]{:T(128)} %bitcast), kind=kLoop, calls=%fused_computation.70 | loop fusion | flops 1916928 | bytes 1191956 | tf_op jit(solution)/shard_map/transpose | solution.py:74
  166.9 27.1 %gather_fusion.1 = f32[7168,24]{1,0:T(8,128)} fusion(f32[12288,24]{1,0:T(8,128)} %bitcast.113, s32[7168]{0:T(1024)S(1)} %fusion.84), kind=kCustom, calls=%fused_computation.1.clone | custom fusion | bytes 1404928 | tf_op jit(solution)/shard_map/jit(_take)/gather | solution.py:54
  194.0 7.0 %broadcast_select_fusion.3 = f32[7168,24]{1,0:T(8,128)} fusion(f32[7168,24]{1,0:T(8,128)} %gather_fusion.1, pred[7168]{0:T(1024)(128)(4,1)S(1)} %compare_and_fusion.3), kind=kLoop, calls=%fused_computation.28 | loop fusion | flops 172032 | bytes 1383424 | tf_op jit(solution)/shard_map/jit(_take)/select_n | solution.py:54
  204.4 4.6 %all-to-all-start = ((f32[8,896,24]{1,2,0:T(8,128)}), f32[8,896,24]{1,2,0:T(8,128)S(1)}, u32[]{:S(2)}, u32[]{:S(2)}) async-start(f32[8,896,24]{1,2,0:T(8,128)} %copy.10), calls=%async_computation | async-start | bytes 1376256 | tf_op jit(solution)/shard_map/all_to_all | solution.py:55
  209.4 18.1 %all-to-all-done = f32[8,896,24]{1,2,0:T(8,128)S(1)} async-done(((f32[8,896,24]{1,2,0:T(8,128)}), f32[8,896,24]{1,2,0:T(8,128)S(1)}, u32[]{:S(2)}, u32[]{:S(2)}) %all-to-all-start) | async-done | bytes 688160 | tf_op jit(solution)/shard_map/all_to_all | solution.py:55
  237.8 4.4 %fusion.59 = f32[2,192,384]{2,1,0:T(8,128)} fusion(f32[2,384,192]{1,2,0:T(8,128)S(1)} %bitcast_divide_fusion.3, f32[2,384,2]{1,2,0:T(2,128)S(1)} %collective-permute-done.1, f32[2,384,2]{1,2,0:T(2,128)S(1)} %collective-permute-done, f32[]{:T(128)} %bitcast.16, f32[]{:T(128)} %bitcast.15, f32[]{:T(128)} %bitcast.14, f32[]{:T(128)} %bitcast.13, f32[]{:T(128)} %bitcast), kind=kLoop, calls=%fused_computation.88 | loop fusion | flops 1916928 | bytes 1191956 | tf_op jit(solution)/shard_map/transpose | solution.py:74
  243.0 27.1 %gather_fusion.3 = f32[7168,24]{1,0:T(8,128)} fusion(f32[12288,24]{1,0:T(8,128)} %bitcast.114, s32[7168]{0:T(1024)S(1)} %fusion.85), kind=kCustom, calls=%fused_computation.5.clone | custom fusion | bytes 1404928 | tf_op jit(solution)/shard_map/jit(_take)/gather | solution.py:54
  270.1 7.0 %broadcast_select_fusion.2 = f32[7168,24]{1,0:T(8,128)} fusion(f32[7168,24]{1,0:T(8,128)} %gather_fusion.3, pred[7168]{0:T(1024)(128)(4,1)S(1)} %compare_and_fusion.2), kind=kLoop, calls=%fused_computation.27 | loop fusion | flops 172032 | bytes 1383424 | tf_op jit(solution)/shard_map/jit(_take)/select_n | solution.py:54
  280.6 4.6 %all-to-all-start.1 = ((f32[8,896,24]{1,2,0:T(8,128)}), f32[8,896,24]{1,2,0:T(8,128)S(1)}, u32[]{:S(2)}, u32[]{:S(2)}) async-start(f32[8,896,24]{1,2,0:T(8,128)} %copy.12), calls=%async_computation.1 | async-start | bytes 1376256 | tf_op jit(solution)/shard_map/all_to_all | solution.py:55
  285.3 18.4 %all-to-all-done.1 = f32[8,896,24]{1,2,0:T(8,128)S(1)} async-done(((f32[8,896,24]{1,2,0:T(8,128)}), f32[8,896,24]{1,2,0:T(8,128)S(1)}, u32[]{:S(2)}, u32[]{:S(2)}) %all-to-all-start.1) | async-done | bytes 688160 | tf_op jit(solution)/shard_map/all_to_all | solution.py:55
  318.6 11.2 %fusion.72 = f32[2,192,3072]{2,1,0:T(8,128)} fusion(f32[2,3072,384]{2,1,0:T(8,128)} %all-gather.11.cloned.1.call-done, f32[2,192,384]{2,1,0:T(8,128)S(1)} %copy-done.2, f32[2]{0:T(128)S(1)} %get-tuple-element.20), kind=kOutput, calls=%fused_computation.113 | convolution fusion | flops 2718056448 | bytes 14745608 | tf_op jit(solution)/shard_map/rfs,rgs->rfg/dot_general | solution.py:21
  329.7 11.2 %fusion.74 = f32[2,192,3072]{2,1,0:T(8,128)} fusion(f32[2,3072,384]{2,1,0:T(8,128)} %all-gather.9.cloned.1.call-done, f32[2,192,384]{2,1,0:T(8,128)S(1)} %copy-done.3, f32[2]{0:T(128)S(1)} %get-tuple-element.21), kind=kOutput, calls=%fused_computation.115 | convolution fusion | flops 2718056448 | bytes 14745608 | tf_op jit(solution)/shard_map/rfs,rgs->rfg/dot_general | solution.py:21
  340.9 11.5 %fusion.78 = f32[2,192,3072]{2,1,0:T(8,128)} fusion(f32[2,3072,384]{2,1,0:T(8,128)} %all-gather.5.cloned.1.call-done, f32[2,192,384]{2,1,0:T(8,128)S(1)} %copy-done.4, f32[2]{0:T(128)S(1)} %get-tuple-element.19), kind=kOutput, calls=%fused_computation.119 | convolution fusion | flops 2718056448 | bytes 14745608 | tf_op jit(solution)/shard_map/rfs,rgs->rfg/dot_general | solution.py:21
  352.5 24.9 %all-gather.7.cloned.1.call-done = f32[2,3072,384]{2,1,0:T(8,128)} async-done(((f32[2,192,384]{2,1,0:T(8,128)}), f32[2,3072,384]{2,1,0:T(8,128)}) %all-gather.7.cloned.1.call-update) | async-done | bytes 9437200 | tf_op jit(solution)/shard_map/all_gather | solution.py:77
  377.4 8.0 %fusion.76 = f32[2,192,3072]{2,1,0:T(8,128)S(1)} fusion(f32[2,3072,384]{2,1,0:T(8,128)} %all-gather.7.cloned.1.call-done, f32[2,192,384]{2,1,0:T(8,128)S(1)} %copy-done.5, f32[2]{0:T(128)S(1)} %get-tuple-element.22), kind=kOutput, calls=%fused_computation.117 | convolution fusion | flops 2718056448 | bytes 14745608 | tf_op jit(solution)/shard_map/rfs,rgs->rfg/dot_general | solution.py:21
  385.4 9.0 %pad_maximum_fusion = f32[8,192,3072]{2,1,0:T(8,128)} fusion(f32[2,192,3072]{2,1,0:T(8,128)} %fusion.72, f32[2,192,3072]{2,1,0:T(8,128)S(1)} %copy-done, f32[2,192,3072]{2,1,0:T(8,128)S(1)} %fusion.76, f32[2,192,3072]{2,1,0:T(8,128)S(1)} %copy-done.1), kind=kLoop, calls=%fused_computation.8 | loop fusion | flops 14155776 | bytes 37748736 | tf_op jit(solution)/shard_map/concatenate | solution.py:79
  (125 shorter events, 72.3 us)
Async XLA Ops:
  42.3 18.8 %copy-start.7 = (s32[64]{0:T(128)S(1)}, s32[64]{0:T(128)}, u32[]{:S(2)}) copy-start(s32[64]{0:T(128)} %param.10) | copy-start | bytes 772
  49.2 31.5 %copy-start.6 = (f32[5]{0:T(128)S(1)}, f32[5]{0:T(128)}, u32[]{:S(2)}) copy-start(f32[5]{0:T(128)} %param.11) | copy-start | bytes 64
  52.6 19.9 %all-to-all-start.3 = ((f32[8,896,24]{1,2,0:T(8,128)}), f32[8,896,24]{1,2,0:T(8,128)S(1)}, u32[]{:S(2)}, u32[]{:S(2)}) async-start(f32[8,896,24]{1,2,0:T(8,128)} %copy.16), calls=%async_computation.3 | async-start | bytes 1376256 | tf_op jit(solution)/shard_map/all_to_all | solution.py:55
  61.0 257.5 %all-gather.11.cloned.1.call-start = ((), (), s32[]{:S(2)}) async-start(), calls=%async_computation.7 | async-start | bytes 10027008 | tf_op jit(solution)/shard_map/all_gather | solution.py:77
  74.7 6.8 %collective-permute-start.6 = (f32[2,384,2]{1,2,0:T(2,128)S(1)}, f32[2,384,2]{1,2,0:T(2,128)S(1)}, u32[]{:S(2)}, u32[]{:S(2)}) collective-permute-start(f32[2,384,2]{1,2,0:T(2,128)S(1)} %get-tuple-element.17), channel_id=1, source_target_pairs={{0,1},{1,2},{2,3},{3,4},{4,5},{5,6},{6,7},{7,8},{8,9},{9,10},{10,1... | collective-permute-start | bytes 18440 | tf_op jit(solution)/shard_map/ppermute | solution.py:15
  78.8 4.9 %collective-permute-start.7 = (f32[2,384,2]{1,2,0:T(2,128)S(1)}, f32[2,384,2]{1,2,0:T(2,128)S(1)}, u32[]{:S(2)}, u32[]{:S(2)}) collective-permute-start(f32[2,384,2]{1,2,0:T(2,128)S(1)} %get-tuple-element.18), channel_id=1, source_target_pairs={{1,0},{2,1},{3,2},{4,3},{5,4},{6,5},{7,6},{8,7},{9,8},{10,9},{11,1... | collective-permute-start | bytes 18440 | tf_op jit(solution)/shard_map/ppermute | solution.py:16
  126.5 24.9 %all-to-all-start.2 = ((f32[8,896,24]{1,2,0:T(8,128)}), f32[8,896,24]{1,2,0:T(8,128)S(1)}, u32[]{:S(2)}, u32[]{:S(2)}) async-start(f32[8,896,24]{1,2,0:T(8,128)} %copy.14), calls=%async_computation.2 | async-start | bytes 1376256 | tf_op jit(solution)/shard_map/all_to_all | solution.py:55
  133.0 196.8 %all-gather.9.cloned.1.call-start = ((), (), s32[]{:S(2)}) async-start(), calls=%async_computation.6 | async-start | bytes 10027008 | tf_op jit(solution)/shard_map/all_gather | solution.py:77
  153.7 4.8 %collective-permute-start.4 = (f32[2,384,2]{1,2,0:T(2,128)S(1)}, f32[2,384,2]{1,2,0:T(2,128)S(1)}, u32[]{:S(2)}, u32[]{:S(2)}) collective-permute-start(f32[2,384,2]{1,2,0:T(2,128)S(1)} %get-tuple-element.15), channel_id=1, source_target_pairs={{0,1},{1,2},{2,3},{3,4},{4,5},{5,6},{6,7},{7,8},{8,9},{9,10},{10,1... | collective-permute-start | bytes 18440 | tf_op jit(solution)/shard_map/ppermute | solution.py:15
  156.5 4.9 %collective-permute-start.5 = (f32[2,384,2]{1,2,0:T(2,128)S(1)}, f32[2,384,2]{1,2,0:T(2,128)S(1)}, u32[]{:S(2)}, u32[]{:S(2)}) collective-permute-start(f32[2,384,2]{1,2,0:T(2,128)S(1)} %get-tuple-element.16), channel_id=1, source_target_pairs={{1,0},{2,1},{3,2},{4,3},{5,4},{6,5},{7,6},{8,7},{9,8},{10,9},{11,1... | collective-permute-start | bytes 18440 | tf_op jit(solution)/shard_map/ppermute | solution.py:16
  204.4 23.2 %all-to-all-start = ((f32[8,896,24]{1,2,0:T(8,128)}), f32[8,896,24]{1,2,0:T(8,128)S(1)}, u32[]{:S(2)}, u32[]{:S(2)}) async-start(f32[8,896,24]{1,2,0:T(8,128)} %copy.10), calls=%async_computation | async-start | bytes 1376256 | tf_op jit(solution)/shard_map/all_to_all | solution.py:55
  209.1 131.9 %all-gather.5.cloned.1.call-start = ((), (), s32[]{:S(2)}) async-start(), calls=%async_computation.4 | async-start | bytes 10027008 | tf_op jit(solution)/shard_map/all_gather | solution.py:77
  229.8 5.0 %collective-permute-start = (f32[2,384,2]{1,2,0:T(2,128)S(1)}, f32[2,384,2]{1,2,0:T(2,128)S(1)}, u32[]{:S(2)}, u32[]{:S(2)}) collective-permute-start(f32[2,384,2]{1,2,0:T(2,128)S(1)} %get-tuple-element.11), channel_id=1, source_target_pairs={{0,1},{1,2},{2,3},{3,4},{4,5},{5,6},{6,7},{7,8},{8,9},{9,10},{10,1... | collective-permute-start | bytes 18440 | tf_op jit(solution)/shard_map/ppermute | solution.py:15
  232.8 4.9 %collective-permute-start.1 = (f32[2,384,2]{1,2,0:T(2,128)S(1)}, f32[2,384,2]{1,2,0:T(2,128)S(1)}, u32[]{:S(2)}, u32[]{:S(2)}) collective-permute-start(f32[2,384,2]{1,2,0:T(2,128)S(1)} %get-tuple-element.12), channel_id=1, source_target_pairs={{1,0},{2,1},{3,2},{4,3},{5,4},{6,5},{7,6},{8,7},{9,8},{10,9},{11,1... | collective-permute-start | bytes 18440 | tf_op jit(solution)/shard_map/ppermute | solution.py:16
  277.1 41.4 %copy-start.2 = (f32[2,192,384]{2,1,0:T(8,128)S(1)}, f32[2,192,384]{2,1,0:T(8,128)}, u32[]{:S(2)}) copy-start(f32[2,192,384]{2,1,0:T(8,128)} %fusion.32) | copy-start | bytes 1769476
  280.6 23.1 %all-to-all-start.1 = ((f32[8,896,24]{1,2,0:T(8,128)}), f32[8,896,24]{1,2,0:T(8,128)S(1)}, u32[]{:S(2)}, u32[]{:S(2)}) async-start(f32[8,896,24]{1,2,0:T(8,128)} %copy.12), calls=%async_computation.1 | async-start | bytes 1376256 | tf_op jit(solution)/shard_map/all_to_all | solution.py:55
  285.2 92.2 %all-gather.7.cloned.1.call-start = ((), (), s32[]{:S(2)}) async-start(), calls=%async_computation.5 | async-start | bytes 10027008 | tf_op jit(solution)/shard_map/all_gather | solution.py:77
  305.9 5.2 %collective-permute-start.2 = (f32[2,384,2]{1,2,0:T(2,128)S(1)}, f32[2,384,2]{1,2,0:T(2,128)S(1)}, u32[]{:S(2)}, u32[]{:S(2)}) collective-permute-start(f32[2,384,2]{1,2,0:T(2,128)S(1)} %get-tuple-element.13), channel_id=1, source_target_pairs={{0,1},{1,2},{2,3},{3,4},{4,5},{5,6},{6,7},{7,8},{8,9},{9,10},{10,1... | collective-permute-start | bytes 18440 | tf_op jit(solution)/shard_map/ppermute | solution.py:15
  309.1 4.9 %collective-permute-start.3 = (f32[2,384,2]{1,2,0:T(2,128)S(1)}, f32[2,384,2]{1,2,0:T(2,128)S(1)}, u32[]{:S(2)}, u32[]{:S(2)}) collective-permute-start(f32[2,384,2]{1,2,0:T(2,128)S(1)} %get-tuple-element.14), channel_id=1, source_target_pairs={{1,0},{2,1},{3,2},{4,3},{5,4},{6,5},{7,6},{8,7},{9,8},{10,9},{11,1... | collective-permute-start | bytes 18440 | tf_op jit(solution)/shard_map/ppermute | solution.py:16
  318.6 11.2 %copy-start.3 = (f32[2,192,384]{2,1,0:T(8,128)S(1)}, f32[2,192,384]{2,1,0:T(8,128)}, u32[]{:S(2)}) copy-start(f32[2,192,384]{2,1,0:T(8,128)} %fusion.41) | copy-start | bytes 1769476
  329.7 11.2 %copy-start.4 = (f32[2,192,384]{2,1,0:T(8,128)S(1)}, f32[2,192,384]{2,1,0:T(8,128)}, u32[]{:S(2)}) copy-start(f32[2,192,384]{2,1,0:T(8,128)} %fusion.59) | copy-start | bytes 1769476
  340.9 36.5 %copy-start.5 = (f32[2,192,384]{2,1,0:T(8,128)S(1)}, f32[2,192,384]{2,1,0:T(8,128)}, u32[]{:S(2)}) copy-start(f32[2,192,384]{2,1,0:T(8,128)} %fusion.50) | copy-start | bytes 1769476
  377.4 8.0 %copy-start = (f32[2,192,3072]{2,1,0:T(8,128)S(1)}, f32[2,192,3072]{2,1,0:T(8,128)}, u32[]{:S(2)}) copy-start(f32[2,192,3072]{2,1,0:T(8,128)} %fusion.74) | copy-start | bytes 14155780
  377.4 8.0 %copy-start.1 = (f32[2,192,3072]{2,1,0:T(8,128)S(1)}, f32[2,192,3072]{2,1,0:T(8,128)}, u32[]{:S(2)}) copy-start(f32[2,192,3072]{2,1,0:T(8,128)} %fusion.78) | copy-start | bytes 14155780
Sparse Core Ops, SparseCore 0:
  88.3 66.1 all-gather.10
  166.1 66.1 all-gather.8
  242.3 66.3 all-gather.4
  318.6 58.7 all-gather.6

commit v8 on v6

--- a/solution.py
+++ b/solution.py
@@ -4,7 +4,7 @@
 from jax.sharding import PartitionSpec as P
 
 REACH = 2
-PARTS = 4
+PARTS = 2
 
 
 def halo_frames(block, width):

time: 398 us -> 389 us (0.977)
  waiting for transfers between devices: 82 us -> 137 us
  between operations: 91.3 us -> 58.2 us
  starting transfers between devices: 43 us -> 24.7 us
  other arithmetic: 40.2 us -> 26.5 us
  local copies, waits for them, and re-layouts: 97.1 us -> 108 us
  matrix products: 42.1 us -> 33.3 us
    all_gather x4 -> x2, waiting for transfers between devices: 33.3 us -> 104 us  [per_device(): right = lax.all_gather(smooth, 'tm', axis=1, tiled=True)]
    gather x8 -> x4, local copies, waits for them, and re-layouts: 83 us -> 96.5 us  [per_device(): chunks = jnp.take(series, wanted, axis=0)]
    all_to_all x4 -> x2, waiting for transfers between devices: 36.8 us -> 26.4 us  [per_device(): got = lax.all_to_all(chunks, 'pix', 0, 0, tiled=True)]
    dot_general x4 -> x2, matrix products: 42.1 us -> 33.3 us  [correlate(): jnp.einsum('rfs,rgs->rfg', left, right, precision=lax.Precision.HIGH, pre...]
    all_to_all x4 -> x2, starting transfers between devices: 21.6 us -> 13.3 us  [per_device(): got = lax.all_to_all(chunks, 'pix', 0, 0, tiled=True)]
    transpose x4 -> x2, other arithmetic: 17.7 us -> 9.45 us  [per_device(): smooth = jnp.swapaxes(smooth, 1, 2)]
    ppermute x4 -> x2, starting transfers between devices: 13.4 us -> 7.29 us  [halo_frames(): low = lax.ppermute(block[..., n - width:], 'tm', forward)]
    ppermute x4 -> x2, waiting for transfers between devices: 11.8 us -> 6.1 us  [halo_frames(): high = lax.ppermute(block[..., :width], 'tm', backward)]
  transfers between devices with their start and end apart: 16 -> 8, of which waited for: 9 -> 6; matrix products, arithmetic and copies ran while one was open for 32% -> 20% of each run, Pallas kernels for 0% -> 0%
where the time goes in v8:
time: 389 us; the launch traced here: 387 us
  waiting for transfers between devices  137 us (35%)
  local copies, waits for them, and re-layouts  108 us (28%)
  between operations  58.2 us (15%)
  matrix products  33.3 us (9%)
  other arithmetic  26.5 us (7%)
  starting transfers between devices  24.7 us (6%)
    all_gather x2, waiting for transfers between devices, per_device(): right = lax.all_gather(smooth, 'tm', axis=1, tiled=True)  104 us
    gather x4, local copies, waits for them, and re-layouts, per_device(): chunks = jnp.take(series, wanted, axis=0)  96.5 us
    dot_general x2, matrix products, correlate(): jnp.einsum('rfs,rgs->rfg', left, right, precision=lax.Precision.HIGH, pre...  33.3 us
    all_to_all x2, waiting for transfers between devices, per_device(): got = lax.all_to_all(chunks, 'pix', 0, 0, tiled=True)  26.4 us
    all_to_all x2, starting transfers between devices, per_device(): got = lax.all_to_all(chunks, 'pix', 0, 0, tiled=True)  13.3 us
    concatenate x1, other arithmetic, per_device(): return jnp.concatenate(outs, 0)  10.6 us
    transpose x2, other arithmetic, per_device(): smooth = jnp.swapaxes(smooth, 1, 2)  9.45 us
  transfers between devices with their start and end apart: 8, of which 6 were waited for; matrix products, arithmetic and copies ran while one was open for 20% of the time, Pallas kernels for 0%

profile of v8, /device:TPU:1, one launch (start us, length us, event | category | flops | bytes accessed | tf_op | source)
XLA Modules:
  0.0 387.4 jit_solution(68569612356899170)
XLA Ops:
  41.1 4.9 %copy.10 = f32[1,24,12288]{1,2,0:T(8,128)} copy(f32[1,24,12288]{2,1,0:T(8,128)} %param.6) | data formatting | bytes 2359296 | tf_op args[0]
  46.0 43.8 %gather_fusion.1 = f32[12288,24]{1,0:T(8,128)} fusion(f32[12288,24]{1,0:T(8,128)} %bitcast.77, s32[12288]{0:T(1024)S(1)} %broadcast_clamp_fusion), kind=kCustom, calls=%fused_computation.1.clone | custom fusion | bytes 2408448 | tf_op jit(solution)/shard_map/jit(_take)/gather | solution.py:51
  89.8 4.3 %copy.12 = f32[8,1536,24]{1,2,0:T(8,128)S(1)} copy(f32[8,1536,24]{2,1,0:T(8,128)} %bitcast.80) | data formatting | bytes 2359296 | tf_op jit(solution)/shard_map/jit(_take)/gather | solution.py:51
  95.3 8.6 %all-to-all-start.1 = ((f32[8,1536,24]{1,2,0:T(8,128)}), f32[8,1536,24]{1,2,0:T(8,128)S(1)}, u32[]{:S(2)}, u32[]{:S(2)}) async-start(f32[8,1536,24]{1,2,0:T(8,128)} %broadcast_select_fusion), calls=%async_computation.1 | async-start | bytes 2359296 | tf_op jit(solution)/shard_map/all_to_all | solution.py:52
  104.6 1.3 slice_subtract_fusion.1
  114.2 5.3 %all-to-all-done.1 = f32[8,1536,24]{1,2,0:T(8,128)S(1)} async-done(((f32[8,1536,24]{1,2,0:T(8,128)}), f32[8,1536,24]{1,2,0:T(8,128)S(1)}, u32[]{:S(2)}, u32[]{:S(2)}) %all-to-all-start.1) | async-done | bytes 1179680 | tf_op jit(solution)/shard_map/all_to_all | solution.py:52
  120.5 4.4 %collective-permute-start.2 = (f32[4,384,2]{1,2,0:T(2,128)S(1)}, f32[4,384,2]{1,2,0:T(2,128)S(1)}, u32[]{:S(2)}, u32[]{:S(2)}) collective-permute-start(f32[4,384,2]{1,2,0:T(2,128)S(1)} %get-tuple-element.20), channel_id=1, source_target_pairs={{0,1},{1,2},{2,3},{3,4},{4,5},{5,6},{6,7},{7,8},{8,9},{9,10},{10,1... | collective-permute-start | bytes 36872 | tf_op jit(solution)/shard_map/ppermute | solution.py:15
  124.9 1.9 collective-permute-start.3
  127.5 2.4 collective-permute-done.3
  129.9 4.7 %fusion.4 = f32[4,192,384]{2,1,0:T(8,128)} fusion(f32[4,384,192]{1,2,0:T(8,128)S(1)} %bitcast_divide_fusion, f32[4,384,2]{1,2,0:T(2,128)S(1)} %collective-permute-done.3, f32[4,384,2]{1,2,0:T(2,128)S(1)} %collective-permute-done.2, f32[]{:T(128)} %bitcast.28, f32[]{:T(128)} %bitcast.27, f32[]{:T(128)} %bitcast.26, f32[]{:T(128)} %bitcast.25, f32[]{:T(128)} %bitcast), kind=kLoop, calls=%fused_computation.23 | loop fusion | flops 3833856 | bytes 2383892 | tf_op jit(solution)/shard_map/transpose | solution.py:69
  134.9 43.9 %gather_fusion = f32[12288,24]{1,0:T(8,128)} fusion(f32[12288,24]{1,0:T(8,128)} %bitcast.78, s32[12288]{0:T(1024)S(1)} %broadcast_clamp_fusion.1), kind=kCustom, calls=%fused_computation.clone | custom fusion | bytes 2408448 | tf_op jit(solution)/shard_map/jit(_take)/gather | solution.py:51
  178.8 4.5 %copy.11 = f32[8,1536,24]{1,2,0:T(8,128)S(1)} copy(f32[8,1536,24]{2,1,0:T(8,128)} %bitcast.79) | data formatting | bytes 2359296 | tf_op jit(solution)/shard_map/jit(_take)/gather | solution.py:51
  183.4 1.2 broadcast_select_fusion.1
  184.5 4.7 %all-to-all-start = ((f32[8,1536,24]{1,2,0:T(8,128)}), f32[8,1536,24]{1,2,0:T(8,128)S(1)}, u32[]{:S(2)}, u32[]{:S(2)}) async-start(f32[8,1536,24]{1,2,0:T(8,128)} %broadcast_select_fusion.1), calls=%async_computation | async-start | bytes 2359296 | tf_op jit(solution)/shard_map/all_to_all | solution.py:52
  197.1 21.1 %all-to-all-done = f32[8,1536,24]{1,2,0:T(8,128)S(1)} async-done(((f32[8,1536,24]{1,2,0:T(8,128)}), f32[8,1536,24]{1,2,0:T(8,128)S(1)}, u32[]{:S(2)}, u32[]{:S(2)}) %all-to-all-start) | async-done | bytes 1179680 | tf_op jit(solution)/shard_map/all_to_all | solution.py:52
  219.2 2.9 collective-permute-start
  222.1 2.1 collective-permute-start.1
  224.2 3.7 collective-permute-done.1
  227.9 4.7 %fusion.13 = f32[4,192,384]{2,1,0:T(8,128)} fusion(f32[4,384,192]{1,2,0:T(8,128)S(1)} %bitcast_divide_fusion.1, f32[4,384,2]{1,2,0:T(2,128)S(1)} %collective-permute-done.1, f32[4,384,2]{1,2,0:T(2,128)S(1)} %collective-permute-done, f32[]{:T(128)} %bitcast.28, f32[]{:T(128)} %bitcast.27, f32[]{:T(128)} %bitcast.26, f32[]{:T(128)} %bitcast.25, f32[]{:T(128)} %bitcast), kind=kLoop, calls=%fused_computation.32 | loop fusion | flops 3833856 | bytes 2383892 | tf_op jit(solution)/shard_map/transpose | solution.py:69
  232.6 16.9 %all-gather.5.cloned.1.call-done = f32[4,3072,384]{2,1,0:T(8,128)} async-done(((f32[4,192,384]{2,1,0:T(8,128)}), f32[4,3072,384]{2,1,0:T(8,128)}) %all-gather.5.cloned.1.call-update) | async-done | bytes 18874384 | tf_op jit(solution)/shard_map/all_gather | solution.py:72
  249.6 16.6 %fusion.22 = f32[4,192,3072]{2,1,0:T(8,128)} fusion(f32[4,3072,384]{2,1,0:T(8,128)} %all-gather.5.cloned.1.call-done, f32[4,192,384]{2,1,0:T(8,128)S(1)} %copy-done.1, f32[4]{0:T(128)S(1)} %get-tuple-element.59), kind=kOutput, calls=%fused_computation.51 | convolution fusion | flops 5436112896 | bytes 29491216 | tf_op jit(solution)/shard_map/rfs,rgs->rfg/dot_general | solution.py:21
  266.2 87.1 %all-gather.3.cloned.1.call-done = f32[4,3072,384]{2,1,0:T(8,128)} async-done(((f32[4,192,384]{2,1,0:T(8,128)}), f32[4,3072,384]{2,1,0:T(8,128)}) %all-gather.3.cloned.1.call-update) | async-done | bytes 18874384 | tf_op jit(solution)/shard_map/all_gather | solution.py:72
  353.3 16.7 %fusion.24 = f32[4,192,3072]{2,1,0:T(8,128)} fusion(f32[4,3072,384]{2,1,0:T(8,128)} %all-gather.3.cloned.1.call-done, f32[4,192,384]{2,1,0:T(8,128)S(1)} %copy-done.2, f32[4]{0:T(128)S(1)} %get-tuple-element.58), kind=kOutput, calls=%fused_computation.53 | convolution fusion | flops 5436112896 | bytes 29491216 | tf_op jit(solution)/shard_map/rfs,rgs->rfg/dot_general | solution.py:21
  369.9 10.6 %pad_maximum_fusion = f32[8,192,3072]{2,1,0:T(8,128)} fusion(f32[4,192,3072]{2,1,0:T(8,128)S(1)} %copy-done, f32[4,192,3072]{2,1,0:T(8,128)} %fusion.24), kind=kLoop, calls=%fused_computation.2 | loop fusion | flops 4718592 | bytes 37748736 | tf_op jit(solution)/shard_map/concatenate | solution.py:74
  (75 shorter events, 10.8 us)
Async XLA Ops:
  95.3 8.7 %copy-start.4 = (s32[64]{0:T(128)S(1)}, s32[64]{0:T(128)}, u32[]{:S(2)}) copy-start(s32[64]{0:T(128)} %param.8) | copy-start | bytes 772
  95.3 24.3 %all-to-all-start.1 = ((f32[8,1536,24]{1,2,0:T(8,128)}), f32[8,1536,24]{1,2,0:T(8,128)S(1)}, u32[]{:S(2)}, u32[]{:S(2)}) async-start(f32[8,1536,24]{1,2,0:T(8,128)} %broadcast_select_fusion), calls=%async_computation.1 | async-start | bytes 2359296 | tf_op jit(solution)/shard_map/all_to_all | solution.py:52
  103.9 145.7 %all-gather.5.cloned.1.call-start = ((), (), s32[]{:S(2)}) async-start(), calls=%async_computation.3 | async-start | bytes 20054016 | tf_op jit(solution)/shard_map/all_gather | solution.py:72
  120.3 6.6 %copy-start.3 = (f32[5]{0:T(128)S(1)}, f32[5]{0:T(128)}, u32[]{:S(2)}) copy-start(f32[5]{0:T(128)} %param.9) | copy-start | bytes 64
  120.5 7.0 %collective-permute-start.2 = (f32[4,384,2]{1,2,0:T(2,128)S(1)}, f32[4,384,2]{1,2,0:T(2,128)S(1)}, u32[]{:S(2)}, u32[]{:S(2)}) collective-permute-start(f32[4,384,2]{1,2,0:T(2,128)S(1)} %get-tuple-element.20), channel_id=1, source_target_pairs={{0,1},{1,2},{2,3},{3,4},{4,5},{5,6},{6,7},{7,8},{8,9},{9,10},{10,1... | collective-permute-start | bytes 36872 | tf_op jit(solution)/shard_map/ppermute | solution.py:15
  124.9 5.0 %collective-permute-start.3 = (f32[4,384,2]{1,2,0:T(2,128)S(1)}, f32[4,384,2]{1,2,0:T(2,128)S(1)}, u32[]{:S(2)}, u32[]{:S(2)}) collective-permute-start(f32[4,384,2]{1,2,0:T(2,128)S(1)} %get-tuple-element.21), channel_id=1, source_target_pairs={{1,0},{2,1},{3,2},{4,3},{5,4},{6,5},{7,6},{8,7},{9,8},{10,9},{11,1... | collective-permute-start | bytes 36872 | tf_op jit(solution)/shard_map/ppermute | solution.py:16
  184.5 33.7 %all-to-all-start = ((f32[8,1536,24]{1,2,0:T(8,128)}), f32[8,1536,24]{1,2,0:T(8,128)S(1)}, u32[]{:S(2)}, u32[]{:S(2)}) async-start(f32[8,1536,24]{1,2,0:T(8,128)} %broadcast_select_fusion.1), calls=%async_computation | async-start | bytes 2359296 | tf_op jit(solution)/shard_map/all_to_all | solution.py:52
  189.2 164.1 %all-gather.3.cloned.1.call-start = ((), (), s32[]{:S(2)}) async-start(), calls=%async_computation.2 | async-start | bytes 20054016 | tf_op jit(solution)/shard_map/all_gather | solution.py:72
  219.2 5.0 %collective-permute-start = (f32[4,384,2]{1,2,0:T(2,128)S(1)}, f32[4,384,2]{1,2,0:T(2,128)S(1)}, u32[]{:S(2)}, u32[]{:S(2)}) collective-permute-start(f32[4,384,2]{1,2,0:T(2,128)S(1)} %get-tuple-element.14), channel_id=1, source_target_pairs={{0,1},{1,2},{2,3},{3,4},{4,5},{5,6},{6,7},{7,8},{8,9},{9,10},{10,1... | collective-permute-start | bytes 36872 | tf_op jit(solution)/shard_map/ppermute | solution.py:15
  222.1 5.8 %collective-permute-start.1 = (f32[4,384,2]{1,2,0:T(2,128)S(1)}, f32[4,384,2]{1,2,0:T(2,128)S(1)}, u32[]{:S(2)}, u32[]{:S(2)}) collective-permute-start(f32[4,384,2]{1,2,0:T(2,128)S(1)} %get-tuple-element.15), channel_id=1, source_target_pairs={{1,0},{2,1},{3,2},{4,3},{5,4},{6,5},{7,6},{8,7},{9,8},{10,9},{11,1... | collective-permute-start | bytes 36872 | tf_op jit(solution)/shard_map/ppermute | solution.py:16
  232.6 17.0 %copy-start.1 = (f32[4,192,384]{2,1,0:T(8,128)S(1)}, f32[4,192,384]{2,1,0:T(8,128)}, u32[]{:S(2)}) copy-start(f32[4,192,384]{2,1,0:T(8,128)} %fusion.4) | copy-start | bytes 3538948
  249.5 103.7 %copy-start.2 = (f32[4,192,384]{2,1,0:T(8,128)S(1)}, f32[4,192,384]{2,1,0:T(8,128)}, u32[]{:S(2)}) copy-start(f32[4,192,384]{2,1,0:T(8,128)} %fusion.13) | copy-start | bytes 3538948
  353.3 16.7 %copy-start = (f32[4,192,3072]{2,1,0:T(8,128)S(1)}, f32[4,192,3072]{2,1,0:T(8,128)}, u32[]{:S(2)}) copy-start(f32[4,192,3072]{2,1,0:T(8,128)} %fusion.22) | copy-start | bytes 28311556
Sparse Core Ops, SparseCore 0:
  134.8 114.6 all-gather.4
  251.2 102.0 all-gather.2

commit v9 on v8

--- a/solution.py
+++ b/solution.py
@@ -71,7 +71,8 @@
         scale = sizes[first : first + step].astype(jnp.float32)
         right = lax.all_gather(smooth, "tm", axis=1, tiled=True)
         outs.append(correlate(smooth * scale[:, None, None], right))
-    return jnp.concatenate(outs, 0)
+    result = lax.optimization_barrier(jnp.pad(jnp.concatenate(outs[:-1], 0), ((0, step), (0, 0), (0, 0))))
+    return lax.dynamic_update_slice_in_dim(result, outs[-1], owned - step, 0)
 
 
 def solution(mesh):

time: 389 us -> 378 us (0.972)
  waiting for transfers between devices: 137 us -> 123 us
  local copies, waits for them, and re-layouts: 108 us -> 121 us
  other arithmetic: 26.5 us -> 16 us
    all_gather x2, waiting for transfers between devices: 104 us -> 90.7 us  [per_device(): right = lax.all_gather(smooth, 'tm', axis=1, tiled=True)]
    pad x0 -> x1, local copies, waits for them, and re-layouts: none -> 13.3 us  [per_device(): jnp.pad(jnp.concatenate(outs[:-1], 0), ((0, step), (0, 0), (0, 0)))]
    concatenate x1 -> x0, other arithmetic: 10.6 us -> none  [per_device(): return jnp.concatenate(outs, 0)]
  transfers between devices with their start and end apart: 8 -> 8, of which waited for: 6 -> 6; matrix products, arithmetic and copies ran while one was open for 20% -> 24% of each run, Pallas kernels for 0% -> 0%
where the time goes in v9:
time: 378 us; the launch traced here: 377 us
  waiting for transfers between devices  123 us (33%)
  local copies, waits for them, and re-layouts  121 us (32%)
  between operations  58.2 us (15%)
  matrix products  33.1 us (9%)
  starting transfers between devices  24.7 us (7%)
  other arithmetic  16 us (4%)
    gather x4, local copies, waits for them, and re-layouts, per_device(): chunks = jnp.take(series, wanted, axis=0)  96.5 us
    all_gather x2, waiting for transfers between devices, per_device(): right = lax.all_gather(smooth, 'tm', axis=1, tiled=True)  90.7 us
    dot_general x2, matrix products, correlate(): jnp.einsum('rfs,rgs->rfg', left, right, precision=lax.Precision.HIGH, pre...  33.1 us
    all_to_all x2, waiting for transfers between devices, per_device(): got = lax.all_to_all(chunks, 'pix', 0, 0, tiled=True)  26.4 us
    all_to_all x2, starting transfers between devices, per_device(): got = lax.all_to_all(chunks, 'pix', 0, 0, tiled=True)  13.3 us
    pad x1, local copies, waits for them, and re-layouts, per_device(): jnp.pad(jnp.concatenate(outs[:-1], 0), ((0, step), (0, 0), (0, 0)))  13.3 us
    transpose x2, other arithmetic, per_device(): smooth = jnp.swapaxes(smooth, 1, 2)  9.62 us
  transfers between devices with their start and end apart: 8, of which 6 were waited for; matrix products, arithmetic and copies ran while one was open for 24% of the time, Pallas kernels for 0%

profile of v9, /device:TPU:1, one launch (start us, length us, event | category | flops | bytes accessed | tf_op | source)
XLA Modules:
  0.0 376.7 jit_solution(11704272782807116783)
XLA Ops:
  41.1 4.9 %copy.10 = f32[1,24,12288]{1,2,0:T(8,128)} copy(f32[1,24,12288]{2,1,0:T(8,128)} %param.6) | data formatting | bytes 2359296 | tf_op args[0]
  45.9 43.8 %gather_fusion = f32[12288,24]{1,0:T(8,128)} fusion(f32[12288,24]{1,0:T(8,128)} %bitcast.77, s32[12288]{0:T(1024)S(1)} %broadcast_clamp_fusion.1), kind=kCustom, calls=%fused_computation.clone | custom fusion | bytes 2408448 | tf_op jit(solution)/shard_map/jit(_take)/gather | solution.py:51
  89.7 4.3 %copy.11 = f32[8,1536,24]{1,2,0:T(8,128)S(1)} copy(f32[8,1536,24]{2,1,0:T(8,128)} %bitcast.80) | data formatting | bytes 2359296 | tf_op jit(solution)/shard_map/jit(_take)/gather | solution.py:51
  95.3 8.6 %all-to-all-start = ((f32[8,1536,24]{1,2,0:T(8,128)}), f32[8,1536,24]{1,2,0:T(8,128)S(1)}, u32[]{:S(2)}, u32[]{:S(2)}) async-start(f32[8,1536,24]{1,2,0:T(8,128)} %broadcast_select_fusion.1), calls=%async_computation | async-start | bytes 2359296 | tf_op jit(solution)/shard_map/all_to_all | solution.py:52
  104.7 1.3 slice_subtract_fusion
  114.2 5.3 %all-to-all-done = f32[8,1536,24]{1,2,0:T(8,128)S(1)} async-done(((f32[8,1536,24]{1,2,0:T(8,128)}), f32[8,1536,24]{1,2,0:T(8,128)S(1)}, u32[]{:S(2)}, u32[]{:S(2)}) %all-to-all-start) | async-done | bytes 1179680 | tf_op jit(solution)/shard_map/all_to_all | solution.py:52
  120.5 4.4 %collective-permute-start = (f32[4,384,2]{1,2,0:T(2,128)S(1)}, f32[4,384,2]{1,2,0:T(2,128)S(1)}, u32[]{:S(2)}, u32[]{:S(2)}) collective-permute-start(f32[4,384,2]{1,2,0:T(2,128)S(1)} %get-tuple-element.20), channel_id=1, source_target_pairs={{0,1},{1,2},{2,3},{3,4},{4,5},{5,6},{6,7},{7,8},{8,9},{9,10},{10,1... | collective-permute-start | bytes 36872 | tf_op jit(solution)/shard_map/ppermute | solution.py:15
  124.9 1.9 collective-permute-start.1
  127.5 2.4 collective-permute-done.1
  129.9 4.8 %fusion.13 = f32[4,192,384]{2,1,0:T(8,128)} fusion(f32[4,384,192]{1,2,0:T(8,128)S(1)} %bitcast_divide_fusion.1, f32[4,384,2]{1,2,0:T(2,128)S(1)} %collective-permute-done.1, f32[4,384,2]{1,2,0:T(2,128)S(1)} %collective-permute-done, f32[]{:T(128)} %bitcast.28, f32[]{:T(128)} %bitcast.27, f32[]{:T(128)} %bitcast.26, f32[]{:T(128)} %bitcast.25, f32[]{:T(128)} %bitcast), kind=kLoop, calls=%fused_computation.32 | loop fusion | flops 3833856 | bytes 2383892 | tf_op jit(solution)/shard_map/transpose | solution.py:69
  135.0 43.9 %gather_fusion.1 = f32[12288,24]{1,0:T(8,128)} fusion(f32[12288,24]{1,0:T(8,128)} %bitcast.78, s32[12288]{0:T(1024)S(1)} %broadcast_clamp_fusion), kind=kCustom, calls=%fused_computation.1.clone | custom fusion | bytes 2408448 | tf_op jit(solution)/shard_map/jit(_take)/gather | solution.py:51
  178.8 4.5 %copy.12 = f32[8,1536,24]{1,2,0:T(8,128)S(1)} copy(f32[8,1536,24]{2,1,0:T(8,128)} %bitcast.79) | data formatting | bytes 2359296 | tf_op jit(solution)/shard_map/jit(_take)/gather | solution.py:51
  183.4 1.2 broadcast_select_fusion
  184.5 4.7 %all-to-all-start.1 = ((f32[8,1536,24]{1,2,0:T(8,128)}), f32[8,1536,24]{1,2,0:T(8,128)S(1)}, u32[]{:S(2)}, u32[]{:S(2)}) async-start(f32[8,1536,24]{1,2,0:T(8,128)} %broadcast_select_fusion), calls=%async_computation.1 | async-start | bytes 2359296 | tf_op jit(solution)/shard_map/all_to_all | solution.py:52
  197.2 21.1 %all-to-all-done.1 = f32[8,1536,24]{1,2,0:T(8,128)S(1)} async-done(((f32[8,1536,24]{1,2,0:T(8,128)}), f32[8,1536,24]{1,2,0:T(8,128)S(1)}, u32[]{:S(2)}, u32[]{:S(2)}) %all-to-all-start.1) | async-done | bytes 1179680 | tf_op jit(solution)/shard_map/all_to_all | solution.py:52
  219.2 2.9 collective-permute-start.2
  222.1 2.1 collective-permute-start.3
  224.2 3.7 collective-permute-done.3
  227.9 4.8 %fusion.4 = f32[4,192,384]{2,1,0:T(8,128)} fusion(f32[4,384,192]{1,2,0:T(8,128)S(1)} %bitcast_divide_fusion, f32[4,384,2]{1,2,0:T(2,128)S(1)} %collective-permute-done.3, f32[4,384,2]{1,2,0:T(2,128)S(1)} %collective-permute-done.2, f32[]{:T(128)} %bitcast.28, f32[]{:T(128)} %bitcast.27, f32[]{:T(128)} %bitcast.26, f32[]{:T(128)} %bitcast.25, f32[]{:T(128)} %bitcast), kind=kLoop, calls=%fused_computation.23 | loop fusion | flops 3833856 | bytes 2383892 | tf_op jit(solution)/shard_map/transpose | solution.py:69
  232.8 16.8 %all-gather.3.cloned.1.call-done = f32[4,3072,384]{2,1,0:T(8,128)} async-done(((f32[4,192,384]{2,1,0:T(8,128)}), f32[4,3072,384]{2,1,0:T(8,128)}) %all-gather.3.cloned.1.call-update) | async-done | bytes 18874384 | tf_op jit(solution)/shard_map/all_gather | solution.py:72
  249.6 16.5 %fusion.23 = f32[4,192,3072]{2,1,0:T(8,128)} fusion(f32[4,3072,384]{2,1,0:T(8,128)} %all-gather.3.cloned.1.call-done, f32[4,192,384]{2,1,0:T(8,128)S(1)} %copy-done, f32[4]{0:T(128)S(1)} %get-tuple-element.59), kind=kOutput, calls=%fused_computation.52 | convolution fusion | flops 5436112896 | bytes 29491216 | tf_op jit(solution)/shard_map/rfs,rgs->rfg/dot_general | solution.py:21
  266.1 13.3 %pad.17 = f32[8,192,3072]{2,1,0:T(8,128)} pad(f32[4,192,3072]{2,1,0:T(8,128)} %fusion.23, f32[]{:T(128)} %constant.34.clone.1), padding=0_4x0_0x0_0 | pad | bytes 28311556 | tf_op jit(solution)/shard_map/jit(_pad)/pad | solution.py:74
  279.4 73.9 %all-gather.5.cloned.1.call-done = f32[4,3072,384]{2,1,0:T(8,128)} async-done(((f32[4,192,384]{2,1,0:T(8,128)}), f32[4,3072,384]{2,1,0:T(8,128)}) %all-gather.5.cloned.1.call-update) | async-done | bytes 18874384 | tf_op jit(solution)/shard_map/all_gather | solution.py:72
  353.3 16.6 %convolution_dynamic-update-slice_fusion = f32[8,192,3072]{2,1,0:T(8,128)} fusion(f32[8,192,3072]{2,1,0:T(8,128)} %pad.17, f32[4,3072,384]{2,1,0:T(8,128)} %all-gather.5.cloned.1.call-done, f32[4,192,384]{2,1,0:T(8,128)S(1)} %copy-done.1, f32[4]{0:T(128)S(1)} %get-tuple-element.58), kind=kOutput, calls=%fused_computation.2 | convolution fusion | flops 5436112896 | bytes 29491216 | tf_op jit(solution)/shard_map/rfs,rgs->rfg/dot_general | solution.py:21
  (73 shorter events, 10.8 us)
Async XLA Ops:
  95.2 8.7 %copy-start.3 = (s32[64]{0:T(128)S(1)}, s32[64]{0:T(128)}, u32[]{:S(2)}) copy-start(s32[64]{0:T(128)} %param.8) | copy-start | bytes 772
  95.3 24.3 %all-to-all-start = ((f32[8,1536,24]{1,2,0:T(8,128)}), f32[8,1536,24]{1,2,0:T(8,128)S(1)}, u32[]{:S(2)}, u32[]{:S(2)}) async-start(f32[8,1536,24]{1,2,0:T(8,128)} %broadcast_select_fusion.1), calls=%async_computation | async-start | bytes 2359296 | tf_op jit(solution)/shard_map/all_to_all | solution.py:52
  103.9 145.7 %all-gather.3.cloned.1.call-start = ((), (), s32[]{:S(2)}) async-start(), calls=%async_computation.2 | async-start | bytes 20054016 | tf_op jit(solution)/shard_map/all_gather | solution.py:72
  120.3 6.6 %copy-start.2 = (f32[5]{0:T(128)S(1)}, f32[5]{0:T(128)}, u32[]{:S(2)}) copy-start(f32[5]{0:T(128)} %param.9) | copy-start | bytes 64
  120.5 7.0 %collective-permute-start = (f32[4,384,2]{1,2,0:T(2,128)S(1)}, f32[4,384,2]{1,2,0:T(2,128)S(1)}, u32[]{:S(2)}, u32[]{:S(2)}) collective-permute-start(f32[4,384,2]{1,2,0:T(2,128)S(1)} %get-tuple-element.20), channel_id=1, source_target_pairs={{0,1},{1,2},{2,3},{3,4},{4,5},{5,6},{6,7},{7,8},{8,9},{9,10},{10,1... | collective-permute-start | bytes 36872 | tf_op jit(solution)/shard_map/ppermute | solution.py:15
  124.9 5.0 %collective-permute-start.1 = (f32[4,384,2]{1,2,0:T(2,128)S(1)}, f32[4,384,2]{1,2,0:T(2,128)S(1)}, u32[]{:S(2)}, u32[]{:S(2)}) collective-permute-start(f32[4,384,2]{1,2,0:T(2,128)S(1)} %get-tuple-element.21), channel_id=1, source_target_pairs={{1,0},{2,1},{3,2},{4,3},{5,4},{6,5},{7,6},{8,7},{9,8},{10,9},{11,1... | collective-permute-start | bytes 36872 | tf_op jit(solution)/shard_map/ppermute | solution.py:16
  184.5 33.7 %all-to-all-start.1 = ((f32[8,1536,24]{1,2,0:T(8,128)}), f32[8,1536,24]{1,2,0:T(8,128)S(1)}, u32[]{:S(2)}, u32[]{:S(2)}) async-start(f32[8,1536,24]{1,2,0:T(8,128)} %broadcast_select_fusion), calls=%async_computation.1 | async-start | bytes 2359296 | tf_op jit(solution)/shard_map/all_to_all | solution.py:52
  189.2 164.1 %all-gather.5.cloned.1.call-start = ((), (), s32[]{:S(2)}) async-start(), calls=%async_computation.3 | async-start | bytes 20054016 | tf_op jit(solution)/shard_map/all_gather | solution.py:72
  219.2 5.0 %collective-permute-start.2 = (f32[4,384,2]{1,2,0:T(2,128)S(1)}, f32[4,384,2]{1,2,0:T(2,128)S(1)}, u32[]{:S(2)}, u32[]{:S(2)}) collective-permute-start(f32[4,384,2]{1,2,0:T(2,128)S(1)} %get-tuple-element.14), channel_id=1, source_target_pairs={{0,1},{1,2},{2,3},{3,4},{4,5},{5,6},{6,7},{7,8},{8,9},{9,10},{10,1... | collective-permute-start | bytes 36872 | tf_op jit(solution)/shard_map/ppermute | solution.py:15
  222.1 5.8 %collective-permute-start.3 = (f32[4,384,2]{1,2,0:T(2,128)S(1)}, f32[4,384,2]{1,2,0:T(2,128)S(1)}, u32[]{:S(2)}, u32[]{:S(2)}) collective-permute-start(f32[4,384,2]{1,2,0:T(2,128)S(1)} %get-tuple-element.15), channel_id=1, source_target_pairs={{1,0},{2,1},{3,2},{4,3},{5,4},{6,5},{7,6},{8,7},{9,8},{10,9},{11,1... | collective-permute-start | bytes 36872 | tf_op jit(solution)/shard_map/ppermute | solution.py:16
  232.7 16.8 %copy-start = (f32[4,192,384]{2,1,0:T(8,128)S(1)}, f32[4,192,384]{2,1,0:T(8,128)}, u32[]{:S(2)}) copy-start(f32[4,192,384]{2,1,0:T(8,128)} %fusion.13) | copy-start | bytes 3538948
  266.1 87.2 %copy-start.1 = (f32[4,192,384]{2,1,0:T(8,128)S(1)}, f32[4,192,384]{2,1,0:T(8,128)}, u32[]{:S(2)}) copy-start(f32[4,192,384]{2,1,0:T(8,128)} %fusion.4) | copy-start | bytes 3538948
Sparse Core Ops, SparseCore 0:
  134.8 114.6 all-gather.2
  251.2 102.0 all-gather.4

commit v10 on v9

--- a/solution.py
+++ b/solution.py
@@ -40,19 +40,26 @@
     sizes = lax.dynamic_index_in_dim(cycle_sizes.reshape(groups, owned), me, 0, keepdims=False)
     slots = jnp.arange(cap, dtype=jnp.int32)
 
-    order = jnp.pad(pixel_order, (0, window))
+    lanes = 128
+    span = window + lanes
+    count = pixels // lanes + span // lanes
+    order = jnp.pad(pixel_order, (0, count * lanes - pixels)).reshape(count, lanes).astype(jnp.float32)
+    aligned = (sends // lanes) * lanes
+    rows = (aligned // lanes)[:, :, None] + jnp.arange(span // lanes, dtype=jnp.int32)
+    pick_rows = (rows[..., None] == jnp.arange(count, dtype=jnp.int32)).astype(jnp.float32)
+    windows = jnp.einsum(
+        "dprk,kl->pdrl", pick_rows, order, precision=lax.Precision.HIGHEST, preferred_element_type=jnp.float32
+    )
+    windows = windows.astype(jnp.int32).reshape(PARTS, groups * span)
     series = block.T
 
     outs = []
     for part in range(PARTS):
-        wanted = jnp.stack(
-            [lax.dynamic_slice_in_dim(order, sends[d, part], window, 0) for d in range(groups)]
-        )
-        chunks = jnp.take(series, wanted, axis=0)
+        chunks = jnp.take(series, windows[part], axis=0).reshape(groups, span, sub)
         got = lax.all_to_all(chunks, "pix", 0, 0, tiled=True)
         got = jnp.pad(got, ((0, 0), (0, cap), (0, 0)))
         first = part * step
-        offsets = mine[first : first + step] - mine[first]
+        offsets = mine[first : first + step] - (mine[first] // lanes) * lanes
         masks = slots[None, :] < sizes[first : first + step, None]
         picked = []
         for l in range(step):

time: 378 us -> 363 us (0.960)
  between operations: 58.2 us -> 33.9 us
  other arithmetic: 16 us -> 35.5 us
  waiting for transfers between devices: 123 us -> 105 us
  local copies, waits for them, and re-layouts: 121 us -> 128 us
    select_n x4 -> x3, other arithmetic: 2.33 us -> 23 us  [the longest x2 22.9 us: per_device(): chunks = jnp.take(series, windows[part], axis=0).reshape(groups, span, sub)]
    all_gather x2, waiting for transfers between devices: 90.7 us -> 74.3 us  [per_device(): right = lax.all_gather(smooth, 'tm', axis=1, tiled=True)]
    reshape x0 -> x2, local copies, waits for them, and re-layouts: none -> 11.3 us  [per_device(): chunks = jnp.take(series, windows[part], axis=0).reshape(groups, span, sub)]
    gather x4 -> x2, local copies, waits for them, and re-layouts: 96.5 us -> 94.9 us  [per_device(): chunks = jnp.take(series, windows[part], axis=0).reshape(groups, span, sub)]
  transfers between devices with their start and end apart: 8 -> 8, of which waited for: 6 -> 6; matrix products, arithmetic and copies ran while one was open for 24% -> 29% of each run, Pallas kernels for 0% -> 0%
where the time goes in v10:
time: 363 us; the launch traced here: 362 us
  local copies, waits for them, and re-layouts  128 us (35%)
  waiting for transfers between devices  105 us (29%)
  other arithmetic  35.5 us (10%)
  matrix products  34.2 us (9%)
  between operations  33.9 us (9%)
  starting transfers between devices  24.6 us (7%)
    gather x2, local copies, waits for them, and re-layouts, per_device(): chunks = jnp.take(series, windows[part], axis=0).reshape(groups, span, sub)  94.9 us
    all_gather x2, waiting for transfers between devices, per_device(): right = lax.all_gather(smooth, 'tm', axis=1, tiled=True)  74.3 us
    dot_general x2, matrix products, correlate(): jnp.einsum('rfs,rgs->rfg', left, right, precision=lax.Precision.HIGH, pre...  33.1 us
    all_to_all x2, waiting for transfers between devices, per_device(): got = lax.all_to_all(chunks, 'pix', 0, 0, tiled=True)  25.1 us
    select_n x2, other arithmetic, per_device(): chunks = jnp.take(series, windows[part], axis=0).reshape(groups, span, sub)  22.9 us
    pad x1, local copies, waits for them, and re-layouts, per_device(): jnp.pad(jnp.concatenate(outs[:-1], 0), ((0, step), (0, 0), (0, 0)))  13.4 us
    all_to_all x2, starting transfers between devices, per_device(): got = lax.all_to_all(chunks, 'pix', 0, 0, tiled=True)  13.2 us
    reshape x2, local copies, waits for them, and re-layouts, per_device(): chunks = jnp.take(series, windows[part], axis=0).reshape(groups, span, sub)  11.3 us
  transfers between devices with their start and end apart: 8, of which 6 were waited for; matrix products, arithmetic and copies ran while one was open for 29% of the time, Pallas kernels for 0%

profile of v10, /device:TPU:1, one launch (start us, length us, event | category | flops | bytes accessed | tf_op | source)
XLA Modules:
  0.0 361.6 jit_solution(6967036540668736226)
XLA Ops:
  8.5 1.1 fusion.25
  9.7 3.9 %copy.10 = f32[1,24,12288]{1,2,0:T(8,128)} copy(f32[1,24,12288]{2,1,0:T(8,128)S(1)} %copy-done.2) | data formatting | bytes 2359296 | tf_op args[0]
  13.6 47.5 %gather_fusion = f32[13312,24]{1,0:T(8,128)} fusion(f32[12288,24]{1,0:T(8,128)} %bitcast.74, s32[13312]{0:T(1024)S(1)} %fusion.48), kind=kCustom, calls=%fused_computation.clone | custom fusion | bytes 2609152 | tf_op jit(solution)/shard_map/jit(_take)/gather | solution.py:58
  61.1 11.4 %broadcast_select_fusion.1 = f32[13312,24]{1,0:T(8,128)} fusion(f32[13312,24]{1,0:T(8,128)} %gather_fusion, pred[13312]{0:T(1024)(128)(4,1)S(1)} %compare_and_fusion.1), kind=kLoop, calls=%fused_computation.4 | loop fusion | flops 319488 | bytes 2569216 | tf_op jit(solution)/shard_map/jit(_take)/select_n | solution.py:58
  72.5 5.5 %copy.11 = f32[8,1664,24]{1,2,0:T(8,128)} copy(f32[8,1664,24]{2,1,0:T(8,128)} %bitcast.76) | data formatting | bytes 2555904 | tf_op jit(solution)/shard_map/reshape | solution.py:58
  78.0 8.6 %all-to-all-start = ((f32[8,1664,24]{1,2,0:T(8,128)}), f32[8,1664,24]{1,2,0:T(8,128)S(1)}, u32[]{:S(2)}, u32[]{:S(2)}) async-start(f32[8,1664,24]{1,2,0:T(8,128)} %copy.11), calls=%async_computation | async-start | bytes 2555904 | tf_op jit(solution)/shard_map/all_to_all | solution.py:59
  100.8 2.5 all-to-all-done
  104.3 4.3 %collective-permute-start = (f32[4,384,2]{1,2,0:T(2,128)S(1)}, f32[4,384,2]{1,2,0:T(2,128)S(1)}, u32[]{:S(2)}, u32[]{:S(2)}) collective-permute-start(f32[4,384,2]{1,2,0:T(2,128)S(1)} %get-tuple-element.24), channel_id=1, source_target_pairs={{0,1},{1,2},{2,3},{3,4},{4,5},{5,6},{6,7},{7,8},{8,9},{9,10},{10,1... | collective-permute-start | bytes 36872 | tf_op jit(solution)/shard_map/ppermute | solution.py:15
  108.6 1.9 collective-permute-start.1
  111.2 2.4 collective-permute-done.1
  113.6 4.8 %fusion.13 = f32[4,192,384]{2,1,0:T(8,128)} fusion(f32[4,384,192]{1,2,0:T(8,128)S(1)} %bitcast_divide_fusion.1, f32[4,384,2]{1,2,0:T(2,128)S(1)} %collective-permute-done.1, f32[4,384,2]{1,2,0:T(2,128)S(1)} %collective-permute-done, f32[]{:T(128)} %bitcast.24, f32[]{:T(128)} %bitcast.23, f32[]{:T(128)} %bitcast.22, f32[]{:T(128)} %bitcast.21, f32[]{:T(128)} %bitcast), kind=kLoop, calls=%fused_computation.34 | loop fusion | flops 3833856 | bytes 2383892 | tf_op jit(solution)/shard_map/transpose | solution.py:76
  118.5 47.5 %gather_fusion.1 = f32[13312,24]{1,0:T(8,128)} fusion(f32[12288,24]{1,0:T(8,128)} %bitcast.75, s32[13312]{0:T(1024)S(1)} %fusion.49), kind=kCustom, calls=%fused_computation.1.clone | custom fusion | bytes 2609152 | tf_op jit(solution)/shard_map/jit(_take)/gather | solution.py:58
  166.0 11.5 %broadcast_select_fusion = f32[13312,24]{1,0:T(8,128)} fusion(f32[13312,24]{1,0:T(8,128)} %gather_fusion.1, pred[13312]{0:T(1024)(128)(4,1)S(1)} %compare_and_fusion), kind=kLoop, calls=%fused_computation.3 | loop fusion | flops 319488 | bytes 2569216 | tf_op jit(solution)/shard_map/jit(_take)/select_n | solution.py:58
  177.5 5.8 %copy.12 = f32[8,1664,24]{1,2,0:T(8,128)} copy(f32[8,1664,24]{2,1,0:T(8,128)} %bitcast.77) | data formatting | bytes 2555904 | tf_op jit(solution)/shard_map/reshape | solution.py:58
  183.3 4.6 %all-to-all-start.1 = ((f32[8,1664,24]{1,2,0:T(8,128)}), f32[8,1664,24]{1,2,0:T(8,128)S(1)}, u32[]{:S(2)}, u32[]{:S(2)}) async-start(f32[8,1664,24]{1,2,0:T(8,128)} %copy.12), calls=%async_computation.1 | async-start | bytes 2555904 | tf_op jit(solution)/shard_map/all_to_all | solution.py:59
  196.5 22.5 %all-to-all-done.1 = f32[8,1664,24]{1,2,0:T(8,128)S(1)} async-done(((f32[8,1664,24]{1,2,0:T(8,128)}), f32[8,1664,24]{1,2,0:T(8,128)S(1)}, u32[]{:S(2)}, u32[]{:S(2)}) %all-to-all-start.1) | async-done | bytes 1277984 | tf_op jit(solution)/shard_map/all_to_all | solution.py:59
  220.0 2.9 collective-permute-start.2
  222.9 2.1 collective-permute-start.3
  225.1 3.7 %collective-permute-done.3 = f32[4,384,2]{1,2,0:T(2,128)S(1)} collective-permute-done((f32[4,384,2]{1,2,0:T(2,128)S(1)}, f32[4,384,2]{1,2,0:T(2,128)S(1)}, u32[]{:S(2)}, u32[]{:S(2)}) %collective-permute-start.3) | collective-permute-done | bytes 12320 | tf_op jit(solution)/shard_map/ppermute | solution.py:16
  228.7 4.8 %fusion.4 = f32[4,192,384]{2,1,0:T(8,128)} fusion(f32[4,384,192]{1,2,0:T(8,128)S(1)} %bitcast_divide_fusion, f32[4,384,2]{1,2,0:T(2,128)S(1)} %collective-permute-done.3, f32[4,384,2]{1,2,0:T(2,128)S(1)} %collective-permute-done.2, f32[]{:T(128)} %bitcast.24, f32[]{:T(128)} %bitcast.23, f32[]{:T(128)} %bitcast.22, f32[]{:T(128)} %bitcast.21, f32[]{:T(128)} %bitcast), kind=kLoop, calls=%fused_computation.25 | loop fusion | flops 3833856 | bytes 2383892 | tf_op jit(solution)/shard_map/transpose | solution.py:76
  234.8 16.5 %fusion.23 = f32[4,192,3072]{2,1,0:T(8,128)} fusion(f32[4,3072,384]{2,1,0:T(8,128)} %all-gather.3.cloned.1.call-done, f32[4,192,384]{2,1,0:T(8,128)S(1)} %copy-done, f32[4]{0:T(128)S(1)} %get-tuple-element.29), kind=kOutput, calls=%fused_computation.54 | convolution fusion | flops 5436112896 | bytes 29491216 | tf_op jit(solution)/shard_map/rfs,rgs->rfg/dot_general | solution.py:21
  251.4 13.4 %pad.17 = f32[8,192,3072]{2,1,0:T(8,128)} pad(f32[4,192,3072]{2,1,0:T(8,128)} %fusion.23, f32[]{:T(128)} %constant.72.clone.1), padding=0_4x0_0x0_0 | pad | bytes 28311556 | tf_op jit(solution)/shard_map/jit(_pad)/pad | solution.py:81
  264.7 73.4 %all-gather.5.cloned.1.call-done = f32[4,3072,384]{2,1,0:T(8,128)} async-done(((f32[4,192,384]{2,1,0:T(8,128)}), f32[4,3072,384]{2,1,0:T(8,128)}) %all-gather.5.cloned.1.call-update) | async-done | bytes 18874384 | tf_op jit(solution)/shard_map/all_gather | solution.py:79
  338.2 16.6 %convolution_dynamic-update-slice_fusion = f32[8,192,3072]{2,1,0:T(8,128)} fusion(f32[8,192,3072]{2,1,0:T(8,128)} %pad.17, f32[4,3072,384]{2,1,0:T(8,128)} %all-gather.5.cloned.1.call-done, f32[4,192,384]{2,1,0:T(8,128)S(1)} %copy-done.1, f32[4]{0:T(128)S(1)} %get-tuple-element.28), kind=kOutput, calls=%fused_computation.2 | convolution fusion | flops 5436112896 | bytes 29491216 | tf_op jit(solution)/shard_map/rfs,rgs->rfg/dot_general | solution.py:21
  (56 shorter events, 8.3 us)
Async XLA Ops:
  6.5 3.1 copy-start.2
  78.0 8.7 %copy-start.4 = (s32[64]{0:T(128)S(1)}, s32[64]{0:T(128)}, u32[]{:S(2)}) copy-start(s32[64]{0:T(128)} %param.8) | copy-start | bytes 772
  78.0 25.3 %all-to-all-start = ((f32[8,1664,24]{1,2,0:T(8,128)}), f32[8,1664,24]{1,2,0:T(8,128)S(1)}, u32[]{:S(2)}, u32[]{:S(2)}) async-start(f32[8,1664,24]{1,2,0:T(8,128)} %copy.11), calls=%async_computation | async-start | bytes 2555904 | tf_op jit(solution)/shard_map/all_to_all | solution.py:59
  86.6 147.8 %all-gather.3.cloned.1.call-start = ((), (), s32[]{:S(2)}) async-start(), calls=%async_computation.2 | async-start | bytes 20054016 | tf_op jit(solution)/shard_map/all_gather | solution.py:79
  104.1 6.5 %copy-start.3 = (f32[5]{0:T(128)S(1)}, f32[5]{0:T(128)}, u32[]{:S(2)}) copy-start(f32[5]{0:T(128)} %param.9) | copy-start | bytes 64
  104.3 6.9 %collective-permute-start = (f32[4,384,2]{1,2,0:T(2,128)S(1)}, f32[4,384,2]{1,2,0:T(2,128)S(1)}, u32[]{:S(2)}, u32[]{:S(2)}) collective-permute-start(f32[4,384,2]{1,2,0:T(2,128)S(1)} %get-tuple-element.24), channel_id=1, source_target_pairs={{0,1},{1,2},{2,3},{3,4},{4,5},{5,6},{6,7},{7,8},{8,9},{9,10},{10,1... | collective-permute-start | bytes 36872 | tf_op jit(solution)/shard_map/ppermute | solution.py:15
  108.6 5.0 %collective-permute-start.1 = (f32[4,384,2]{1,2,0:T(2,128)S(1)}, f32[4,384,2]{1,2,0:T(2,128)S(1)}, u32[]{:S(2)}, u32[]{:S(2)}) collective-permute-start(f32[4,384,2]{1,2,0:T(2,128)S(1)} %get-tuple-element.25), channel_id=1, source_target_pairs={{1,0},{2,1},{3,2},{4,3},{5,4},{6,5},{7,6},{8,7},{9,8},{10,9},{11,1... | collective-permute-start | bytes 36872 | tf_op jit(solution)/shard_map/ppermute | solution.py:16
  183.3 35.8 %all-to-all-start.1 = ((f32[8,1664,24]{1,2,0:T(8,128)}), f32[8,1664,24]{1,2,0:T(8,128)S(1)}, u32[]{:S(2)}, u32[]{:S(2)}) async-start(f32[8,1664,24]{1,2,0:T(8,128)} %copy.12), calls=%async_computation.1 | async-start | bytes 2555904 | tf_op jit(solution)/shard_map/all_to_all | solution.py:59
  187.9 150.3 %all-gather.5.cloned.1.call-start = ((), (), s32[]{:S(2)}) async-start(), calls=%async_computation.3 | async-start | bytes 20054016 | tf_op jit(solution)/shard_map/all_gather | solution.py:79
  220.0 5.0 %collective-permute-start.2 = (f32[4,384,2]{1,2,0:T(2,128)S(1)}, f32[4,384,2]{1,2,0:T(2,128)S(1)}, u32[]{:S(2)}, u32[]{:S(2)}) collective-permute-start(f32[4,384,2]{1,2,0:T(2,128)S(1)} %get-tuple-element.22), channel_id=1, source_target_pairs={{0,1},{1,2},{2,3},{3,4},{4,5},{5,6},{6,7},{7,8},{8,9},{9,10},{10,1... | collective-permute-start | bytes 36872 | tf_op jit(solution)/shard_map/ppermute | solution.py:15
  222.9 5.8 %collective-permute-start.3 = (f32[4,384,2]{1,2,0:T(2,128)S(1)}, f32[4,384,2]{1,2,0:T(2,128)S(1)}, u32[]{:S(2)}, u32[]{:S(2)}) collective-permute-start(f32[4,384,2]{1,2,0:T(2,128)S(1)} %get-tuple-element.23), channel_id=1, source_target_pairs={{1,0},{2,1},{3,2},{4,3},{5,4},{6,5},{7,6},{8,7},{9,8},{10,9},{11,1... | collective-permute-start | bytes 36872 | tf_op jit(solution)/shard_map/ppermute | solution.py:16
  233.6 1.3 copy-start
  251.4 86.8 %copy-start.1 = (f32[4,192,384]{2,1,0:T(8,128)S(1)}, f32[4,192,384]{2,1,0:T(8,128)}, u32[]{:S(2)}) copy-start(f32[4,192,384]{2,1,0:T(8,128)} %fusion.4) | copy-start | bytes 3538948
Sparse Core Ops, SparseCore 0:
  118.6 115.8 all-gather.2
  236.1 102.0 all-gather.4

commit v11 on v10

--- a/solution.py
+++ b/solution.py
@@ -55,7 +55,7 @@
 
     outs = []
     for part in range(PARTS):
-        chunks = jnp.take(series, windows[part], axis=0).reshape(groups, span, sub)
+        chunks = series.at[windows[part]].get(mode="promise_in_bounds").reshape(groups, span, sub)
         got = lax.all_to_all(chunks, "pix", 0, 0, tiled=True)
         got = jnp.pad(got, ((0, 0), (0, cap), (0, 0)))
         first = part * step

time: 363 us -> 351 us (0.967)
  other arithmetic: 35.5 us -> 12.7 us
  waiting for transfers between devices: 105 us -> 117 us
    select_n x2, other arithmetic: 22.9 us -> 0.11 us  [per_device(): series.at[windows[part]].get(mode='promise_in_bounds')]
    all_gather x2, waiting for transfers between devices: 74.3 us -> 86.3 us  [per_device(): right = lax.all_gather(smooth, 'tm', axis=1, tiled=True)]
  transfers between devices with their start and end apart: 8 -> 8, of which waited for: 6 -> 6; matrix products, arithmetic and copies ran while one was open for 29% -> 26% of each run, Pallas kernels for 0% -> 0%
where the time goes in v11:
time: 351 us; the launch traced here: 350 us
  local copies, waits for them, and re-layouts  127 us (36%)
  waiting for transfers between devices  117 us (33%)
  matrix products  34.2 us (10%)
  between operations  33.9 us (10%)
  starting transfers between devices  24.7 us (7%)
  other arithmetic  12.7 us (4%)
    gather x2, local copies, waits for them, and re-layouts, per_device(): series.at[windows[part]].get(mode='promise_in_bounds')  94.9 us
    all_gather x2, waiting for transfers between devices, per_device(): right = lax.all_gather(smooth, 'tm', axis=1, tiled=True)  86.3 us
    dot_general x2, matrix products, correlate(): jnp.einsum('rfs,rgs->rfg', left, right, precision=lax.Precision.HIGH, pre...  33.1 us
    all_to_all x2, waiting for transfers between devices, per_device(): got = lax.all_to_all(chunks, 'pix', 0, 0, tiled=True)  25.1 us
    all_to_all x2, starting transfers between devices, per_device(): got = lax.all_to_all(chunks, 'pix', 0, 0, tiled=True)  13.6 us
    pad x1, local copies, waits for them, and re-layouts, per_device(): jnp.pad(jnp.concatenate(outs[:-1], 0), ((0, step), (0, 0), (0, 0)))  13.3 us
    reshape x2, local copies, waits for them, and re-layouts, per_device(): series.at[windows[part]].get(mode='promise_in_bounds')  11.1 us
    transpose x2, other arithmetic, per_device(): smooth = jnp.swapaxes(smooth, 1, 2)  9.62 us
  transfers between devices with their start and end apart: 8, of which 6 were waited for; matrix products, arithmetic and copies ran while one was open for 26% of the time, Pallas kernels for 0%

profile of v11, /device:TPU:1, one launch (start us, length us, event | category | flops | bytes accessed | tf_op | source)
XLA Modules:
  0.0 350.3 jit_solution(16429635653975175881)
XLA Ops:
  6.5 0.8 copy.10
  8.5 1.1 fusion.25
  9.8 3.9 %copy.9 = f32[1,24,12288]{1,2,0:T(8,128)} copy(f32[1,24,12288]{2,1,0:T(8,128)S(1)} %copy-done.2) | data formatting | bytes 2359296 | tf_op args[0]
  13.7 47.5 %gather_fusion = f32[13312,24]{1,0:T(8,128)} fusion(f32[12288,24]{1,0:T(8,128)} %bitcast.76, s32[13312]{0:T(1024)S(1)} %broadcast_clamp_fusion.1), kind=kCustom, calls=%fused_computation | custom fusion | bytes 2609152 | tf_op jit(solution)/shard_map/gather | solution.py:58
  61.2 5.5 %copy.11 = f32[8,1664,24]{1,2,0:T(8,128)} copy(f32[8,1664,24]{2,1,0:T(8,128)} %bitcast.79) | data formatting | bytes 2555904 | tf_op jit(solution)/shard_map/reshape | solution.py:58
  66.7 8.6 %all-to-all-start = ((f32[8,1664,24]{1,2,0:T(8,128)}), f32[8,1664,24]{1,2,0:T(8,128)S(1)}, u32[]{:S(2)}, u32[]{:S(2)}) async-start(f32[8,1664,24]{1,2,0:T(8,128)} %copy.11), calls=%async_computation | async-start | bytes 2555904 | tf_op jit(solution)/shard_map/all_to_all | solution.py:59
  89.5 2.5 all-to-all-done
  92.9 4.3 %collective-permute-start = (f32[4,384,2]{1,2,0:T(2,128)S(1)}, f32[4,384,2]{1,2,0:T(2,128)S(1)}, u32[]{:S(2)}, u32[]{:S(2)}) collective-permute-start(f32[4,384,2]{1,2,0:T(2,128)S(1)} %get-tuple-element.23), channel_id=1, source_target_pairs={{0,1},{1,2},{2,3},{3,4},{4,5},{5,6},{6,7},{7,8},{8,9},{9,10},{10,1... | collective-permute-start | bytes 36872 | tf_op jit(solution)/shard_map/ppermute | solution.py:15
  97.3 1.9 collective-permute-start.1
  99.9 2.4 collective-permute-done.1
  102.3 4.8 %fusion.13 = f32[4,192,384]{2,1,0:T(8,128)} fusion(f32[4,384,192]{1,2,0:T(8,128)S(1)} %bitcast_divide_fusion.1, f32[4,384,2]{1,2,0:T(2,128)S(1)} %collective-permute-done.1, f32[4,384,2]{1,2,0:T(2,128)S(1)} %collective-permute-done, f32[]{:T(128)} %bitcast.25, f32[]{:T(128)} %bitcast.24, f32[]{:T(128)} %bitcast.23, f32[]{:T(128)} %bitcast.22, f32[]{:T(128)} %bitcast), kind=kLoop, calls=%fused_computation.32 | loop fusion | flops 3833856 | bytes 2383892 | tf_op jit(solution)/shard_map/transpose | solution.py:76
  107.3 47.5 %gather_fusion.1 = f32[13312,24]{1,0:T(8,128)} fusion(f32[12288,24]{1,0:T(8,128)} %bitcast.77, s32[13312]{0:T(1024)S(1)} %broadcast_clamp_fusion), kind=kCustom, calls=%fused_computation.1 | custom fusion | bytes 2609152 | tf_op jit(solution)/shard_map/gather | solution.py:58
  154.7 5.6 %copy.12 = f32[8,1664,24]{1,2,0:T(8,128)} copy(f32[8,1664,24]{2,1,0:T(8,128)} %bitcast.78) | data formatting | bytes 2555904 | tf_op jit(solution)/shard_map/reshape | solution.py:58
  160.3 5.0 %all-to-all-start.1 = ((f32[8,1664,24]{1,2,0:T(8,128)}), f32[8,1664,24]{1,2,0:T(8,128)S(1)}, u32[]{:S(2)}, u32[]{:S(2)}) async-start(f32[8,1664,24]{1,2,0:T(8,128)} %copy.12), calls=%async_computation.1 | async-start | bytes 2555904 | tf_op jit(solution)/shard_map/all_to_all | solution.py:59
  173.9 22.5 %all-to-all-done.1 = f32[8,1664,24]{1,2,0:T(8,128)S(1)} async-done(((f32[8,1664,24]{1,2,0:T(8,128)}), f32[8,1664,24]{1,2,0:T(8,128)S(1)}, u32[]{:S(2)}, u32[]{:S(2)}) %all-to-all-start.1) | async-done | bytes 1277984 | tf_op jit(solution)/shard_map/all_to_all | solution.py:59
  197.4 2.7 collective-permute-start.2
  200.1 2.1 collective-permute-start.3
  202.2 3.7 %collective-permute-done.3 = f32[4,384,2]{1,2,0:T(2,128)S(1)} collective-permute-done((f32[4,384,2]{1,2,0:T(2,128)S(1)}, f32[4,384,2]{1,2,0:T(2,128)S(1)}, u32[]{:S(2)}, u32[]{:S(2)}) %collective-permute-start.3) | collective-permute-done | bytes 12320 | tf_op jit(solution)/shard_map/ppermute | solution.py:16
  205.9 4.8 %fusion.4 = f32[4,192,384]{2,1,0:T(8,128)} fusion(f32[4,384,192]{1,2,0:T(8,128)S(1)} %bitcast_divide_fusion, f32[4,384,2]{1,2,0:T(2,128)S(1)} %collective-permute-done.3, f32[4,384,2]{1,2,0:T(2,128)S(1)} %collective-permute-done.2, f32[]{:T(128)} %bitcast.25, f32[]{:T(128)} %bitcast.24, f32[]{:T(128)} %bitcast.23, f32[]{:T(128)} %bitcast.22, f32[]{:T(128)} %bitcast), kind=kLoop, calls=%fused_computation.23 | loop fusion | flops 3833856 | bytes 2383892 | tf_op jit(solution)/shard_map/transpose | solution.py:76
  210.7 12.4 %all-gather.3.cloned.1.call-done = f32[4,3072,384]{2,1,0:T(8,128)} async-done(((f32[4,192,384]{2,1,0:T(8,128)}), f32[4,3072,384]{2,1,0:T(8,128)}) %all-gather.3.cloned.1.call-update) | async-done | bytes 18874384 | tf_op jit(solution)/shard_map/all_gather | solution.py:79
  223.1 16.5 %fusion.23 = f32[4,192,3072]{2,1,0:T(8,128)} fusion(f32[4,3072,384]{2,1,0:T(8,128)} %all-gather.3.cloned.1.call-done, f32[4,192,384]{2,1,0:T(8,128)S(1)} %copy-done, f32[4]{0:T(128)S(1)} %get-tuple-element.28), kind=kOutput, calls=%fused_computation.52 | convolution fusion | flops 5436112896 | bytes 29491216 | tf_op jit(solution)/shard_map/rfs,rgs->rfg/dot_general | solution.py:21
  239.6 13.3 %pad.17 = f32[8,192,3072]{2,1,0:T(8,128)} pad(f32[4,192,3072]{2,1,0:T(8,128)} %fusion.23, f32[]{:T(128)} %constant.65.clone.1), padding=0_4x0_0x0_0 | pad | bytes 28311556 | tf_op jit(solution)/shard_map/jit(_pad)/pad | solution.py:81
  252.9 73.9 %all-gather.5.cloned.1.call-done = f32[4,3072,384]{2,1,0:T(8,128)} async-done(((f32[4,192,384]{2,1,0:T(8,128)}), f32[4,3072,384]{2,1,0:T(8,128)}) %all-gather.5.cloned.1.call-update) | async-done | bytes 18874384 | tf_op jit(solution)/shard_map/all_gather | solution.py:79
  326.8 16.6 %convolution_dynamic-update-slice_fusion = f32[8,192,3072]{2,1,0:T(8,128)} fusion(f32[8,192,3072]{2,1,0:T(8,128)} %pad.17, f32[4,3072,384]{2,1,0:T(8,128)} %all-gather.5.cloned.1.call-done, f32[4,192,384]{2,1,0:T(8,128)S(1)} %copy-done.1, f32[4]{0:T(128)S(1)} %get-tuple-element.27), kind=kOutput, calls=%fused_computation.2 | convolution fusion | flops 5436112896 | bytes 29491216 | tf_op jit(solution)/shard_map/rfs,rgs->rfg/dot_general | solution.py:21
  (54 shorter events, 6.4 us)
Async XLA Ops:
  6.5 3.2 copy-start.2
  66.7 8.7 %copy-start.4 = (s32[64]{0:T(128)S(1)}, s32[64]{0:T(128)}, u32[]{:S(2)}) copy-start(s32[64]{0:T(128)} %param.6) | copy-start | bytes 772
  66.7 25.3 %all-to-all-start = ((f32[8,1664,24]{1,2,0:T(8,128)}), f32[8,1664,24]{1,2,0:T(8,128)S(1)}, u32[]{:S(2)}, u32[]{:S(2)}) async-start(f32[8,1664,24]{1,2,0:T(8,128)} %copy.11), calls=%async_computation | async-start | bytes 2555904 | tf_op jit(solution)/shard_map/all_to_all | solution.py:59
  75.3 147.8 %all-gather.3.cloned.1.call-start = ((), (), s32[]{:S(2)}) async-start(), calls=%async_computation.2 | async-start | bytes 20054016 | tf_op jit(solution)/shard_map/all_gather | solution.py:79
  92.7 6.5 %copy-start.3 = (f32[5]{0:T(128)S(1)}, f32[5]{0:T(128)}, u32[]{:S(2)}) copy-start(f32[5]{0:T(128)} %param.7) | copy-start | bytes 64
  92.9 6.9 %collective-permute-start = (f32[4,384,2]{1,2,0:T(2,128)S(1)}, f32[4,384,2]{1,2,0:T(2,128)S(1)}, u32[]{:S(2)}, u32[]{:S(2)}) collective-permute-start(f32[4,384,2]{1,2,0:T(2,128)S(1)} %get-tuple-element.23), channel_id=1, source_target_pairs={{0,1},{1,2},{2,3},{3,4},{4,5},{5,6},{6,7},{7,8},{8,9},{9,10},{10,1... | collective-permute-start | bytes 36872 | tf_op jit(solution)/shard_map/ppermute | solution.py:15
  97.3 5.0 %collective-permute-start.1 = (f32[4,384,2]{1,2,0:T(2,128)S(1)}, f32[4,384,2]{1,2,0:T(2,128)S(1)}, u32[]{:S(2)}, u32[]{:S(2)}) collective-permute-start(f32[4,384,2]{1,2,0:T(2,128)S(1)} %get-tuple-element.24), channel_id=1, source_target_pairs={{1,0},{2,1},{3,2},{4,3},{5,4},{6,5},{7,6},{8,7},{9,8},{10,9},{11,1... | collective-permute-start | bytes 36872 | tf_op jit(solution)/shard_map/ppermute | solution.py:16
  160.3 36.1 %all-to-all-start.1 = ((f32[8,1664,24]{1,2,0:T(8,128)}), f32[8,1664,24]{1,2,0:T(8,128)S(1)}, u32[]{:S(2)}, u32[]{:S(2)}) async-start(f32[8,1664,24]{1,2,0:T(8,128)} %copy.12), calls=%async_computation.1 | async-start | bytes 2555904 | tf_op jit(solution)/shard_map/all_to_all | solution.py:59
  165.3 161.5 %all-gather.5.cloned.1.call-start = ((), (), s32[]{:S(2)}) async-start(), calls=%async_computation.3 | async-start | bytes 20054016 | tf_op jit(solution)/shard_map/all_gather | solution.py:79
  197.4 4.8 %collective-permute-start.2 = (f32[4,384,2]{1,2,0:T(2,128)S(1)}, f32[4,384,2]{1,2,0:T(2,128)S(1)}, u32[]{:S(2)}, u32[]{:S(2)}) collective-permute-start(f32[4,384,2]{1,2,0:T(2,128)S(1)} %get-tuple-element.21), channel_id=1, source_target_pairs={{0,1},{1,2},{2,3},{3,4},{4,5},{5,6},{6,7},{7,8},{8,9},{9,10},{10,1... | collective-permute-start | bytes 36872 | tf_op jit(solution)/shard_map/ppermute | solution.py:15
  200.1 5.8 %collective-permute-start.3 = (f32[4,384,2]{1,2,0:T(2,128)S(1)}, f32[4,384,2]{1,2,0:T(2,128)S(1)}, u32[]{:S(2)}, u32[]{:S(2)}) collective-permute-start(f32[4,384,2]{1,2,0:T(2,128)S(1)} %get-tuple-element.22), channel_id=1, source_target_pairs={{1,0},{2,1},{3,2},{4,3},{5,4},{6,5},{7,6},{8,7},{9,8},{10,9},{11,1... | collective-permute-start | bytes 36872 | tf_op jit(solution)/shard_map/ppermute | solution.py:16
  210.7 12.4 %copy-start = (f32[4,192,384]{2,1,0:T(8,128)S(1)}, f32[4,192,384]{2,1,0:T(8,128)}, u32[]{:S(2)}) copy-start(f32[4,192,384]{2,1,0:T(8,128)} %fusion.13) | copy-start | bytes 3538948
  239.6 87.2 %copy-start.1 = (f32[4,192,384]{2,1,0:T(8,128)S(1)}, f32[4,192,384]{2,1,0:T(8,128)}, u32[]{:S(2)}) copy-start(f32[4,192,384]{2,1,0:T(8,128)} %fusion.4) | copy-start | bytes 3538948
Sparse Core Ops, SparseCore 0:
  107.2 115.8 all-gather.2
  224.8 102.0 all-gather.4

commit v12 on v11

--- a/solution.py
+++ b/solution.py
@@ -69,15 +69,24 @@
         picked = jnp.transpose(picked, (0, 2, 1, 3)).reshape(step, cap, tblk)
 
         total = jnp.sum(picked, axis=1, keepdims=True)
-        rimmed = halo_frames(picked / total, REACH)
-        smooth = kernel[0] * rimmed[..., 0:tblk]
-        for shift_step in range(1, 2 * REACH + 1):
-            smooth = smooth + kernel[shift_step] * rimmed[..., shift_step : shift_step + tblk]
-        smooth = jnp.swapaxes(smooth, 1, 2)
-
-        scale = sizes[first : first + step].astype(jnp.float32)
-        right = lax.all_gather(smooth, "tm", axis=1, tiled=True)
-        outs.append(correlate(smooth * scale[:, None, None], right))
+        scaled = picked / total
+        scale = sizes[first : first + step].astype(jnp.float32)[:, None, None]
+        if part == 0:
+            whole = lax.all_gather(jnp.swapaxes(scaled, 1, 2), "tm", axis=1, tiled=True)
+            frames_all = whole.shape[1]
+            rimmed = jnp.pad(whole, ((0, 0), (REACH, REACH), (0, 0)))
+            right = kernel[0] * rimmed[:, 0:frames_all]
+            for shift_step in range(1, 2 * REACH + 1):
+                right = right + kernel[shift_step] * rimmed[:, shift_step : shift_step + frames_all]
+            smooth = lax.dynamic_slice_in_dim(right, lax.axis_index("tm") * tblk, tblk, 1)
+        else:
+            rimmed = halo_frames(scaled, REACH)
+            smooth = kernel[0] * rimmed[..., 0:tblk]
+            for shift_step in range(1, 2 * REACH + 1):
+                smooth = smooth + kernel[shift_step] * rimmed[..., shift_step : shift_step + tblk]
+            smooth = jnp.swapaxes(smooth, 1, 2)
+            right = lax.all_gather(smooth, "tm", axis=1, tiled=True)
+        outs.append(correlate(smooth * scale, right))
     result = lax.optimization_barrier(jnp.pad(jnp.concatenate(outs[:-1], 0), ((0, step), (0, 0), (0, 0))))
     return lax.dynamic_update_slice_in_dim(result, outs[-1], owned - step, 0)
 

time: 351 us -> 338 us (0.963)
  waiting for transfers between devices: 117 us -> 69.3 us
  other arithmetic: 12.7 us -> 51.4 us
  starting transfers between devices: 24.7 us -> 20.5 us
    all_gather x2 -> x1, waiting for transfers between devices: 86.3 us -> 30.6 us  [per_device(): right = lax.all_gather(smooth, 'tm', axis=1, tiled=True)]
    add x0 -> x1, other arithmetic: none -> 42.6 us  [per_device(): right + kernel[shift_step] * rimmed[:, shift_step:shift_step + frames_all]]
    all_gather x0 -> x1, waiting for transfers between devices: none -> 13.1 us  [per_device(): whole = lax.all_gather(jnp.swapaxes(scaled, 1, 2), 'tm', axis=1, tiled=True)]
    ppermute x2 -> x1, waiting for transfers between devices: 6.09 us -> 0.01 us  [halo_frames(): high = lax.ppermute(block[..., :width], 'tm', backward)]
    transpose x2 -> x1, other arithmetic: 9.62 us -> 4.72 us  [per_device(): smooth = jnp.swapaxes(smooth, 1, 2)]
    ppermute x2 -> x1, starting transfers between devices: 7.01 us -> 2.38 us  [halo_frames(): low = lax.ppermute(block[..., n - width:], 'tm', forward)]
  transfers between devices with their start and end apart: 8 -> 6, of which waited for: 6 -> 5; matrix products, arithmetic and copies ran while one was open for 26% -> 40% of each run, Pallas kernels for 0% -> 0%
where the time goes in v12:
time: 338 us; the launch traced here: 337 us
  local copies, waits for them, and re-layouts  128 us (38%)
  waiting for transfers between devices  69.3 us (21%)
  other arithmetic  51.4 us (15%)
  matrix products  34 us (10%)
  between operations  33.9 us (10%)
  starting transfers between devices  20.5 us (6%)
    gather x2, local copies, waits for them, and re-layouts, per_device(): series.at[windows[part]].get(mode='promise_in_bounds')  94.9 us
    add x1, other arithmetic, per_device(): right + kernel[shift_step] * rimmed[:, shift_step:shift_step + frames_all]  42.6 us
    dot_general x2, matrix products, correlate(): jnp.einsum('rfs,rgs->rfg', left, right, precision=lax.Precision.HIGH, pre...  33.7 us
    all_gather x1, waiting for transfers between devices, per_device(): right = lax.all_gather(smooth, 'tm', axis=1, tiled=True)  30.6 us
    all_to_all x2, waiting for transfers between devices, per_device(): got = lax.all_to_all(chunks, 'pix', 0, 0, tiled=True)  25.4 us
    all_to_all x2, starting transfers between devices, per_device(): got = lax.all_to_all(chunks, 'pix', 0, 0, tiled=True)  14.5 us
    pad x1, local copies, waits for them, and re-layouts, per_device(): jnp.pad(jnp.concatenate(outs[:-1], 0), ((0, step), (0, 0), (0, 0)))  13.4 us
    all_gather x1, waiting for transfers between devices, per_device(): whole = lax.all_gather(jnp.swapaxes(scaled, 1, 2), 'tm', axis=1, tiled=True)  13.1 us
  transfers between devices with their start and end apart: 6, of which 5 were waited for; matrix products, arithmetic and copies ran while one was open for 40% of the time, Pallas kernels for 0%

profile of v12, /device:TPU:1, one launch (start us, length us, event | category | flops | bytes accessed | tf_op | source)
XLA Modules:
  0.0 337.4 jit_solution(4494635523298920984)
XLA Ops:
  6.5 0.7 copy.10
  7.5 0.7 sub.31
  8.2 4.9 %copy.9 = f32[1,24,12288]{1,2,0:T(8,128)} copy(f32[1,24,12288]{2,1,0:T(8,128)} %param.4) | data formatting | bytes 2359296 | tf_op args[0]
  13.7 47.5 %gather_fusion = f32[13312,24]{1,0:T(8,128)} fusion(f32[12288,24]{1,0:T(8,128)} %bitcast.75, s32[13312]{0:T(1024)S(1)} %broadcast_clamp_fusion.1), kind=kCustom, calls=%fused_computation | custom fusion | bytes 2609152 | tf_op jit(solution)/shard_map/gather | solution.py:58
  61.2 5.5 %copy.11 = f32[8,1664,24]{1,2,0:T(8,128)} copy(f32[8,1664,24]{2,1,0:T(8,128)} %bitcast.78) | data formatting | bytes 2555904 | tf_op jit(solution)/shard_map/reshape | solution.py:58
  66.7 8.6 %all-to-all-start = ((f32[8,1664,24]{1,2,0:T(8,128)}), f32[8,1664,24]{1,2,0:T(8,128)S(1)}, u32[]{:S(2)}, u32[]{:S(2)}) async-start(f32[8,1664,24]{1,2,0:T(8,128)} %copy.11), calls=%async_computation | async-start | bytes 2555904 | tf_op jit(solution)/shard_map/all_to_all | solution.py:59
  81.0 0.7 fusion.53
  89.5 2.5 all-to-all-done
  92.8 1.2 bitcast_divide_fusion.1
  94.1 47.5 %gather_fusion.1 = f32[13312,24]{1,0:T(8,128)} fusion(f32[12288,24]{1,0:T(8,128)} %bitcast.76, s32[13312]{0:T(1024)S(1)} %broadcast_clamp_fusion), kind=kCustom, calls=%fused_computation.1 | custom fusion | bytes 2609152 | tf_op jit(solution)/shard_map/gather | solution.py:58
  141.6 5.6 %copy.12 = f32[8,1664,24]{1,2,0:T(8,128)} copy(f32[8,1664,24]{2,1,0:T(8,128)} %bitcast.77) | data formatting | bytes 2555904 | tf_op jit(solution)/shard_map/reshape | solution.py:58
  147.2 5.9 %all-to-all-start.1 = ((f32[8,1664,24]{1,2,0:T(8,128)}), f32[8,1664,24]{1,2,0:T(8,128)S(1)}, u32[]{:S(2)}, u32[]{:S(2)}) async-start(f32[8,1664,24]{1,2,0:T(8,128)} %copy.12), calls=%async_computation.1 | async-start | bytes 2555904 | tf_op jit(solution)/shard_map/all_to_all | solution.py:59
  153.2 0.7 fusion.50
  161.7 22.9 %all-to-all-done.1 = f32[8,1664,24]{1,2,0:T(8,128)S(1)} async-done(((f32[8,1664,24]{1,2,0:T(8,128)}), f32[8,1664,24]{1,2,0:T(8,128)S(1)}, u32[]{:S(2)}, u32[]{:S(2)}) %all-to-all-start.1) | async-done | bytes 1277984 | tf_op jit(solution)/shard_map/all_to_all | solution.py:59
  185.6 3.5 %collective-permute-start.1 = (f32[4,384,2]{1,2,0:T(2,128)S(1)}, f32[4,384,2]{1,2,0:T(2,128)S(1)}, u32[]{:S(2)}, u32[]{:S(2)}) collective-permute-start(f32[4,384,2]{1,2,0:T(2,128)S(1)} %get-tuple-element.22), channel_id=1, source_target_pairs={{1,0},{2,1},{3,2},{4,3},{5,4},{6,5},{7,6},{8,7},{9,8},{10,9},{11,1... | collective-permute-start | bytes 36872 | tf_op jit(solution)/shard_map/ppermute | solution.py:16
  189.1 2.4 collective-permute-start
  191.5 0.7 fusion.52
  192.3 4.7 %fusion.5 = f32[4,192,384]{2,1,0:T(8,128)} fusion(f32[4,384,192]{1,2,0:T(8,128)S(1)} %bitcast_divide_fusion, f32[4,384,2]{1,2,0:T(2,128)S(1)} %collective-permute-done.1, f32[4,384,2]{1,2,0:T(2,128)S(1)} %collective-permute-done, f32[]{:T(128)} %bitcast.26, f32[]{:T(128)} %bitcast.25, f32[]{:T(128)} %bitcast.24, f32[]{:T(128)} %bitcast.23, f32[]{:T(128)} %bitcast), kind=kLoop, calls=%fused_computation.22 | loop fusion | flops 3833856 | bytes 2383892 | tf_op jit(solution)/shard_map/transpose | solution.py:87
  197.1 13.1 %all-gather.3.cloned.1.call-done = f32[4,3072,384]{2,1,0:T(8,128)} async-done(((f32[4,192,384]{2,1,0:T(8,128)}), f32[4,3072,384]{2,1,0:T(8,128)}) %all-gather.3.cloned.1.call-update) | async-done | bytes 18874384 | tf_op jit(solution)/shard_map/all_gather | solution.py:75
  210.2 42.6 %multiply_add_fusion = f32[4,3072,384]{2,1,0:T(8,128)} fusion(f32[4,3072,384]{2,1,0:T(8,128)} %all-gather.3.cloned.1.call-done, f32[]{:T(128)} %bitcast.26, f32[]{:T(128)} %bitcast.25, f32[]{:T(128)} %bitcast.24, f32[]{:T(128)} %bitcast.23, f32[]{:T(128)} %bitcast), kind=kLoop, calls=%fused_computation.2 | loop fusion | flops 42467328 | bytes 37748756 | tf_op jit(solution)/shard_map/add | solution.py:80
  252.8 17.1 %fusion.13 = f32[4,192,3072]{2,1,0:T(8,128)} fusion(f32[4,3072,384]{2,1,0:T(8,128)} %multiply_add_fusion, s32[]{:T(128)S(6)} %select_n.106, f32[4]{0:T(128)S(1)} %get-tuple-element.26), kind=kOutput, calls=%fused_computation.38 | convolution fusion | flops 5436112896 | bytes 29491220 | tf_op jit(solution)/shard_map/rfs,rgs->rfg/dot_general | solution.py:21
  270.0 13.4 %pad.22 = f32[8,192,3072]{2,1,0:T(8,128)} pad(f32[4,192,3072]{2,1,0:T(8,128)} %fusion.13, f32[]{:T(128)} %constant.69.clone.1), padding=0_4x0_0x0_0 | pad | bytes 28311556 | tf_op jit(solution)/shard_map/jit(_pad)/pad | solution.py:90
  283.4 30.6 %all-gather.5.cloned.1.call-done = f32[4,3072,384]{2,1,0:T(8,128)} async-done(((f32[4,192,384]{2,1,0:T(8,128)}), f32[4,3072,384]{2,1,0:T(8,128)}) %all-gather.5.cloned.1.call-update) | async-done | bytes 18874384 | tf_op jit(solution)/shard_map/all_gather | solution.py:88
  313.9 16.6 %convolution_dynamic-update-slice_fusion = f32[8,192,3072]{2,1,0:T(8,128)} fusion(f32[8,192,3072]{2,1,0:T(8,128)} %pad.22, f32[4,3072,384]{2,1,0:T(8,128)} %all-gather.5.cloned.1.call-done, f32[4,192,384]{2,1,0:T(8,128)S(1)} %copy-done, f32[4]{0:T(128)S(1)} %get-tuple-element.25), kind=kOutput, calls=%fused_computation.5 | convolution fusion | flops 5436112896 | bytes 29491216 | tf_op jit(solution)/shard_map/rfs,rgs->rfg/dot_general | solution.py:21
  (47 shorter events, 3.9 us)
Async XLA Ops:
  8.2 5.0 %copy-start.3 = (s32[12288]{0:T(1024)S(1)}, s32[12288]{0:T(1024)}, u32[]{:S(2)}) copy-start(s32[12288]{0:T(1024)} %param.5) | copy-start | bytes 147460
  66.7 8.7 %copy-start.2 = (s32[64]{0:T(128)S(1)}, s32[64]{0:T(128)}, u32[]{:S(2)}) copy-start(s32[64]{0:T(128)} %param.6) | copy-start | bytes 772
  66.7 25.3 %all-to-all-start = ((f32[8,1664,24]{1,2,0:T(8,128)}), f32[8,1664,24]{1,2,0:T(8,128)S(1)}, u32[]{:S(2)}, u32[]{:S(2)}) async-start(f32[8,1664,24]{1,2,0:T(8,128)} %copy.11), calls=%async_computation | async-start | bytes 2555904 | tf_op jit(solution)/shard_map/all_to_all | solution.py:59
  75.3 134.9 %all-gather.3.cloned.1.call-start = ((), (), s32[]{:S(2)}) async-start(), calls=%async_computation.2 | async-start | bytes 20054016 | tf_op jit(solution)/shard_map/all_gather | solution.py:75
  147.2 37.5 %all-to-all-start.1 = ((f32[8,1664,24]{1,2,0:T(8,128)}), f32[8,1664,24]{1,2,0:T(8,128)S(1)}, u32[]{:S(2)}, u32[]{:S(2)}) async-start(f32[8,1664,24]{1,2,0:T(8,128)} %copy.12), calls=%async_computation.1 | async-start | bytes 2555904 | tf_op jit(solution)/shard_map/all_to_all | solution.py:59
  153.1 160.8 %all-gather.5.cloned.1.call-start = ((), (), s32[]{:S(2)}) async-start(), calls=%async_computation.3 | async-start | bytes 20054016 | tf_op jit(solution)/shard_map/all_gather | solution.py:88
  185.4 6.1 %copy-start.1 = (f32[5]{0:T(128)S(1)}, f32[5]{0:T(128)}, u32[]{:S(2)}) copy-start(f32[5]{0:T(128)} %param.7) | copy-start | bytes 64
  185.6 6.6 %collective-permute-start.1 = (f32[4,384,2]{1,2,0:T(2,128)S(1)}, f32[4,384,2]{1,2,0:T(2,128)S(1)}, u32[]{:S(2)}, u32[]{:S(2)}) collective-permute-start(f32[4,384,2]{1,2,0:T(2,128)S(1)} %get-tuple-element.22), channel_id=1, source_target_pairs={{1,0},{2,1},{3,2},{4,3},{5,4},{6,5},{7,6},{8,7},{9,8},{10,9},{11,1... | collective-permute-start | bytes 36872 | tf_op jit(solution)/shard_map/ppermute | solution.py:16
  189.1 3.2 collective-permute-start
  270.0 44.0 %copy-start = (f32[4,192,384]{2,1,0:T(8,128)S(1)}, f32[4,192,384]{2,1,0:T(8,128)}, u32[]{:S(2)}) copy-start(f32[4,192,384]{2,1,0:T(8,128)} %fusion.5) | copy-start | bytes 3538948
Sparse Core Ops, SparseCore 0:
  94.1 116.0 all-gather.2
  211.9 102.0 all-gather.4

commit v13 on v12

--- a/solution.py
+++ b/solution.py
@@ -40,7 +40,7 @@
     sizes = lax.dynamic_index_in_dim(cycle_sizes.reshape(groups, owned), me, 0, keepdims=False)
     slots = jnp.arange(cap, dtype=jnp.int32)
 
-    lanes = 128
+    lanes = 32
     span = window + lanes
     count = pixels // lanes + span // lanes
     order = jnp.pad(pixel_order, (0, count * lanes - pixels)).reshape(count, lanes).astype(jnp.float32)

time: 338 us -> 319 us (0.944)
  local copies, waits for them, and re-layouts: 128 us -> 87.2 us
  waiting for transfers between devices: 69.3 us -> 90 us
    gather x2, local copies, waits for them, and re-layouts: 94.9 us -> 53.4 us  [per_device(): series.at[windows[part]].get(mode='promise_in_bounds')]
    all_gather x1, waiting for transfers between devices: 13.1 us -> 33.8 us  [per_device(): whole = lax.all_gather(jnp.swapaxes(scaled, 1, 2), 'tm', axis=1, tiled=True)]
  transfers between devices with their start and end apart: 6 -> 6, of which waited for: 5 -> 5; matrix products, arithmetic and copies ran while one was open for 40% -> 36% of each run, Pallas kernels for 0% -> 0%
where the time goes in v13:
time: 319 us
  waiting for transfers between devices  90 us (28%)
  local copies, waits for them, and re-layouts  87.2 us (27%)
  other arithmetic  51.6 us (16%)
  matrix products  35.5 us (11%)
  between operations  33.9 us (11%)
  starting transfers between devices  20.3 us (6%)
    gather x2, local copies, waits for them, and re-layouts, per_device(): series.at[windows[part]].get(mode='promise_in_bounds')  53.4 us
    add x1, other arithmetic, per_device(): right + kernel[shift_step] * rimmed[:, shift_step:shift_step + frames_all]  42.6 us
    all_gather x1, waiting for transfers between devices, per_device(): whole = lax.all_gather(jnp.swapaxes(scaled, 1, 2), 'tm', axis=1, tiled=True)  33.8 us
    dot_general x2, matrix products, correlate(): jnp.einsum('rfs,rgs->rfg', left, right, precision=lax.Precision.HIGH, pre...  33.7 us
    all_gather x1, waiting for transfers between devices, per_device(): right = lax.all_gather(smooth, 'tm', axis=1, tiled=True)  30.6 us
    all_to_all x2, waiting for transfers between devices, per_device(): got = lax.all_to_all(chunks, 'pix', 0, 0, tiled=True)  25.5 us
    all_to_all x2, starting transfers between devices, per_device(): got = lax.all_to_all(chunks, 'pix', 0, 0, tiled=True)  14.4 us
    pad x1, local copies, waits for them, and re-layouts, per_device(): jnp.pad(jnp.concatenate(outs[:-1], 0), ((0, step), (0, 0), (0, 0)))  13.4 us
  transfers between devices with their start and end apart: 6, of which 5 were waited for; matrix products, arithmetic and copies ran while one was open for 36% of the time, Pallas kernels for 0%

profile of v13, /device:TPU:1, one launch (start us, length us, event | category | flops | bytes accessed | tf_op | source)
XLA Modules:
  0.0 318.5 jit_solution(11208440504326385332)
XLA Ops:
  6.5 0.7 copy.10
  7.5 0.7 sub.31
  8.2 4.9 %copy.9 = f32[1,24,12288]{1,2,0:T(8,128)} copy(f32[1,24,12288]{2,1,0:T(8,128)} %param.4) | data formatting | bytes 2359296 | tf_op args[0]
  13.4 1.8 fusion.18
  15.7 26.7 %gather_fusion = f32[12544,24]{1,0:T(8,128)} fusion(f32[12288,24]{1,0:T(8,128)} %bitcast.65, s32[13312]{0:T(1024)S(1)} %pad_clamp_fusion.1), kind=kCustom, calls=%fused_computation | custom fusion | bytes 2458624 | tf_op jit(solution)/shard_map/gather | solution.py:58
  42.4 5.4 %copy.13 = f32[8,1568,24]{1,2,0:T(8,128)} copy(f32[8,1568,24]{2,1,0:T(8,128)} %bitcast.68) | data formatting | bytes 2408448 | tf_op jit(solution)/shard_map/reshape | solution.py:58
  47.8 8.6 %all-to-all-start = ((f32[8,1568,24]{1,2,0:T(8,128)}), f32[8,1568,24]{1,2,0:T(8,128)S(1)}, u32[]{:S(2)}, u32[]{:S(2)}) async-start(f32[8,1568,24]{1,2,0:T(8,128)} %copy.13), calls=%async_computation | async-start | bytes 2555904 | tf_op jit(solution)/shard_map/all_to_all | solution.py:59
  62.2 0.7 fusion.54
  70.6 2.5 all-to-all-done
  73.9 1.2 bitcast_divide_fusion.1
  75.6 26.7 %gather_fusion.1 = f32[12544,24]{1,0:T(8,128)} fusion(f32[12288,24]{1,0:T(8,128)} %bitcast.66, s32[13312]{0:T(1024)S(1)} %pad_clamp_fusion), kind=kCustom, calls=%fused_computation.1 | custom fusion | bytes 2458624 | tf_op jit(solution)/shard_map/gather | solution.py:58
  102.3 5.6 %copy.15 = f32[8,1568,24]{1,2,0:T(8,128)} copy(f32[8,1568,24]{2,1,0:T(8,128)} %bitcast.67) | data formatting | bytes 2408448 | tf_op jit(solution)/shard_map/reshape | solution.py:58
  107.9 5.8 %all-to-all-start.1 = ((f32[8,1568,24]{1,2,0:T(8,128)}), f32[8,1568,24]{1,2,0:T(8,128)S(1)}, u32[]{:S(2)}, u32[]{:S(2)}) async-start(f32[8,1568,24]{1,2,0:T(8,128)} %copy.15), calls=%async_computation.1 | async-start | bytes 2555904 | tf_op jit(solution)/shard_map/all_to_all | solution.py:59
  122.3 23.0 %all-to-all-done.1 = f32[8,1568,24]{1,2,0:T(8,128)S(1)} async-done(((f32[8,1568,24]{1,2,0:T(8,128)}), f32[8,1568,24]{1,2,0:T(8,128)S(1)}, u32[]{:S(2)}, u32[]{:S(2)}) %all-to-all-start.1) | async-done | bytes 1204256 | tf_op jit(solution)/shard_map/all_to_all | solution.py:59
  146.2 3.4 %collective-permute-start.1 = (f32[4,384,2]{1,2,0:T(2,128)S(1)}, f32[4,384,2]{1,2,0:T(2,128)S(1)}, u32[]{:S(2)}, u32[]{:S(2)}) collective-permute-start(f32[4,384,2]{1,2,0:T(2,128)S(1)} %get-tuple-element.22), channel_id=1, source_target_pairs={{1,0},{2,1},{3,2},{4,3},{5,4},{6,5},{7,6},{8,7},{9,8},{10,9},{11,1... | collective-permute-start | bytes 36872 | tf_op jit(solution)/shard_map/ppermute | solution.py:16
  149.6 2.4 collective-permute-start
  152.0 0.7 fusion.53
  152.8 4.7 %fusion.6 = f32[4,192,384]{2,1,0:T(8,128)} fusion(f32[4,384,192]{1,2,0:T(8,128)S(1)} %bitcast_divide_fusion, f32[4,384,2]{1,2,0:T(2,128)S(1)} %collective-permute-done.1, f32[4,384,2]{1,2,0:T(2,128)S(1)} %collective-permute-done, f32[]{:T(128)} %bitcast.23, f32[]{:T(128)} %bitcast.22, f32[]{:T(128)} %bitcast.21, f32[]{:T(128)} %bitcast.20, f32[]{:T(128)} %bitcast), kind=kLoop, calls=%fused_computation.24 | loop fusion | flops 3833856 | bytes 2383892 | tf_op jit(solution)/shard_map/transpose | solution.py:87
  157.6 33.8 %all-gather.3.cloned.1.call-done = f32[4,3072,384]{2,1,0:T(8,128)} async-done(((f32[4,192,384]{2,1,0:T(8,128)}), f32[4,3072,384]{2,1,0:T(8,128)}) %all-gather.3.cloned.1.call-update) | async-done | bytes 18874384 | tf_op jit(solution)/shard_map/all_gather | solution.py:75
  191.3 42.6 %multiply_add_fusion = f32[4,3072,384]{2,1,0:T(8,128)} fusion(f32[4,3072,384]{2,1,0:T(8,128)} %all-gather.3.cloned.1.call-done, f32[]{:T(128)} %bitcast.23, f32[]{:T(128)} %bitcast.22, f32[]{:T(128)} %bitcast.21, f32[]{:T(128)} %bitcast.20, f32[]{:T(128)} %bitcast), kind=kLoop, calls=%fused_computation.2 | loop fusion | flops 42467328 | bytes 37748756 | tf_op jit(solution)/shard_map/add | solution.py:80
  234.0 17.2 %fusion.14 = f32[4,192,3072]{2,1,0:T(8,128)} fusion(f32[4,3072,384]{2,1,0:T(8,128)} %multiply_add_fusion, s32[]{:T(128)S(6)} %select_n.106, f32[4]{0:T(128)S(1)} %get-tuple-element.26), kind=kOutput, calls=%fused_computation.40 | convolution fusion | flops 5436112896 | bytes 29491220 | tf_op jit(solution)/shard_map/rfs,rgs->rfg/dot_general | solution.py:21
  251.1 13.4 %pad.22 = f32[8,192,3072]{2,1,0:T(8,128)} pad(f32[4,192,3072]{2,1,0:T(8,128)} %fusion.14, f32[]{:T(128)} %constant.69.clone.1), padding=0_4x0_0x0_0 | pad | bytes 28311556 | tf_op jit(solution)/shard_map/jit(_pad)/pad | solution.py:90
  264.5 30.6 %all-gather.5.cloned.1.call-done = f32[4,3072,384]{2,1,0:T(8,128)} async-done(((f32[4,192,384]{2,1,0:T(8,128)}), f32[4,3072,384]{2,1,0:T(8,128)}) %all-gather.5.cloned.1.call-update) | async-done | bytes 18874384 | tf_op jit(solution)/shard_map/all_gather | solution.py:88
  295.1 16.6 %convolution_dynamic-update-slice_fusion = f32[8,192,3072]{2,1,0:T(8,128)} fusion(f32[8,192,3072]{2,1,0:T(8,128)} %pad.22, f32[4,3072,384]{2,1,0:T(8,128)} %all-gather.5.cloned.1.call-done, f32[4,192,384]{2,1,0:T(8,128)S(1)} %copy-done, f32[4]{0:T(128)S(1)} %get-tuple-element.25), kind=kOutput, calls=%fused_computation.5 | convolution fusion | flops 5436112896 | bytes 29491216 | tf_op jit(solution)/shard_map/rfs,rgs->rfg/dot_general | solution.py:21
  (51 shorter events, 5.2 us)
Async XLA Ops:
  8.2 5.0 %copy-start.1 = (s32[12288]{0:T(1024)S(1)}, s32[12288]{0:T(1024)}, u32[]{:S(2)}) copy-start(s32[12288]{0:T(1024)} %param.5) | copy-start | bytes 147460
  47.8 8.7 %copy-start.3 = (s32[64]{0:T(128)S(1)}, s32[64]{0:T(128)}, u32[]{:S(2)}) copy-start(s32[64]{0:T(128)} %param.6) | copy-start | bytes 772
  47.8 25.3 %all-to-all-start = ((f32[8,1568,24]{1,2,0:T(8,128)}), f32[8,1568,24]{1,2,0:T(8,128)S(1)}, u32[]{:S(2)}, u32[]{:S(2)}) async-start(f32[8,1568,24]{1,2,0:T(8,128)} %copy.13), calls=%async_computation | async-start | bytes 2555904 | tf_op jit(solution)/shard_map/all_to_all | solution.py:59
  56.5 134.9 %all-gather.3.cloned.1.call-start = ((), (), s32[]{:S(2)}) async-start(), calls=%async_computation.2 | async-start | bytes 20054016 | tf_op jit(solution)/shard_map/all_gather | solution.py:75
  107.9 37.4 %all-to-all-start.1 = ((f32[8,1568,24]{1,2,0:T(8,128)}), f32[8,1568,24]{1,2,0:T(8,128)S(1)}, u32[]{:S(2)}, u32[]{:S(2)}) async-start(f32[8,1568,24]{1,2,0:T(8,128)} %copy.15), calls=%async_computation.1 | async-start | bytes 2555904 | tf_op jit(solution)/shard_map/all_to_all | solution.py:59
  113.7 181.4 %all-gather.5.cloned.1.call-start = ((), (), s32[]{:S(2)}) async-start(), calls=%async_computation.3 | async-start | bytes 20054016 | tf_op jit(solution)/shard_map/all_gather | solution.py:88
  146.0 6.0 %copy-start.2 = (f32[5]{0:T(128)S(1)}, f32[5]{0:T(128)}, u32[]{:S(2)}) copy-start(f32[5]{0:T(128)} %param.7) | copy-start | bytes 64
  146.2 6.5 %collective-permute-start.1 = (f32[4,384,2]{1,2,0:T(2,128)S(1)}, f32[4,384,2]{1,2,0:T(2,128)S(1)}, u32[]{:S(2)}, u32[]{:S(2)}) collective-permute-start(f32[4,384,2]{1,2,0:T(2,128)S(1)} %get-tuple-element.22), channel_id=1, source_target_pairs={{1,0},{2,1},{3,2},{4,3},{5,4},{6,5},{7,6},{8,7},{9,8},{10,9},{11,1... | collective-permute-start | bytes 36872 | tf_op jit(solution)/shard_map/ppermute | solution.py:16
  149.6 3.2 %collective-permute-start = (f32[4,384,2]{1,2,0:T(2,128)S(1)}, f32[4,384,2]{1,2,0:T(2,128)S(1)}, u32[]{:S(2)}, u32[]{:S(2)}) collective-permute-start(f32[4,384,2]{1,2,0:T(2,128)S(1)} %get-tuple-element.21), channel_id=1, source_target_pairs={{0,1},{1,2},{2,3},{3,4},{4,5},{5,6},{6,7},{7,8},{8,9},{9,10},{10,1... | collective-permute-start | bytes 36872 | tf_op jit(solution)/shard_map/ppermute | solution.py:15
  251.1 44.0 %copy-start = (f32[4,192,384]{2,1,0:T(8,128)S(1)}, f32[4,192,384]{2,1,0:T(8,128)}, u32[]{:S(2)}) copy-start(f32[4,192,384]{2,1,0:T(8,128)} %fusion.6) | copy-start | bytes 3538948
Sparse Core Ops, SparseCore 0:
  75.3 116.0 all-gather.2
  193.0 102.0 all-gather.4

commit v14 on v13

--- a/solution.py
+++ b/solution.py
@@ -4,7 +4,6 @@
 from jax.sharding import PartitionSpec as P
 
 REACH = 2
-PARTS = 2
 
 
 def halo_frames(block, width):
@@ -30,41 +29,40 @@
     cap = 2 * pixels // cycles
     groups = lax.axis_size("pix")
     owned = cycles // groups
-    step = owned // PARTS
-    window = step * cap
+    counts = [owned - owned * 5 // 8, owned * 5 // 8]
+    firsts = [sum(counts[:i]) for i in range(len(counts))]
     tblk = groups * sub
     starts = (jnp.cumsum(cycle_sizes) - cycle_sizes).astype(jnp.int32).reshape(groups, owned)
-    sends = starts[:, ::step]
     me = lax.axis_index("pix")
     mine = lax.dynamic_index_in_dim(starts, me, 0, keepdims=False)
     sizes = lax.dynamic_index_in_dim(cycle_sizes.reshape(groups, owned), me, 0, keepdims=False)
     slots = jnp.arange(cap, dtype=jnp.int32)
 
     lanes = 32
-    span = window + lanes
-    count = pixels // lanes + span // lanes
+    longest = max(counts) * cap + lanes
+    count = pixels // lanes + longest // lanes
     order = jnp.pad(pixel_order, (0, count * lanes - pixels)).reshape(count, lanes).astype(jnp.float32)
-    aligned = (sends // lanes) * lanes
-    rows = (aligned // lanes)[:, :, None] + jnp.arange(span // lanes, dtype=jnp.int32)
-    pick_rows = (rows[..., None] == jnp.arange(count, dtype=jnp.int32)).astype(jnp.float32)
-    windows = jnp.einsum(
-        "dprk,kl->pdrl", pick_rows, order, precision=lax.Precision.HIGHEST, preferred_element_type=jnp.float32
-    )
-    windows = windows.astype(jnp.int32).reshape(PARTS, groups * span)
     series = block.T
 
     outs = []
-    for part in range(PARTS):
-        chunks = series.at[windows[part]].get(mode="promise_in_bounds").reshape(groups, span, sub)
+    for part, (step, first) in enumerate(zip(counts, firsts)):
+        span = step * cap + lanes
+        aligned = (starts[:, first] // lanes) * lanes
+        rows = (aligned // lanes)[:, None] + jnp.arange(span // lanes, dtype=jnp.int32)
+        pick_rows = (rows[..., None] == jnp.arange(count, dtype=jnp.int32)).astype(jnp.float32)
+        window = jnp.einsum(
+            "drk,kl->drl", pick_rows, order, precision=lax.Precision.HIGHEST, preferred_element_type=jnp.float32
+        )
+        window = window.astype(jnp.int32).reshape(groups * span)
+        chunks = series.at[window].get(mode="promise_in_bounds").reshape(groups, span, sub)
         got = lax.all_to_all(chunks, "pix", 0, 0, tiled=True)
         got = jnp.pad(got, ((0, 0), (0, cap), (0, 0)))
-        first = part * step
         offsets = mine[first : first + step] - (mine[first] // lanes) * lanes
         masks = slots[None, :] < sizes[first : first + step, None]
         picked = []
         for l in range(step):
-            rows = lax.dynamic_slice_in_dim(got, offsets[l], cap, 1)
-            picked.append(jnp.where(masks[l][None, :, None], rows, 0.0))
+            taken = lax.dynamic_slice_in_dim(got, offsets[l], cap, 1)
+            picked.append(jnp.where(masks[l][None, :, None], taken, 0.0))
         picked = jnp.stack(picked)
         picked = jnp.transpose(picked, (0, 2, 1, 3)).reshape(step, cap, tblk)
 
@@ -87,8 +85,9 @@
             smooth = jnp.swapaxes(smooth, 1, 2)
             right = lax.all_gather(smooth, "tm", axis=1, tiled=True)
         outs.append(correlate(smooth * scale, right))
-    result = lax.optimization_barrier(jnp.pad(jnp.concatenate(outs[:-1], 0), ((0, step), (0, 0), (0, 0))))
-    return lax.dynamic_update_slice_in_dim(result, outs[-1], owned - step, 0)
+    last = counts[-1]
+    result = lax.optimization_barrier(jnp.pad(jnp.concatenate(outs[:-1], 0), ((0, last), (0, 0), (0, 0))))
+    return lax.dynamic_update_slice_in_dim(result, outs[-1], owned - last, 0)
 
 
 def solution(mesh):

time: 319 us -> 315 us (0.987)
  other arithmetic: 51.6 us -> 44.3 us
  waiting for transfers between devices: 90 us -> 95.8 us
    all_gather x1, waiting for transfers between devices: 33.8 us -> 0.02 us  [per_device(): whole = lax.all_gather(jnp.swapaxes(scaled, 1, 2), 'tm', axis=1, tiled=True)]
    all_gather x1, waiting for transfers between devices: 30.6 us -> 63.8 us  [per_device(): right = lax.all_gather(smooth, 'tm', axis=1, tiled=True)]
    add x1, other arithmetic: 42.6 us -> 33.8 us  [per_device(): right + kernel[shift_step] * rimmed[:, shift_step:shift_step + frames_all]]
    all_to_all x2, waiting for transfers between devices: 25.5 us -> 28.9 us  [per_device(): got = lax.all_to_all(chunks, 'pix', 0, 0, tiled=True)]
    reshape x2 -> x4, local copies, waits for them, and re-layouts: 11 us -> 10.3 us  [the longest x2 10 us: per_device(): series.at[window].get(mode='promise_in_bounds').reshape(groups, span, sub)]
  transfers between devices with their start and end apart: 6 -> 6, of which waited for: 5 -> 4; matrix products, arithmetic and copies ran while one was open for 36% -> 35% of each run, Pallas kernels for 0% -> 0%
where the time goes in v14:
time: 315 us; the launch traced here: 314 us
  waiting for transfers between devices  95.8 us (30%)
  local copies, waits for them, and re-layouts  84.6 us (27%)
  other arithmetic  44.3 us (14%)
  matrix products  35.4 us (11%)
  between operations  33.7 us (11%)
  starting transfers between devices  20.5 us (7%)
    all_gather x1, waiting for transfers between devices, per_device(): right = lax.all_gather(smooth, 'tm', axis=1, tiled=True)  63.8 us
    gather x2, local copies, waits for them, and re-layouts, per_device(): series.at[window].get(mode='promise_in_bounds').reshape(groups, span, sub)  53.4 us
    add x1, other arithmetic, per_device(): right + kernel[shift_step] * rimmed[:, shift_step:shift_step + frames_all]  33.8 us
    dot_general x2, matrix products, correlate(): jnp.einsum('rfs,rgs->rfg', left, right, precision=lax.Precision.HIGH, pre...  33.6 us
    all_to_all x2, waiting for transfers between devices, per_device(): got = lax.all_to_all(chunks, 'pix', 0, 0, tiled=True)  28.9 us
    all_to_all x2, starting transfers between devices, per_device(): got = lax.all_to_all(chunks, 'pix', 0, 0, tiled=True)  14.5 us
    pad x1, local copies, waits for them, and re-layouts, per_device(): jnp.pad(jnp.concatenate(outs[:-1], 0), ((0, last), (0, 0), (0, 0)))  12.7 us
    reshape x2, local copies, waits for them, and re-layouts, per_device(): series.at[window].get(mode='promise_in_bounds').reshape(groups, span, sub)  10 us
  transfers between devices with their start and end apart: 6, of which 4 were waited for; matrix products, arithmetic and copies ran while one was open for 35% of the time, Pallas kernels for 0%

profile of v14, /device:TPU:1, one launch (start us, length us, event | category | flops | bytes accessed | tf_op | source)
XLA Modules:
  0.0 314.3 jit_solution(2399621395003718831)
XLA Ops:
  6.5 0.8 copy.10
  7.6 0.7 sub.37
  8.6 0.8 pad_convert_fusion
  9.5 0.8 convolution_convert_fusion.1
  10.8 4.0 %copy.9 = f32[1,24,12288]{1,2,0:T(8,128)} copy(f32[1,24,12288]{2,1,0:T(8,128)S(1)} %copy-done.1) | data formatting | bytes 2359296 | tf_op args[0]
  14.8 21.1 %gather_fusion = f32[9472,24]{1,0:T(8,128)} fusion(f32[12288,24]{1,0:T(8,128)} %bitcast.76, s32[10240]{0:T(1024)S(1)} %pad_clamp_fusion.1), kind=kCustom, calls=%fused_computation | custom fusion | bytes 1856512 | tf_op jit(solution)/shard_map/gather | solution.py:57
  35.8 3.9 %copy.13 = f32[8,1184,24]{1,2,0:T(8,128)} copy(f32[8,1184,24]{2,1,0:T(8,128)} %bitcast.79) | data formatting | bytes 1818624 | tf_op jit(solution)/shard_map/reshape | solution.py:57
  39.8 8.6 %all-to-all-start = ((f32[8,1184,24]{1,2,0:T(8,128)}), f32[8,1184,24]{1,2,0:T(8,128)S(1)}, u32[]{:S(2)}, u32[]{:S(2)}) async-start(f32[8,1184,24]{1,2,0:T(8,128)} %copy.13), calls=%async_computation | async-start | bytes 1966080 | tf_op jit(solution)/shard_map/all_to_all | solution.py:58
  58.3 3.6 %all-to-all-done = f32[8,1184,24]{1,2,0:T(8,128)S(1)} async-done(((f32[8,1184,24]{1,2,0:T(8,128)}), f32[8,1184,24]{1,2,0:T(8,128)S(1)}, u32[]{:S(2)}, u32[]{:S(2)}) %all-to-all-start) | async-done | bytes 909344 | tf_op jit(solution)/shard_map/all_to_all | solution.py:58
  62.5 1.1 bitcast_divide_fusion.1
  63.7 0.9 convolution_convert_fusion
  65.2 32.3 %gather_fusion.1 = f32[15616,24]{1,0:T(8,128)} fusion(f32[12288,24]{1,0:T(8,128)} %bitcast.77, s32[16384]{0:T(1024)S(1)} %pad_clamp_fusion), kind=kCustom, calls=%fused_computation.1 | custom fusion | bytes 3060736 | tf_op jit(solution)/shard_map/gather | solution.py:57
  97.5 6.1 %copy.16 = f32[8,1952,24]{1,2,0:T(8,128)} copy(f32[8,1952,24]{2,1,0:T(8,128)} %bitcast.78) | data formatting | bytes 2998272 | tf_op jit(solution)/shard_map/reshape | solution.py:57
  103.6 5.9 %all-to-all-start.1 = ((f32[8,1952,24]{1,2,0:T(8,128)}), f32[8,1952,24]{1,2,0:T(8,128)S(1)}, u32[]{:S(2)}, u32[]{:S(2)}) async-start(f32[8,1952,24]{1,2,0:T(8,128)} %copy.16), calls=%async_computation.1 | async-start | bytes 3145728 | tf_op jit(solution)/shard_map/all_to_all | solution.py:58
  122.0 25.3 %all-to-all-done.1 = f32[8,1952,24]{1,2,0:T(8,128)S(1)} async-done(((f32[8,1952,24]{1,2,0:T(8,128)}), f32[8,1952,24]{1,2,0:T(8,128)S(1)}, u32[]{:S(2)}, u32[]{:S(2)}) %all-to-all-start.1) | async-done | bytes 1499168 | tf_op jit(solution)/shard_map/all_to_all | solution.py:58
  148.7 3.8 %collective-permute-start = (f32[5,384,2]{1,2,0:T(2,128)S(1)}, f32[5,384,2]{1,2,0:T(2,128)S(1)}, u32[]{:S(2)}, u32[]{:S(2)}) collective-permute-start(f32[5,384,2]{1,2,0:T(2,128)S(1)} %get-tuple-element.15), channel_id=1, source_target_pairs={{0,1},{1,2},{2,3},{3,4},{4,5},{5,6},{6,7},{7,8},{8,9},{9,10},{10,1... | collective-permute-start | bytes 46088 | tf_op jit(solution)/shard_map/ppermute | solution.py:14
  152.5 2.1 collective-permute-start.1
  155.3 3.1 collective-permute-done.1
  158.4 5.0 %fusion.5 = f32[5,192,384]{2,1,0:T(8,128)} fusion(f32[5,384,192]{1,2,0:T(8,128)S(1)} %bitcast_divide_fusion, f32[5,384,2]{1,2,0:T(2,128)S(1)} %collective-permute-done.1, f32[5,384,2]{1,2,0:T(2,128)S(1)} %collective-permute-done, f32[]{:T(128)} %bitcast.20, f32[]{:T(128)} %bitcast.19, f32[]{:T(128)} %bitcast.18, f32[]{:T(128)} %bitcast.17, f32[]{:T(128)} %bitcast), kind=kLoop, calls=%fused_computation.19 | loop fusion | flops 4792320 | bytes 2979860 | tf_op jit(solution)/shard_map/transpose | solution.py:85
  163.5 33.8 %multiply_add_fusion = f32[3,3072,384]{2,1,0:T(8,128)} fusion(f32[3,3072,384]{2,1,0:T(8,128)} %all-gather.3.cloned.1.call-done, f32[]{:T(128)} %bitcast.20, f32[]{:T(128)} %bitcast.19, f32[]{:T(128)} %bitcast.18, f32[]{:T(128)} %bitcast.17, f32[]{:T(128)} %bitcast), kind=kLoop, calls=%fused_computation.2 | loop fusion | flops 31850496 | bytes 28311572 | tf_op jit(solution)/shard_map/add | solution.py:78
  197.3 13.4 %fusion.13 = f32[3,192,3072]{2,1,0:T(8,128)} fusion(f32[3,3072,384]{2,1,0:T(8,128)} %multiply_add_fusion, s32[]{:T(128)S(6)} %select_n.119, f32[3]{0:T(128)S(1)} %get-tuple-element.29), kind=kOutput, calls=%fused_computation.40 | convolution fusion | flops 4077084672 | bytes 22118416 | tf_op jit(solution)/shard_map/rfs,rgs->rfg/dot_general | solution.py:20
  210.7 12.7 %pad.23 = f32[8,192,3072]{2,1,0:T(8,128)} pad(f32[3,192,3072]{2,1,0:T(8,128)} %fusion.13, f32[]{:T(128)} %constant.86.clone.1), padding=0_5x0_0x0_0 | pad | bytes 25952260 | tf_op jit(solution)/shard_map/jit(_pad)/pad | solution.py:89
  223.5 63.8 %all-gather.5.cloned.1.call-done = f32[5,3072,384]{2,1,0:T(8,128)} async-done(((f32[5,192,384]{2,1,0:T(8,128)}), f32[5,3072,384]{2,1,0:T(8,128)}) %all-gather.5.cloned.1.call-update) | async-done | bytes 23592976 | tf_op jit(solution)/shard_map/all_gather | solution.py:86
  287.2 20.2 %convolution_dynamic-update-slice_fusion = f32[8,192,3072]{2,1,0:T(8,128)} fusion(f32[8,192,3072]{2,1,0:T(8,128)} %pad.23, f32[5,3072,384]{2,1,0:T(8,128)} %all-gather.5.cloned.1.call-done, f32[5,192,384]{2,1,0:T(8,128)S(1)} %copy-done, f32[5]{0:T(128)S(1)} %get-tuple-element.20), kind=kOutput, calls=%fused_computation.5 | convolution fusion | flops 6795141120 | bytes 36864020 | tf_op jit(solution)/shard_map/rfs,rgs->rfg/dot_general | solution.py:20
  (56 shorter events, 6.7 us)
Async XLA Ops:
  6.5 4.2 %copy-start.1 = (f32[1,24,12288]{2,1,0:T(8,128)S(1)}, f32[1,24,12288]{2,1,0:T(8,128)}, u32[]{:S(2)}) copy-start(f32[1,24,12288]{2,1,0:T(8,128)} %param.4) | copy-start | bytes 3538948
  39.8 8.7 %copy-start.3 = (s32[64]{0:T(128)S(1)}, s32[64]{0:T(128)}, u32[]{:S(2)}) copy-start(s32[64]{0:T(128)} %param.6) | copy-start | bytes 772
  39.8 22.1 %all-to-all-start = ((f32[8,1184,24]{1,2,0:T(8,128)}), f32[8,1184,24]{1,2,0:T(8,128)S(1)}, u32[]{:S(2)}, u32[]{:S(2)}) async-start(f32[8,1184,24]{1,2,0:T(8,128)} %copy.13), calls=%async_computation | async-start | bytes 1966080 | tf_op jit(solution)/shard_map/all_to_all | solution.py:58
  48.4 115.1 %all-gather.3.cloned.1.call-start = ((), (), s32[]{:S(2)}) async-start(), calls=%async_computation.2 | async-start | bytes 15040512 | tf_op jit(solution)/shard_map/all_gather | solution.py:73
  103.6 43.8 %all-to-all-start.1 = ((f32[8,1952,24]{1,2,0:T(8,128)}), f32[8,1952,24]{1,2,0:T(8,128)S(1)}, u32[]{:S(2)}, u32[]{:S(2)}) async-start(f32[8,1952,24]{1,2,0:T(8,128)} %copy.16), calls=%async_computation.1 | async-start | bytes 3145728 | tf_op jit(solution)/shard_map/all_to_all | solution.py:58
  109.5 177.7 %all-gather.5.cloned.1.call-start = ((), (), s32[]{:S(2)}) async-start(), calls=%async_computation.3 | async-start | bytes 25067520 | tf_op jit(solution)/shard_map/all_gather | solution.py:86
  148.4 6.2 %copy-start.2 = (f32[5]{0:T(128)S(1)}, f32[5]{0:T(128)}, u32[]{:S(2)}) copy-start(f32[5]{0:T(128)} %param.7) | copy-start | bytes 64
  148.7 6.6 %collective-permute-start = (f32[5,384,2]{1,2,0:T(2,128)S(1)}, f32[5,384,2]{1,2,0:T(2,128)S(1)}, u32[]{:S(2)}, u32[]{:S(2)}) collective-permute-start(f32[5,384,2]{1,2,0:T(2,128)S(1)} %get-tuple-element.15), channel_id=1, source_target_pairs={{0,1},{1,2},{2,3},{3,4},{4,5},{5,6},{6,7},{7,8},{8,9},{9,10},{10,1... | collective-permute-start | bytes 46088 | tf_op jit(solution)/shard_map/ppermute | solution.py:14
  152.5 5.9 %collective-permute-start.1 = (f32[5,384,2]{1,2,0:T(2,128)S(1)}, f32[5,384,2]{1,2,0:T(2,128)S(1)}, u32[]{:S(2)}, u32[]{:S(2)}) collective-permute-start(f32[5,384,2]{1,2,0:T(2,128)S(1)} %get-tuple-element.16), channel_id=1, source_target_pairs={{1,0},{2,1},{3,2},{4,3},{5,4},{6,5},{7,6},{8,7},{9,8},{10,9},{11,1... | collective-permute-start | bytes 46088 | tf_op jit(solution)/shard_map/ppermute | solution.py:15
  210.7 76.5 %copy-start = (f32[5,192,384]{2,1,0:T(8,128)S(1)}, f32[5,192,384]{2,1,0:T(8,128)}, u32[]{:S(2)}) copy-start(f32[5,192,384]{2,1,0:T(8,128)} %fusion.5) | copy-start | bytes 4423684
Sparse Core Ops, SparseCore 0:
  63.7 97.0 all-gather.2
  163.6 123.6 all-gather.4

commit v15 on v14

--- a/solution.py
+++ b/solution.py
@@ -38,7 +38,7 @@
     sizes = lax.dynamic_index_in_dim(cycle_sizes.reshape(groups, owned), me, 0, keepdims=False)
     slots = jnp.arange(cap, dtype=jnp.int32)
 
-    lanes = 32
+    lanes = 16
     longest = max(counts) * cap + lanes
     count = pixels // lanes + longest // lanes
     order = jnp.pad(pixel_order, (0, count * lanes - pixels)).reshape(count, lanes).astype(jnp.float32)

time: 315 us -> 317 us (level)
  no operation moved by 1% of the time
where the time goes in v15:
time: 317 us; the launch traced here: 316 us
  waiting for transfers between devices  95.8 us (30%)
  local copies, waits for them, and re-layouts  84.9 us (27%)
  other arithmetic  44.4 us (14%)
  matrix products  37 us (12%)
  between operations  33.7 us (11%)
  starting transfers between devices  20.3 us (6%)
    all_gather x1, waiting for transfers between devices, per_device(): right = lax.all_gather(smooth, 'tm', axis=1, tiled=True)  64 us
    gather x2, local copies, waits for them, and re-layouts, per_device(): series.at[window].get(mode='promise_in_bounds').reshape(groups, span, sub)  53.4 us
    add x1, other arithmetic, per_device(): right + kernel[shift_step] * rimmed[:, shift_step:shift_step + frames_all]  34 us
    dot_general x2, matrix products, correlate(): jnp.einsum('rfs,rgs->rfg', left, right, precision=lax.Precision.HIGH, pre...  33.6 us
    all_to_all x2, waiting for transfers between devices, per_device(): got = lax.all_to_all(chunks, 'pix', 0, 0, tiled=True)  28.9 us
    all_to_all x2, starting transfers between devices, per_device(): got = lax.all_to_all(chunks, 'pix', 0, 0, tiled=True)  14.5 us
    pad x1, local copies, waits for them, and re-layouts, per_device(): jnp.pad(jnp.concatenate(outs[:-1], 0), ((0, last), (0, 0), (0, 0)))  12.7 us
    reshape x2, local copies, waits for them, and re-layouts, per_device(): series.at[window].get(mode='promise_in_bounds').reshape(groups, span, sub)  10 us
  transfers between devices with their start and end apart: 6, of which 4 were waited for; matrix products, arithmetic and copies ran while one was open for 35% of the time, Pallas kernels for 0%

profile of v15, /device:TPU:1, one launch (start us, length us, event | category | flops | bytes accessed | tf_op | source)
XLA Modules:
  0.0 316.1 jit_solution(7960660431794776523)
XLA Ops:
  6.5 0.8 copy.10
  7.6 0.7 sub.37
  8.6 0.8 pad_convert_fusion
  9.6 1.6 fusion.17
  11.7 4.0 %copy.9 = f32[1,24,12288]{1,2,0:T(8,128)} copy(f32[1,24,12288]{2,1,0:T(8,128)S(1)} %copy-done.1) | data formatting | bytes 2359296 | tf_op args[0]
  15.7 21.1 %gather_fusion = f32[9344,24]{1,0:T(8,128)} fusion(f32[12288,24]{1,0:T(8,128)} %bitcast.76, s32[10240]{0:T(1024)S(1)} %pad_clamp_fusion.1), kind=kCustom, calls=%fused_computation | custom fusion | bytes 1831424 | tf_op jit(solution)/shard_map/gather | solution.py:57
  36.7 3.9 %copy.13 = f32[8,1168,24]{1,2,0:T(8,128)} copy(f32[8,1168,24]{2,1,0:T(8,128)} %bitcast.79) | data formatting | bytes 1794048 | tf_op jit(solution)/shard_map/reshape | solution.py:57
  40.6 8.6 %all-to-all-start = ((f32[8,1168,24]{1,2,0:T(8,128)}), f32[8,1168,24]{1,2,0:T(8,128)S(1)}, u32[]{:S(2)}, u32[]{:S(2)}) async-start(f32[8,1168,24]{1,2,0:T(8,128)} %copy.13), calls=%async_computation | async-start | bytes 1966080 | tf_op jit(solution)/shard_map/all_to_all | solution.py:58
  59.2 3.6 %all-to-all-done = f32[8,1168,24]{1,2,0:T(8,128)S(1)} async-done(((f32[8,1168,24]{1,2,0:T(8,128)}), f32[8,1168,24]{1,2,0:T(8,128)S(1)}, u32[]{:S(2)}, u32[]{:S(2)}) %all-to-all-start) | async-done | bytes 897056 | tf_op jit(solution)/shard_map/all_to_all | solution.py:58
  63.4 1.1 bitcast_divide_fusion.1
  64.6 1.8 fusion.18
  67.1 32.3 %gather_fusion.1 = f32[15488,24]{1,0:T(8,128)} fusion(f32[12288,24]{1,0:T(8,128)} %bitcast.77, s32[16384]{0:T(1024)S(1)} %pad_clamp_fusion), kind=kCustom, calls=%fused_computation.1 | custom fusion | bytes 3035648 | tf_op jit(solution)/shard_map/gather | solution.py:57
  99.4 6.1 %copy.16 = f32[8,1936,24]{1,2,0:T(8,128)} copy(f32[8,1936,24]{2,1,0:T(8,128)} %bitcast.78) | data formatting | bytes 2973696 | tf_op jit(solution)/shard_map/reshape | solution.py:57
  105.5 5.9 %all-to-all-start.1 = ((f32[8,1936,24]{1,2,0:T(8,128)}), f32[8,1936,24]{1,2,0:T(8,128)S(1)}, u32[]{:S(2)}, u32[]{:S(2)}) async-start(f32[8,1936,24]{1,2,0:T(8,128)} %copy.16), calls=%async_computation.1 | async-start | bytes 3145728 | tf_op jit(solution)/shard_map/all_to_all | solution.py:58
  124.0 25.3 %all-to-all-done.1 = f32[8,1936,24]{1,2,0:T(8,128)S(1)} async-done(((f32[8,1936,24]{1,2,0:T(8,128)}), f32[8,1936,24]{1,2,0:T(8,128)S(1)}, u32[]{:S(2)}, u32[]{:S(2)}) %all-to-all-start.1) | async-done | bytes 1486880 | tf_op jit(solution)/shard_map/all_to_all | solution.py:58
  150.6 3.6 %collective-permute-start = (f32[5,384,2]{1,2,0:T(2,128)S(1)}, f32[5,384,2]{1,2,0:T(2,128)S(1)}, u32[]{:S(2)}, u32[]{:S(2)}) collective-permute-start(f32[5,384,2]{1,2,0:T(2,128)S(1)} %get-tuple-element.15), channel_id=1, source_target_pairs={{0,1},{1,2},{2,3},{3,4},{4,5},{5,6},{6,7},{7,8},{8,9},{9,10},{10,1... | collective-permute-start | bytes 46088 | tf_op jit(solution)/shard_map/ppermute | solution.py:14
  154.3 2.1 collective-permute-start.1
  157.1 2.7 collective-permute-done.1
  159.8 5.0 %fusion.8 = f32[5,192,384]{2,1,0:T(8,128)} fusion(f32[5,384,192]{1,2,0:T(8,128)S(1)} %bitcast_divide_fusion, f32[5,384,2]{1,2,0:T(2,128)S(1)} %collective-permute-done.1, f32[5,384,2]{1,2,0:T(2,128)S(1)} %collective-permute-done, f32[]{:T(128)} %bitcast.20, f32[]{:T(128)} %bitcast.19, f32[]{:T(128)} %bitcast.18, f32[]{:T(128)} %bitcast.17, f32[]{:T(128)} %bitcast), kind=kLoop, calls=%fused_computation.24 | loop fusion | flops 4792320 | bytes 2979860 | tf_op jit(solution)/shard_map/transpose | solution.py:85
  164.9 34.0 %multiply_add_fusion = f32[3,3072,384]{2,1,0:T(8,128)} fusion(f32[3,3072,384]{2,1,0:T(8,128)} %all-gather.3.cloned.1.call-done, f32[]{:T(128)} %bitcast.20, f32[]{:T(128)} %bitcast.19, f32[]{:T(128)} %bitcast.18, f32[]{:T(128)} %bitcast.17, f32[]{:T(128)} %bitcast), kind=kLoop, calls=%fused_computation.2 | loop fusion | flops 31850496 | bytes 28311572 | tf_op jit(solution)/shard_map/add | solution.py:78
  198.9 13.4 %fusion.19 = f32[3,192,3072]{2,1,0:T(8,128)} fusion(f32[3,3072,384]{2,1,0:T(8,128)} %multiply_add_fusion, s32[]{:T(128)S(6)} %select_n.119, f32[3]{0:T(128)S(1)} %get-tuple-element.29), kind=kOutput, calls=%fused_computation.45 | convolution fusion | flops 4077084672 | bytes 22118416 | tf_op jit(solution)/shard_map/rfs,rgs->rfg/dot_general | solution.py:20
  212.3 12.7 %pad.23 = f32[8,192,3072]{2,1,0:T(8,128)} pad(f32[3,192,3072]{2,1,0:T(8,128)} %fusion.19, f32[]{:T(128)} %constant.86.clone.1), padding=0_5x0_0x0_0 | pad | bytes 25952260 | tf_op jit(solution)/shard_map/jit(_pad)/pad | solution.py:89
  225.0 64.0 %all-gather.5.cloned.1.call-done = f32[5,3072,384]{2,1,0:T(8,128)} async-done(((f32[5,192,384]{2,1,0:T(8,128)}), f32[5,3072,384]{2,1,0:T(8,128)}) %all-gather.5.cloned.1.call-update) | async-done | bytes 23592976 | tf_op jit(solution)/shard_map/all_gather | solution.py:86
  289.1 20.2 %convolution_dynamic-update-slice_fusion = f32[8,192,3072]{2,1,0:T(8,128)} fusion(f32[8,192,3072]{2,1,0:T(8,128)} %pad.23, f32[5,3072,384]{2,1,0:T(8,128)} %all-gather.5.cloned.1.call-done, f32[5,192,384]{2,1,0:T(8,128)S(1)} %copy-done, f32[5]{0:T(128)S(1)} %get-tuple-element.20), kind=kOutput, calls=%fused_computation.5 | convolution fusion | flops 6795141120 | bytes 36864020 | tf_op jit(solution)/shard_map/rfs,rgs->rfg/dot_general | solution.py:20
  (56 shorter events, 7.0 us)
Async XLA Ops:
  6.5 5.1 %copy-start.1 = (f32[1,24,12288]{2,1,0:T(8,128)S(1)}, f32[1,24,12288]{2,1,0:T(8,128)}, u32[]{:S(2)}) copy-start(f32[1,24,12288]{2,1,0:T(8,128)} %param.4) | copy-start | bytes 3538948
  40.6 8.7 %copy-start.3 = (s32[64]{0:T(128)S(1)}, s32[64]{0:T(128)}, u32[]{:S(2)}) copy-start(s32[64]{0:T(128)} %param.6) | copy-start | bytes 772
  40.6 22.1 %all-to-all-start = ((f32[8,1168,24]{1,2,0:T(8,128)}), f32[8,1168,24]{1,2,0:T(8,128)S(1)}, u32[]{:S(2)}, u32[]{:S(2)}) async-start(f32[8,1168,24]{1,2,0:T(8,128)} %copy.13), calls=%async_computation | async-start | bytes 1966080 | tf_op jit(solution)/shard_map/all_to_all | solution.py:58
  49.2 115.7 %all-gather.3.cloned.1.call-start = ((), (), s32[]{:S(2)}) async-start(), calls=%async_computation.2 | async-start | bytes 15040512 | tf_op jit(solution)/shard_map/all_gather | solution.py:73
  105.5 43.8 %all-to-all-start.1 = ((f32[8,1936,24]{1,2,0:T(8,128)}), f32[8,1936,24]{1,2,0:T(8,128)S(1)}, u32[]{:S(2)}, u32[]{:S(2)}) async-start(f32[8,1936,24]{1,2,0:T(8,128)} %copy.16), calls=%async_computation.1 | async-start | bytes 3145728 | tf_op jit(solution)/shard_map/all_to_all | solution.py:58
  111.4 177.7 %all-gather.5.cloned.1.call-start = ((), (), s32[]{:S(2)}) async-start(), calls=%async_computation.3 | async-start | bytes 25067520 | tf_op jit(solution)/shard_map/all_gather | solution.py:86
  150.3 6.1 %copy-start.2 = (f32[5]{0:T(128)S(1)}, f32[5]{0:T(128)}, u32[]{:S(2)}) copy-start(f32[5]{0:T(128)} %param.7) | copy-start | bytes 64
  150.6 6.4 %collective-permute-start = (f32[5,384,2]{1,2,0:T(2,128)S(1)}, f32[5,384,2]{1,2,0:T(2,128)S(1)}, u32[]{:S(2)}, u32[]{:S(2)}) collective-permute-start(f32[5,384,2]{1,2,0:T(2,128)S(1)} %get-tuple-element.15), channel_id=1, source_target_pairs={{0,1},{1,2},{2,3},{3,4},{4,5},{5,6},{6,7},{7,8},{8,9},{9,10},{10,1... | collective-permute-start | bytes 46088 | tf_op jit(solution)/shard_map/ppermute | solution.py:14
  154.3 5.5 %collective-permute-start.1 = (f32[5,384,2]{1,2,0:T(2,128)S(1)}, f32[5,384,2]{1,2,0:T(2,128)S(1)}, u32[]{:S(2)}, u32[]{:S(2)}) collective-permute-start(f32[5,384,2]{1,2,0:T(2,128)S(1)} %get-tuple-element.16), channel_id=1, source_target_pairs={{1,0},{2,1},{3,2},{4,3},{5,4},{6,5},{7,6},{8,7},{9,8},{10,9},{11,1... | collective-permute-start | bytes 46088 | tf_op jit(solution)/shard_map/ppermute | solution.py:15
  212.3 76.8 %copy-start = (f32[5,192,384]{2,1,0:T(8,128)S(1)}, f32[5,192,384]{2,1,0:T(8,128)}, u32[]{:S(2)}) copy-start(f32[5,192,384]{2,1,0:T(8,128)} %fusion.8) | copy-start | bytes 4423684
Sparse Core Ops, SparseCore 0:
  64.6 96.8 all-gather.2
  165.0 124.0 all-gather.4
